TPU v7x, 256 devices: a whole 4x4x8 slice. The times are simulated.
256 devices in a mesh: cfg: 2 (over z_lo), seq: 16 (over z_hi, x), wblk: 8 (over y, core).
Axes of the slice: x: 4, y: 4, z: 8 (z_hi: 4, z_lo: 2; z = z_hi * 2 + z_lo), core: 2. Of those that a mesh axis runs over, the one named last changes fastest.
Arguments:
- text_tokens: bfloat16 [2, 2, 512, 3072], P('cfg', None, 'seq', 'wblk'), may hold values from -16 to 16
- image_tokens: bfloat16 [2, 4096, 3072], P(None, 'seq', 'wblk'), may hold values from -16 to 16
- pooled_vector: float32 [2, 3072], P('cfg', 'seq'), may hold values from -6 to 6
- mod_weight: bfloat16 [3072, 3, 3072], P('seq', None, 'wblk'), may hold values from -0.109375 to 0.109375
- qkv_weight: bfloat16 [3072, 3, 16, 128], P('seq', None, 'wblk'), may hold values from -0.109375 to 0.109375
- up_weight: bfloat16 [3072, 6144], P('seq', 'wblk'), may hold values from -0.109375 to 0.109375
- query_gain: float32 [128], replicated, may hold values from 0.6 to 10
- key_gain: float32 [128], replicated, may hold values from 0.6 to 10
- attn_weight: bfloat16 [2048, 3072], P('wblk', 'seq'), may hold values from -0.125 to 0.125
- down_weight: bfloat16 [6144, 3072], P('wblk', 'seq'), may hold values from -0.078125 to 0.078125
- lengths: int32 [2], replicated, may hold values from 1 to 512, as said below
- timestep: int32 [1], replicated, may hold values from 0 to 27
Outputs:
- text_out: bfloat16 [2, 2, 512, 3072], P('cfg', None, 'seq', 'wblk')
- velocity: float32 [2, 4096, 3072], P('cfg', 'seq', 'wblk')
- new_image: float32 [2, 4096, 3072], P('cfg', 'seq', 'wblk')
Inputs may be any that keep to these rules, and one draw needn't show every extreme that they name: `lengths`: some prompt has all 512 text tokens live in every draw.
All inputs are finite; a program needn't handle non-finite values.
Results may differ from a plain program's by a relative error of at most 0.025.
Values may be sent and summed in bfloat16 or wider, within the bound.
No kernel may reach another device: no remote copies, remote signals or barrier semaphores. Data moves between devices by JAX's collectives and lax.ppermute only.
A program may use at most 128 MiB of HBM per device.

v0:
```python
import math

import jax
import jax.numpy as jnp
from jax import lax
from jax.sharding import PartitionSpec as P

D = 3072
HD = 128
GRID = 64
STEPS = 28


epsilon = 1e-06
guidance = 3.5
time_shift = 3.0
rope_theta = 10000.0


def plan(timestep):
    step_index = timestep[0].astype(jnp.float32)
    time_now = 1.0 - step_index / STEPS
    time_next = 1.0 - (step_index + 1.0) / STEPS
    sigma_now = time_shift * time_now / (1.0 + (time_shift - 1.0) * time_now)
    sigma_next = time_shift * time_next / (1.0 + (time_shift - 1.0) * time_next)
    return (sigma_now, sigma_next - sigma_now)


def time_embedding(sigma_now, dim_count):
    halfwidth = dim_count // 2
    frequency = jnp.exp(-math.log(10000.0) * jnp.arange(halfwidth, dtype=jnp.float32) / halfwidth)
    angles = 1000.0 * sigma_now * frequency
    return jnp.concatenate([jnp.cos(angles), jnp.sin(angles)])


def inverse_freq(dim_count):
    return rope_theta ** (-jnp.arange(0, dim_count, 2, dtype=jnp.float32) / dim_count)


def rotary_angles(height_pos, width_pos):
    still_dims = HD // 8
    axis_dims = (HD - still_dims) // 2
    return jnp.concatenate(
        [
            jnp.zeros((height_pos.shape[0], still_dims // 2), jnp.float32),
            height_pos[:, None] * inverse_freq(axis_dims)[None],
            width_pos[:, None] * inverse_freq(axis_dims)[None],
        ],
        axis=1,
    )


def rotate(vectors, angles):
    paired_dims = vectors.reshape(vectors.shape[:-1] + (HD // 2, 2))
    cosine_table = jnp.cos(angles)[:, None, :]
    sine_table = jnp.sin(angles)[:, None, :]
    first_part = paired_dims[..., 0]
    second_part = paired_dims[..., 1]
    turned = jnp.stack(
        [
            first_part * cosine_table - second_part * sine_table,
            first_part * sine_table + second_part * cosine_table,
        ],
        axis=-1,
    )
    return turned.reshape(vectors.shape)


def head_norm(vectors, gain_vector):
    return (
        vectors
        * lax.rsqrt(jnp.mean(vectors * vectors, axis=-1, keepdims=True) + epsilon)
        * gain_vector
    )


def input_folder(source, pieces):
    width_rows = pieces[0].shape[0]
    first_total = jnp.dot(
        source, pieces[0].reshape(width_rows, -1), preferred_element_type=jnp.float32
    )
    second_total = jnp.dot(source, pieces[1], preferred_element_type=jnp.float32)
    return (first_total, second_total)


def output_folder(attended, activated, pieces):
    block_cols = jnp.dot(attended, pieces[0], preferred_element_type=jnp.float32)
    block_cols = block_cols + jnp.dot(activated, pieces[1], preferred_element_type=jnp.float32)
    return block_cols


def shards(
    text_tokens,
    image_tokens,
    pooled_vector,
    mod_weight,
    qkv_weight,
    up_weight,
    query_gain,
    key_gain,
    attn_weight,
    down_weight,
    lengths,
    timestep,
):
    seq_pos = lax.axis_index("seq")
    cfg_pos = lax.axis_index("cfg")
    prompts = image_tokens.shape[0]
    image_rows = image_tokens.shape[1]
    text_rows = text_tokens.shape[2]
    local_len = text_rows + image_rows
    dim_local = image_tokens.shape[2]
    dim_seq = pooled_vector.shape[1]
    heads_local = qkv_weight.shape[2]
    row_count = prompts * local_len
    sigma_now, step_size = plan(timestep)
    embedded = lax.dynamic_slice_in_dim(time_embedding(sigma_now, D), seq_pos * dim_seq, dim_seq)
    cond_vec = jax.nn.silu(pooled_vector[0] + embedded).astype(jnp.bfloat16)[None]
    mod_terms = jnp.dot(
        cond_vec, mod_weight.reshape(dim_seq, 3 * dim_local), preferred_element_type=jnp.float32
    )
    modulation = lax.psum(mod_terms.reshape(3, dim_local), "seq")
    local_rows = jnp.concatenate([text_tokens[0], image_tokens], axis=1)
    hidden = local_rows.astype(jnp.float32)
    totals, squares = lax.psum(
        (jnp.sum(hidden, axis=-1), jnp.sum(hidden * hidden, axis=-1)), "wblk"
    )
    average = (totals / D)[..., None]
    variance = (squares / D)[..., None] - average * average
    normed = (
        (hidden - average) * lax.rsqrt(variance + epsilon) * (1.0 + modulation[1]) + modulation[0]
    ).astype(jnp.bfloat16)
    gathered = lax.all_gather(normed, "wblk", axis=2, tiled=True)
    token_rows = gathered.reshape(row_count, D)
    projected, mlp_units = input_folder(
        token_rows,
        (
            lax.all_gather(qkv_weight, "seq", axis=0, tiled=True),
            lax.all_gather(up_weight, "seq", axis=0, tiled=True),
        ),
    )
    projected = projected.reshape(prompts, local_len, 3, heads_local, HD)
    image_index = seq_pos * image_rows + jnp.arange(image_rows, dtype=jnp.int32)
    height_pos = jnp.concatenate(
        [jnp.zeros((text_rows,), jnp.float32), (image_index // GRID).astype(jnp.float32)]
    )
    width_pos = jnp.concatenate(
        [jnp.zeros((text_rows,), jnp.float32), (image_index % GRID).astype(jnp.float32)]
    )
    angles = rotary_angles(height_pos, width_pos)
    queries = rotate(head_norm(projected[:, :, 0], query_gain), angles).astype(jnp.bfloat16)
    key_rows = rotate(head_norm(projected[:, :, 1], key_gain), angles).astype(jnp.bfloat16)
    values = projected[:, :, 2].astype(jnp.bfloat16)
    scale_factor = HD ** (-0.5)
    running_max = jnp.full((prompts, heads_local, local_len), -1e30, jnp.float32)
    key_piece = lax.all_gather(key_rows, "seq", axis=1, tiled=True)
    value_piece = lax.all_gather(values, "seq", axis=1, tiled=True)
    width_keys = key_piece.shape[1]
    where_global = jnp.arange(width_keys, dtype=jnp.int32)
    shard_index = where_global // local_len
    within = where_global % local_len
    text_index = shard_index * text_rows + within
    key_live = (within >= text_rows)[None, :] | (text_index[None, :] < lengths[:, None])
    scores = (
        jnp.einsum("pqhd,pkhd->phqk", queries, key_piece, preferred_element_type=jnp.float32)
        * scale_factor
    )
    scores = jnp.where(key_live[:, None, None, :], scores, -1e30)
    new_max = jnp.maximum(running_max, jnp.max(scores, axis=-1))
    weights = jnp.exp(scores - new_max[..., None])
    denominator = jnp.sum(weights, axis=-1)
    numerator = jnp.einsum(
        "phqk,pkhd->phqd",
        weights.astype(jnp.bfloat16),
        value_piece,
        preferred_element_type=jnp.float32,
    )
    running_max, denominator, numerator = (new_max, denominator, numerator)
    attended = (numerator / denominator[..., None]).astype(jnp.bfloat16)
    attended = attended.transpose(0, 2, 1, 3).reshape(row_count, heads_local * HD)
    activated = jax.nn.gelu(mlp_units, approximate=True).astype(jnp.bfloat16)
    branch_terms = output_folder(
        attended,
        activated,
        (
            lax.all_gather(attn_weight, "seq", axis=1, tiled=True),
            lax.all_gather(down_weight, "seq", axis=1, tiled=True),
        ),
    )
    branch = lax.psum_scatter(
        branch_terms.reshape(prompts, local_len, D).astype(jnp.bfloat16),
        "wblk",
        scatter_dimension=2,
        tiled=True,
    ).astype(jnp.float32)
    layer_out = hidden + modulation[2] * branch
    text_out = layer_out[:, :text_rows].astype(jnp.bfloat16)[None]
    image_out = layer_out[:, text_rows:]
    paired = lax.all_to_all(
        image_out[:, None].astype(jnp.bfloat16), "cfg", split_axis=0, concat_axis=1, tiled=True
    ).astype(jnp.float32)
    velocity = paired[:, 1] + guidance * (paired[:, 0] - paired[:, 1])
    own_prompts = prompts // 2
    latent = lax.dynamic_slice_in_dim(image_tokens, cfg_pos * own_prompts, own_prompts, 0).astype(
        jnp.float32
    )
    new_image = latent + step_size * velocity
    return (text_out, velocity, new_image)


def solution(mesh):
    in_specs = (
        P("cfg", None, "seq", "wblk"),
        P(None, "seq", "wblk"),
        P("cfg", "seq"),
        P("seq", None, "wblk"),
        P("seq", None, "wblk", None),
        P("seq", "wblk"),
        P(),
        P(),
        P("wblk", "seq"),
        P("wblk", "seq"),
        P(),
        P(),
    )
    out_specs = (P("cfg", None, "seq", "wblk"), P("cfg", "seq", "wblk"), P("cfg", "seq", "wblk"))
    return jax.shard_map(shards, mesh=mesh, in_specs=in_specs, out_specs=out_specs, check_vma=False)
```

profile of v0, /device:TPU:2, one launch (start us, length us, event | category | flops | bytes accessed | tf_op | source)
XLA Modules:
  0.0 606.9 jit_solution(16747836014548433341)
XLA Ops:
  7.2 0.0 all-gather.11.cloned.1.call-start
  7.2 0.7 all-gather.11.cloned.1.call-update
  7.9 0.0 all-gather.9.cloned.1.call-start
  8.7 0.1 fusion.65
  8.7 0.8 fusion.73
  9.5 0.2 fusion.45
  9.7 1.3 convert_reduce_fusion
  11.0 15.1 %all-reduce.2 = (f32[2,288]{1,0:T(2,128)S(1)}, f32[2,288]{1,0:T(2,128)S(1)}) all-reduce(f32[2,288]{1,0:T(2,128)S(1)} %get-tuple-element.6, f32[2,288]{1,0:T(2,128)S(1)} %get-tuple-element.5), channel_id=1, replica_groups=mesh['cfg'=2,'seq'=16,'wblk'=8] {'wblk'}, use_global_device_ids=true, to_apply=%region_4.5 | all-reduce | flops 1152 | bytes 9216 | tf_op jit(solution)/shard_map/psum | solution.py:125
  26.1 46.2 %psum.21 = f32[3,384]{1,0:T(4,128)S(1)} all-reduce(f32[3,384]{1,0:T(4,128)S(1)} %bitcast.105), channel_id=1, replica_groups=mesh['cfg'=2,'seq'=16,'wblk'=8] {'seq'}, use_global_device_ids=true, to_apply=%region_0.1 | all-reduce | flops 1152 | bytes 9216 | tf_op jit(solution)/shard_map/psum | solution.py:122
  72.4 2.0 fusion.36
  74.4 0.0 all-gather.17.cloned.1.call-start
  74.5 0.7 all-gather.17.cloned.1.call-update
  75.2 0.0 all-gather.19.cloned.1.call-start
  75.2 0.5 all-gather.19.cloned.1.call-update
  75.7 0.0 all-gather.13.cloned.1.call-start
  75.8 0.8 mul.324
  76.6 0.8 mul.305
  77.4 0.1 concatenate.25
  77.5 0.1 concatenate.26
  77.6 0.1 broadcast_multiply_fusion.1
  77.6 0.4 fusion.56
  78.1 13.8 %all-gather.11.cloned.1.call-done = bf16[3072,3,2,128]{3,2,1,0:T(2,128)(2,1)} async-done(((bf16[192,3,2,128]{3,2,1,0:T(2,128)(2,1)}), bf16[3072,3,2,128]{3,2,1,0:T(2,128)(2,1)}) %all-gather.11.cloned.1.call-update) | async-done | bytes 4718608 | tf_op jit(solution)/shard_map/all_gather | solution.py:138
  91.9 12.5 %copy.34 = bf16[3072,3,2,128]{0,3,2,1:T(8,128)(2,1)} copy(bf16[3072,3,2,128]{3,2,1,0:T(2,128)(2,1)} %all-gather.11.cloned.1.call-done) | data formatting | bytes 9437184 | tf_op jit(solution)/shard_map/reshape | solution.py:80
  104.4 23.5 %all-gather.9.cloned.1.call-done = bf16[2,288,3072]{2,1,0:T(8,128)(2,1)} async-done(((bf16[2,288,384]{2,1,0:T(8,128)(2,1)}), bf16[2,288,3072]{2,1,0:T(8,128)(2,1)}) %all-gather.9.cloned.1.call-update) | async-done | bytes 3538960 | tf_op jit(solution)/shard_map/all_gather | solution.py:133
  127.9 6.8 %fusion.6 = f32[2,288,3,2,128]{4,1,3,2,0:T(8,128)S(1)} fusion(bf16[3072,3,2,128]{0,3,2,1:T(8,128)(2,1)} %copy.34, bf16[2,288,3072]{2,1,0:T(8,128)(2,1)} %all-gather.9.cloned.1.call-done), kind=kOutput, calls=%fused_computation.8 | convolution fusion | flops 2717908992 | bytes 10027008 | tf_op jit(solution)/shard_map/dot_general | solution.py:79
  134.6 0.5 multiply_reduce_fusion.1
  135.2 0.7 copy-done.3
  135.9 0.5 copy.26
  136.4 0.5 copy.25
  136.9 0.4 multiply_multiply_fusion.1
  137.3 0.4 multiply_multiply_fusion.2
  137.7 0.8 subtract_convert_fusion.1
  138.5 0.6 pad_maximum_fusion.2
  139.1 1.1 copy.27
  140.2 0.0 all-gather.21.cloned.1.call-start
  140.2 1.8 slice.102
  142.1 0.0 all-gather.15.cloned.1.call-start
  142.1 0.7 all-gather.15.cloned.1.call-update
  142.8 0.2 reduce-scatter.4.cloned.1.call-start
  143.1 0.1 compare_or_fusion
  143.2 0.6 pad_maximum_fusion.1
  143.8 64.8 %all-gather.17.cloned.1.call-done = bf16[3072,768]{1,0:T(8,128)(2,1)} async-done(((bf16[192,768]{1,0:T(8,128)(2,1)}), bf16[3072,768]{1,0:T(8,128)(2,1)}) %all-gather.17.cloned.1.call-update) | async-done | bytes 4718608 | tf_op jit(solution)/shard_map/all_gather | solution.py:139
  208.6 82.8 %all-gather.19.cloned.1.call-done = bf16[768,3072]{0,1:T(8,128)(2,1)} async-done(((bf16[768,192]{0,1:T(8,128)(2,1)}), bf16[768,3072]{0,1:T(8,128)(2,1)}) %all-gather.19.cloned.1.call-update) | async-done | bytes 4718608 | tf_op jit(solution)/shard_map/all_gather | solution.py:187
  291.5 15.0 %fusion.39 = f32[576,3072]{1,0:T(8,128)} fusion(bf16[768,3072]{0,1:T(8,128)(2,1)} %all-gather.19.cloned.1.call-done, bf16[576,3072]{1,0:T(8,128)(2,1)} %bitcast.108, bf16[3072,768]{1,0:T(8,128)(2,1)} %all-gather.17.cloned.1.call-done), kind=kOutput, calls=%fused_computation.34 | convolution fusion | flops 5439799296 | bytes 20054016 | tf_op jit(solution)/shard_map/dot_general | solution.py:88
  306.5 68.4 %all-gather.13.cloned.1.call-done = bf16[2,4608,2,128]{3,1,2,0:T(8,128)(2,1)} async-done(((bf16[2,288,2,128]{3,1,2,0:T(8,128)(2,1)}), bf16[2,4608,2,128]{3,1,2,0:T(8,128)(2,1)}) %all-gather.13.cloned.1.call-update) | async-done | bytes 4718608 | tf_op jit(solution)/shard_map/all_gather | solution.py:156
  374.9 13.5 %fusion = (f32[2,2,288]{2,1,0:T(2,128)S(1)}, f32[2,2,288,4608]{3,2,1,0:T(8,128)}) fusion(pred[2,4608]{1,0:T(4,128)(4,1)S(1)} %compare_or_fusion, bf16[2,4608,2,128]{3,1,2,0:T(8,128)(2,1)} %all-gather.13.cloned.1.call-done, bf16[2,288,2,128]{1,2,3,0:T(2,128)(2,1)S(1)} %bitcast.100), kind=kOutput, calls=%fused_computation.2 | convolution fusion | flops 1374878592 | bytes 26260992 | tf_op jit(solution)/shard_map/pqhd,pkhd->phqk/dot_general | solution.py:165
  388.4 10.3 %fusion.1 = f32[2,2,288]{2,1,0:T(2,128)S(1)} fusion(f32[2,2,288,4608]{3,2,1,0:T(8,128)} %get-tuple-element.29, f32[2,2,288]{2,1,0:T(2,128)S(1)} %broadcast_maximum_fusion, pred[2,4608]{1,0:T(4,128)(4,1)S(1)} %compare_or_fusion), kind=kLoop, calls=%fused_computation.3 | loop fusion | flops 21232512 | bytes 21252096 | tf_op jit(solution)/shard_map/reduce_sum | solution.py:171
  398.7 59.5 %all-gather.21.cloned.1.call-done = bf16[2,4608,1,2,128]{4,1,3,2,0:T(8,128)(2,1)} async-done(((bf16[2,288,1,2,128]{4,1,3,2,0:T(8,128)(2,1)}), bf16[2,4608,1,2,128]{4,1,3,2,0:T(8,128)(2,1)}) %all-gather.21.cloned.1.call-update) | async-done | bytes 4718608 | tf_op jit(solution)/shard_map/all_gather | solution.py:157
  458.3 10.9 %fusion.28 = bf16[2,288,2,128]{3,1,2,0:T(8,128)(2,1)S(1)} fusion(bf16[2,4608,1,2,128]{4,1,3,2,0:T(8,128)(2,1)} %all-gather.21.cloned.1.call-done, f32[2,2,288,4608]{3,2,1,0:T(8,128)} %get-tuple-element.29, f32[2,2,288]{2,1,0:T(2,128)S(1)} %broadcast_maximum_fusion, pred[2,4608]{1,0:T(4,128)(4,1)S(1)} %compare_or_fusion, f32[2,288,2]{1,2,0:T(2,128)S(1)} %bitcast.106), kind=kOutput, calls=%fused_computation.27 | convolution fusion | flops 1380483072 | bytes 26265600 | tf_op jit(solution)/shard_map/phqk,pkhd->phqd/dot_general | solution.py:172
  469.2 0.2 copy.29
  469.5 50.2 %all-gather.15.cloned.1.call-done = bf16[256,3072]{0,1:T(8,128)(2,1)} async-done(((bf16[256,192]{0,1:T(8,128)(2,1)}), bf16[256,3072]{0,1:T(8,128)(2,1)}) %all-gather.15.cloned.1.call-update) | async-done | bytes 1572880 | tf_op jit(solution)/shard_map/all_gather | solution.py:186
  519.6 6.4 %add_convert_fusion = bf16[576,3072]{1,0:T(8,128)(2,1)} fusion(f32[576,3072]{1,0:T(8,128)} %fusion.39, bf16[256,3072]{0,1:T(8,128)(2,1)} %all-gather.15.cloned.1.call-done, bf16[72,8,2,128]{3,2,1,0:T(2,128)(2,1)S(1)} %bitcast.101), kind=kOutput, calls=%fused_computation.7 | convolution fusion | flops 909508608 | bytes 12484608 | tf_op jit(solution)/shard_map/dot_general | solution.py:87
  526.0 12.3 %copy.35 = bf16[2,288,3072]{1,0,2:T(2,128)(2,1)} copy(bf16[2,288,3072]{2,1,0:T(8,128)(2,1)} %bitcast.95) | data formatting | bytes 7077888
  538.3 10.2 %reshape.323 = bf16[3072,576]{1,0:T(8,128)(2,1)} reshape(bf16[3072,2,288]{2,1,0:T(2,128)(2,1)} %bitcast.94) | data formatting | bytes 7077888
  548.5 37.4 %reduce-scatter.4.cloned.1.call-done = bf16[384,576]{1,0:T(8,128)(2,1)} async-done(((bf16[3072,576]{1,0:T(8,128)(2,1)}), bf16[384,576]{1,0:T(8,128)(2,1)}) %reduce-scatter.4.cloned.1.call-update) | async-done | bytes 442384
  585.9 2.1 reshape.324
  588.0 0.7 copy.36
  588.7 0.1 fusion.38
  588.9 0.8 slice_bitcast_fusion.2
  589.7 3.5 all-to-all-start
  593.2 0.6 slice_bitcast_fusion.3
  593.8 5.2 all-to-all-done
  599.0 0.1 bitcast_convert_fusion
  599.1 1.0 multiply_add_fusion
  (28 shorter events, 0.2 us)
Async XLA Ops:
  7.2 2.3 copy-start
  7.2 84.7 %all-gather.11.cloned.1.call-start = ((), (), s32[]{:S(2)}) async-start(), calls=%async_computation.3 | async-start | bytes 5013504 | tf_op jit(solution)/shard_map/all_gather | solution.py:138
  7.9 120.0 %all-gather.9.cloned.1.call-start = ((), (), s32[]{:S(2)}) async-start(), calls=%async_computation.2 | async-start | bytes 3981312 | tf_op jit(solution)/shard_map/all_gather | solution.py:133
  74.4 134.2 %all-gather.17.cloned.1.call-start = ((), (), s32[]{:S(2)}) async-start(), calls=%async_computation.6 | async-start | bytes 5013504 | tf_op jit(solution)/shard_map/all_gather | solution.py:139
  75.2 216.3 %all-gather.19.cloned.1.call-start = ((), (), s32[]{:S(2)}) async-start(), calls=%async_computation.7 | async-start | bytes 5013504 | tf_op jit(solution)/shard_map/all_gather | solution.py:187
  75.7 299.1 %all-gather.13.cloned.1.call-start = ((), (), s32[]{:S(2)}) async-start(), calls=%async_computation.4 | async-start | bytes 5013504 | tf_op jit(solution)/shard_map/all_gather | solution.py:156
  134.6 1.2 copy-start.3
  136.4 6.7 %copy-start.5 = (s32[2]{0:T(128)S(1)}, s32[2]{0:T(128)}, u32[]{:S(2)}) copy-start(s32[2]{0:T(128)} %param.22) | copy-start | bytes 28
  140.2 318.1 %all-gather.21.cloned.1.call-start = ((), (), s32[]{:S(2)}) async-start(), calls=%async_computation.8 | async-start | bytes 5013504 | tf_op jit(solution)/shard_map/all_gather | solution.py:157
  142.1 377.6 %all-gather.15.cloned.1.call-start = ((), (), s32[]{:S(2)}) async-start(), calls=%async_computation.5 | async-start | bytes 1671168 | tf_op jit(solution)/shard_map/all_gather | solution.py:186
  142.8 443.1 %reduce-scatter.4.cloned.1.call-start = ((), (), s32[]{:S(2)}) async-start(), calls=%async_computation.9 | async-start | bytes 4423680
  548.5 40.2 %copy-start.2 = (bf16[2,256,384]{2,1,0:T(8,128)(2,1)S(1)}, bf16[2,256,384]{2,1,0:T(8,128)(2,1)}, u32[]{:S(2)}) copy-start(bf16[2,256,384]{2,1,0:T(8,128)(2,1)} %param.13) | copy-start | bytes 1179652
  548.5 40.3 %copy-start.4 = (bf16[1,2,32,384]{3,2,1,0:T(8,128)(2,1)S(1)}, bf16[1,2,32,384]{3,2,1,0:T(8,128)(2,1)}, u32[]{:S(2)}) copy-start(bf16[1,2,32,384]{3,2,1,0:T(8,128)(2,1)} %param.12) | copy-start | bytes 147460
  548.5 51.5 %copy-start.1 = (bf16[192,3,384]{2,0,1:T(8,128)(2,1)S(1)}, bf16[192,3,384]{2,0,1:T(8,128)(2,1)}, u32[]{:S(2)}) copy-start(bf16[192,3,384]{2,0,1:T(8,128)(2,1)} %param.15) | copy-start | bytes 1327108
  589.7 9.3 %all-to-all-start = ((bf16[2,1,256,384]{3,2,1,0:T(8,128)(2,1)}), bf16[2,1,256,384]{3,2,1,0:T(8,128)(2,1)S(1)}, u32[]{:S(2)}, u32[]{:S(2)}) async-start(bf16[2,1,256,384]{3,2,1,0:T(8,128)(2,1)} %slice_bitcast_fusion.2), calls=%async_computation | async-start | bytes 786432 | tf_op jit(solution)/shard_map/all_to_all | solution.py:199
Sparse Core Ops, SparseCore 0:
  10.4 81.3 all-gather.10
  93.7 34.1 all-gather.8
  130.3 78.2 all-gather.16
  210.9 80.5 all-gather.18
  294.3 80.5 all-gather.12
  377.7 80.5 all-gather.20
  460.7 58.8 all-gather.14
  548.6 37.2 reduce-scatter.3
where the time goes:
time: 608 us; the launch traced here: 607 us
  waiting for transfers between devices  408 us (67%)
  blocking collectives  61.3 us (10%)
  matrix products  52.8 us (9%)
  local copies, waits for them, and re-layouts  45.8 us (8%)
  other arithmetic  19.5 us (3%)
  between operations  15.2 us (2%)
    all_gather x1, waiting for transfers between devices, shards(): lax.all_gather(down_weight, 'seq', axis=1, tiled=True)  82.8 us
    all_gather x1, waiting for transfers between devices, shards(): key_piece = lax.all_gather(key_rows, 'seq', axis=1, tiled=True)  68.4 us
    all_gather x1, waiting for transfers between devices, shards(): lax.all_gather(up_weight, 'seq', axis=0, tiled=True)  64.8 us
    all_gather x1, waiting for transfers between devices, shards(): value_piece = lax.all_gather(values, 'seq', axis=1, tiled=True)  59.5 us
    all_gather x1, waiting for transfers between devices, shards(): lax.all_gather(attn_weight, 'seq', axis=1, tiled=True)  50.2 us
    psum x1, blocking collectives, shards(): modulation = lax.psum(mod_terms.reshape(3, dim_local), 'seq')  46.2 us
    unnamed x9, waiting for transfers between devices  40 us
    unnamed x16, local copies, waits for them, and re-layouts  26 us
  transfers between devices with their start and end apart: 9, of which 9 were waited for; matrix products, arithmetic and copies ran while one was open for 14% of the time, Pallas kernels for 0%

commit v1 on v0

--- a/solution.py
+++ b/solution.py
@@ -152,31 +152,49 @@
     key_rows = rotate(head_norm(projected[:, :, 1], key_gain), angles).astype(jnp.bfloat16)
     values = projected[:, :, 2].astype(jnp.bfloat16)
     scale_factor = HD ** (-0.5)
-    running_max = jnp.full((prompts, heads_local, local_len), -1e30, jnp.float32)
-    key_piece = lax.all_gather(key_rows, "seq", axis=1, tiled=True)
-    value_piece = lax.all_gather(values, "seq", axis=1, tiled=True)
-    width_keys = key_piece.shape[1]
+    seq_count = lax.psum(1, "seq")
+    pair_count = prompts * heads_local
+    subs = seq_count // pair_count
+    sub_rows = local_len // subs
+    pair_keys = key_rows.transpose(0, 2, 1, 3).reshape(pair_count, local_len, HD)
+    pair_values = values.transpose(0, 2, 1, 3).reshape(pair_count, local_len, HD)
+    pair_queries = queries.transpose(0, 2, 1, 3).reshape(seq_count, sub_rows, HD)
+    send = jnp.concatenate(
+        [
+            jnp.broadcast_to(pair_keys[:, None], (pair_count, subs, local_len, HD)).reshape(
+                seq_count, local_len, HD
+            ),
+            jnp.broadcast_to(pair_values[:, None], (pair_count, subs, local_len, HD)).reshape(
+                seq_count, local_len, HD
+            ),
+            pair_queries,
+        ],
+        axis=1,
+    )
+    received = lax.all_to_all(send, "seq", 0, 0, tiled=True)
+    key_piece = received[:, :local_len].reshape(seq_count * local_len, HD)
+    value_piece = received[:, local_len : 2 * local_len].reshape(seq_count * local_len, HD)
+    query_piece = received[:, 2 * local_len :].reshape(seq_count * sub_rows, HD)
+    my_prompt = seq_pos // subs // heads_local
+    width_keys = key_piece.shape[0]
     where_global = jnp.arange(width_keys, dtype=jnp.int32)
     shard_index = where_global // local_len
     within = where_global % local_len
     text_index = shard_index * text_rows + within
-    key_live = (within >= text_rows)[None, :] | (text_index[None, :] < lengths[:, None])
+    key_live = (within >= text_rows) | (text_index < lengths[my_prompt])
     scores = (
-        jnp.einsum("pqhd,pkhd->phqk", queries, key_piece, preferred_element_type=jnp.float32)
-        * scale_factor
-    )
-    scores = jnp.where(key_live[:, None, None, :], scores, -1e30)
-    new_max = jnp.maximum(running_max, jnp.max(scores, axis=-1))
-    weights = jnp.exp(scores - new_max[..., None])
-    denominator = jnp.sum(weights, axis=-1)
-    numerator = jnp.einsum(
-        "phqk,pkhd->phqd",
-        weights.astype(jnp.bfloat16),
-        value_piece,
-        preferred_element_type=jnp.float32,
-    )
-    running_max, denominator, numerator = (new_max, denominator, numerator)
-    attended = (numerator / denominator[..., None]).astype(jnp.bfloat16)
+        jnp.dot(query_piece, key_piece.T, preferred_element_type=jnp.float32) * scale_factor
+    )
+    scores = jnp.where(key_live[None, :], scores, -1e30)
+    top_score = jnp.max(scores, axis=-1, keepdims=True)
+    weights = jnp.exp(scores - top_score)
+    denominator = jnp.sum(weights, axis=-1, keepdims=True)
+    numerator = jnp.dot(
+        weights.astype(jnp.bfloat16), value_piece, preferred_element_type=jnp.float32
+    )
+    mixed = (numerator / denominator).astype(jnp.bfloat16).reshape(seq_count, sub_rows, HD)
+    returned = lax.all_to_all(mixed, "seq", 0, 0, tiled=True)
+    attended = returned.reshape(prompts, heads_local, local_len, HD)
     attended = attended.transpose(0, 2, 1, 3).reshape(row_count, heads_local * HD)
     activated = jax.nn.gelu(mlp_units, approximate=True).astype(jnp.bfloat16)
     branch_terms = output_folder(

time: 608 us -> 488 us (0.80)
  waiting for transfers between devices: 408 us -> 283 us
  starting transfers between devices: 3.96 us -> 20.9 us
  matrix products: 52.8 us -> 43 us
    all_gather x2 -> x0, waiting for transfers between devices: 128 us -> none  [the longest x1 68.4 us: shards(): key_piece = lax.all_gather(key_rows, 'seq', axis=1, tiled=True)]
    all_to_all x0 -> x2, waiting for transfers between devices: none -> 100 us  [the longest x1 100 us: shards(): received = lax.all_to_all(send, 'seq', 0, 0, tiled=True)]
    all_gather x1, waiting for transfers between devices: 64.8 us -> 0.02 us  [shards(): lax.all_gather(up_weight, 'seq', axis=0, tiled=True)]
    all_gather x1, waiting for transfers between devices: 82.8 us -> 54.5 us  [shards(): lax.all_gather(down_weight, 'seq', axis=1, tiled=True)]
    all_to_all x0 -> x2, starting transfers between devices: none -> 16.8 us  [the longest x1 10.1 us: shards(): received = lax.all_to_all(send, 'seq', 0, 0, tiled=True)]
    dot_general x2, matrix products: 24.5 us -> 14.6 us  [the longest x1 11.1 us: shards(): jnp.dot(weights.astype(jnp.bfloat16), value_piece, preferred_element_type...]
    reduce_sum x1, other arithmetic: 10.3 us -> 4.23 us  [shards(): denominator = jnp.sum(weights, axis=-1, keepdims=True)]
    unnamed x9 -> x7, waiting for transfers between devices: 40 us -> 39.6 us
  transfers between devices with their start and end apart: 9 -> 9, of which waited for: 9 -> 7; matrix products, arithmetic and copies ran while one was open for 14% -> 14% of each run, Pallas kernels for 0% -> 0%
where the time goes in v1:
time: 488 us; the launch traced here: 486 us
  waiting for transfers between devices  283 us (58%)
  blocking collectives  61.4 us (13%)
  local copies, waits for them, and re-layouts  47.1 us (10%)
  matrix products  43 us (9%)
  starting transfers between devices  20.9 us (4%)
  other arithmetic  15.6 us (3%)
  between operations  15.2 us (3%)
    all_to_all x1, waiting for transfers between devices, shards(): received = lax.all_to_all(send, 'seq', 0, 0, tiled=True)  100 us
    all_gather x1, waiting for transfers between devices, shards(): lax.all_gather(down_weight, 'seq', axis=1, tiled=True)  54.5 us
    psum x1, blocking collectives, shards(): modulation = lax.psum(mod_terms.reshape(3, dim_local), 'seq')  46.3 us
    all_gather x1, waiting for transfers between devices, shards(): lax.all_gather(attn_weight, 'seq', axis=1, tiled=True)  46 us
    unnamed x7, waiting for transfers between devices  39.6 us
    unnamed x16, local copies, waits for them, and re-layouts  28.2 us
    all_gather x1, waiting for transfers between devices, shards(): gathered = lax.all_gather(normed, 'wblk', axis=2, tiled=True)  23.6 us
    psum x1, blocking collectives, shards(): lax.psum((jnp.sum(hidden, axis=-1), jnp.sum(hidden * hidden, axis=-1)), '...  15.1 us
  transfers between devices with their start and end apart: 9, of which 7 were waited for; matrix products, arithmetic and copies ran while one was open for 14% of the time, Pallas kernels for 0%

profile of v1, /device:TPU:2, one launch (start us, length us, event | category | flops | bytes accessed | tf_op | source)
XLA Modules:
  0.0 486.1 jit_solution(3172526040136737661)
XLA Ops:
  7.2 0.7 all-gather.8.cloned.1.call-update
  8.7 0.1 fusion.55
  8.7 0.8 fusion.63
  9.5 0.2 fusion.35
  9.7 1.3 convert_reduce_fusion
  11.0 15.1 %all-reduce.2 = (f32[2,288]{1,0:T(2,128)S(1)}, f32[2,288]{1,0:T(2,128)S(1)}) all-reduce(f32[2,288]{1,0:T(2,128)S(1)} %get-tuple-element.6, f32[2,288]{1,0:T(2,128)S(1)} %get-tuple-element.5), channel_id=1, replica_groups=mesh['cfg'=2,'seq'=16,'wblk'=8] {'wblk'}, use_global_device_ids=true, to_apply=%region_4.5 | all-reduce | flops 1152 | bytes 9216 | tf_op jit(solution)/shard_map/psum | solution.py:125
  26.1 46.3 %psum.21 = f32[3,384]{1,0:T(4,128)S(1)} all-reduce(f32[3,384]{1,0:T(4,128)S(1)} %bitcast.121), channel_id=1, replica_groups=mesh['cfg'=2,'seq'=16,'wblk'=8] {'seq'}, use_global_device_ids=true, to_apply=%region_0.1 | all-reduce | flops 1152 | bytes 9216 | tf_op jit(solution)/shard_map/psum | solution.py:122
  72.5 2.0 fusion.26
  74.5 0.0 all-gather.12.cloned.1.call-start
  74.6 0.7 all-gather.12.cloned.1.call-update
  75.3 0.5 all-gather.14.cloned.1.call-update
  75.8 0.8 mul.324
  76.6 0.8 mul.305
  77.4 0.1 concatenate.28
  77.5 0.1 concatenate.29
  77.6 0.1 broadcast_multiply_fusion.1
  77.7 0.4 fusion.44
  78.1 13.8 %all-gather.8.cloned.1.call-done = bf16[3072,3,2,128]{3,2,1,0:T(2,128)(2,1)} async-done(((bf16[192,3,2,128]{3,2,1,0:T(2,128)(2,1)}), bf16[3072,3,2,128]{3,2,1,0:T(2,128)(2,1)}) %all-gather.8.cloned.1.call-update) | async-done | bytes 4718608 | tf_op jit(solution)/shard_map/all_gather | solution.py:138
  91.9 12.4 %copy.38 = bf16[3072,3,2,128]{0,3,2,1:T(8,128)(2,1)} copy(bf16[3072,3,2,128]{3,2,1,0:T(2,128)(2,1)} %all-gather.8.cloned.1.call-done) | data formatting | bytes 9437184 | tf_op jit(solution)/shard_map/reshape | solution.py:80
  104.3 23.6 %all-gather.6.cloned.1.call-done = bf16[2,288,3072]{2,1,0:T(8,128)(2,1)} async-done(((bf16[2,288,384]{2,1,0:T(8,128)(2,1)}), bf16[2,288,3072]{2,1,0:T(8,128)(2,1)}) %all-gather.6.cloned.1.call-update) | async-done | bytes 3538960 | tf_op jit(solution)/shard_map/all_gather | solution.py:133
  127.9 6.8 %fusion.6 = f32[2,288,3,2,128]{4,1,3,2,0:T(8,128)S(1)} fusion(bf16[3072,3,2,128]{0,3,2,1:T(8,128)(2,1)} %copy.38, bf16[2,288,3072]{2,1,0:T(8,128)(2,1)} %all-gather.6.cloned.1.call-done), kind=kOutput, calls=%fused_computation.8 | convolution fusion | flops 2717908992 | bytes 10027008 | tf_op jit(solution)/shard_map/dot_general | solution.py:79
  134.7 0.5 multiply_reduce_fusion.1
  135.2 0.5 copy.31
  135.7 0.5 copy.29
  136.2 0.4 multiply_multiply_fusion.1
  136.6 0.4 multiply_multiply_fusion.2
  137.0 0.8 subtract_convert_fusion.1
  137.8 0.6 pad_maximum_fusion.2
  138.4 0.5 copy.30
  138.9 0.6 pad_maximum_fusion.3
  139.4 0.5 copy.32
  139.9 0.2 broadcast_in_dim.23
  140.1 0.2 broadcast_in_dim.29
  140.3 1.7 pad_maximum_fusion
  142.0 10.1 %all-to-all-start = ((bf16[16,648,128]{2,1,0:T(8,128)(2,1)}), bf16[16,648,128]{2,1,0:T(8,128)(2,1)S(1)}, u32[]{:S(2)}, u32[]{:S(2)}) async-start(bf16[16,648,128]{2,1,0:T(8,128)(2,1)} %pad_maximum_fusion), calls=%async_computation | async-start | bytes 5308416 | tf_op jit(solution)/shard_map/all_to_all | solution.py:174
  152.1 0.2 all-gather.10.cloned.1.call-start
  152.3 0.4 all-gather.10.cloned.1.call-update
  152.7 0.6 dynamic_slice.10
  153.3 0.7 fusion.54
  154.0 100.2 %all-to-all-done = bf16[16,648,128]{2,1,0:T(8,128)(2,1)S(1)} async-done(((bf16[16,648,128]{2,1,0:T(8,128)(2,1)}), bf16[16,648,128]{2,1,0:T(8,128)(2,1)S(1)}, u32[]{:S(2)}, u32[]{:S(2)}) %all-to-all-start) | async-done | bytes 2654240 | tf_op jit(solution)/shard_map/all_to_all | solution.py:174
  254.1 0.2 fusion.69
  254.3 3.5 fusion.70
  257.8 4.2 fusion.1
  262.1 2.8 copy-done.2
  264.9 11.1 %fusion.12 = bf16[1152,128]{1,0:T(8,128)(2,1)} fusion(bf16[4608,128]{1,0:T(8,128)(2,1)S(1)} %bitcast.103, f32[1152,4608]{1,0:T(8,128)} %copy-done.2, f32[1152]{0:T(1024)S(1)} %get-tuple-element.30, f32[1152]{0:T(1024)S(1)} %fusion.1), kind=kOutput, calls=%fused_computation.14 | convolution fusion | flops 1369866240 | bytes 22717440 | tf_op jit(solution)/shard_map/dot_general | solution.py:192
  276.0 6.7 %all-to-all-start.1 = ((bf16[16,72,128]{2,1,0:T(8,128)(2,1)}), bf16[16,72,128]{2,1,0:T(8,128)(2,1)S(1)}, u32[]{:S(2)}, u32[]{:S(2)}) async-start(bf16[16,72,128]{2,1,0:T(8,128)(2,1)} %bitcast.28), calls=%async_computation.1 | async-start | bytes 589824 | tf_op jit(solution)/shard_map/all_to_all | solution.py:196
  282.7 0.3 reduce-scatter.4.cloned.1.call-start
  283.0 54.5 %all-gather.14.cloned.1.call-done = bf16[768,3072]{0,1:T(8,128)(2,1)} async-done(((bf16[768,192]{0,1:T(8,128)(2,1)}), bf16[768,3072]{0,1:T(8,128)(2,1)}) %all-gather.14.cloned.1.call-update) | async-done | bytes 4718608 | tf_op jit(solution)/shard_map/all_gather | solution.py:205
  337.5 15.0 %fusion.29 = f32[576,3072]{1,0:T(8,128)} fusion(bf16[768,3072]{0,1:T(8,128)(2,1)} %all-gather.14.cloned.1.call-done, bf16[576,3072]{1,0:T(8,128)(2,1)} %bitcast.123, bf16[3072,768]{1,0:T(8,128)(2,1)} %all-gather.12.cloned.1.call-done), kind=kOutput, calls=%fused_computation.33 | convolution fusion | flops 5439799296 | bytes 20054016 | tf_op jit(solution)/shard_map/dot_general | solution.py:88
  352.5 0.2 copy.33
  352.7 46.0 %all-gather.10.cloned.1.call-done = bf16[256,3072]{0,1:T(8,128)(2,1)} async-done(((bf16[256,192]{0,1:T(8,128)(2,1)}), bf16[256,3072]{0,1:T(8,128)(2,1)}) %all-gather.10.cloned.1.call-update) | async-done | bytes 1572880 | tf_op jit(solution)/shard_map/all_gather | solution.py:204
  398.7 6.5 %add_convert_fusion = bf16[576,3072]{1,0:T(8,128)(2,1)} fusion(f32[576,3072]{1,0:T(8,128)} %fusion.29, bf16[256,3072]{0,1:T(8,128)(2,1)} %all-gather.10.cloned.1.call-done, bf16[72,8,2,128]{3,2,1,0:T(2,128)(2,1)S(1)} %bitcast.113), kind=kOutput, calls=%fused_computation.7 | convolution fusion | flops 909508608 | bytes 12484608 | tf_op jit(solution)/shard_map/dot_general | solution.py:87
  405.2 12.3 %copy.39 = bf16[2,288,3072]{1,0,2:T(2,128)(2,1)} copy(bf16[2,288,3072]{2,1,0:T(8,128)(2,1)} %bitcast.102) | data formatting | bytes 7077888
  417.5 10.2 %reshape.318 = bf16[3072,576]{1,0:T(8,128)(2,1)} reshape(bf16[3072,2,288]{2,1,0:T(2,128)(2,1)} %bitcast.101) | data formatting | bytes 7077888
  427.7 37.4 %reduce-scatter.4.cloned.1.call-done = bf16[384,576]{1,0:T(8,128)(2,1)} async-done(((bf16[3072,576]{1,0:T(8,128)(2,1)}), bf16[384,576]{1,0:T(8,128)(2,1)}) %reduce-scatter.4.cloned.1.call-update) | async-done | bytes 442384
  465.0 2.2 reshape.319
  467.2 0.7 copy.40
  467.9 0.1 fusion.28
  468.1 0.8 slice_bitcast_fusion.2
  468.9 3.5 all-to-all-start.2
  472.4 0.6 slice_bitcast_fusion.3
  473.0 5.2 %all-to-all-done.2 = bf16[2,1,256,384]{3,2,1,0:T(8,128)(2,1)S(1)} async-done(((bf16[2,1,256,384]{3,2,1,0:T(8,128)(2,1)}), bf16[2,1,256,384]{3,2,1,0:T(8,128)(2,1)S(1)}, u32[]{:S(2)}, u32[]{:S(2)}) %all-to-all-start.2) | async-done | bytes 393248 | tf_op jit(solution)/shard_map/all_to_all | solution.py:217
  478.2 0.1 bitcast_convert_fusion
  478.3 1.0 multiply_add_fusion
  (30 shorter events, 0.4 us)
Async XLA Ops:
  7.2 2.3 copy-start
  7.2 84.7 %all-gather.8.cloned.1.call-start = ((), (), s32[]{:S(2)}) async-start(), calls=%async_computation.5 | async-start | bytes 5013504 | tf_op jit(solution)/shard_map/all_gather | solution.py:138
  7.9 120.0 %all-gather.6.cloned.1.call-start = ((), (), s32[]{:S(2)}) async-start(), calls=%async_computation.4 | async-start | bytes 3981312 | tf_op jit(solution)/shard_map/all_gather | solution.py:133
  74.5 208.5 %all-gather.12.cloned.1.call-start = ((), (), s32[]{:S(2)}) async-start(), calls=%async_computation.7 | async-start | bytes 5013504 | tf_op jit(solution)/shard_map/all_gather | solution.py:139
  75.2 262.3 %all-gather.14.cloned.1.call-start = ((), (), s32[]{:S(2)}) async-start(), calls=%async_computation.8 | async-start | bytes 5013504 | tf_op jit(solution)/shard_map/all_gather | solution.py:205
  142.0 10.8 %copy-start.5 = (s32[2]{0:T(128)S(1)}, s32[2]{0:T(128)}, u32[]{:S(2)}) copy-start(s32[2]{0:T(128)} %param.22) | copy-start | bytes 28
  142.0 112.2 %all-to-all-start = ((bf16[16,648,128]{2,1,0:T(8,128)(2,1)}), bf16[16,648,128]{2,1,0:T(8,128)(2,1)S(1)}, u32[]{:S(2)}, u32[]{:S(2)}) async-start(bf16[16,648,128]{2,1,0:T(8,128)(2,1)} %pad_maximum_fusion), calls=%async_computation | async-start | bytes 5308416 | tf_op jit(solution)/shard_map/all_to_all | solution.py:174
  152.1 246.6 %all-gather.10.cloned.1.call-start = ((), (), s32[]{:S(2)}) async-start(), calls=%async_computation.6 | async-start | bytes 1671168 | tf_op jit(solution)/shard_map/all_gather | solution.py:204
  257.8 7.1 %copy-start.2 = (f32[1152,4608]{1,0:T(8,128)}, f32[1152,4608]{1,0:T(8,128)S(1)}, u32[]{:S(2)}) copy-start(f32[1152,4608]{1,0:T(8,128)S(1)} %get-tuple-element.31) | copy-start | bytes 63700996
  276.0 76.5 %all-to-all-start.1 = ((bf16[16,72,128]{2,1,0:T(8,128)(2,1)}), bf16[16,72,128]{2,1,0:T(8,128)(2,1)S(1)}, u32[]{:S(2)}, u32[]{:S(2)}) async-start(bf16[16,72,128]{2,1,0:T(8,128)(2,1)} %bitcast.28), calls=%async_computation.1 | async-start | bytes 589824 | tf_op jit(solution)/shard_map/all_to_all | solution.py:196
  282.7 182.3 %reduce-scatter.4.cloned.1.call-start = ((), (), s32[]{:S(2)}) async-start(), calls=%async_computation.9 | async-start | bytes 4423680
  427.6 40.3 %copy-start.3 = (bf16[2,256,384]{2,1,0:T(8,128)(2,1)S(1)}, bf16[2,256,384]{2,1,0:T(8,128)(2,1)}, u32[]{:S(2)}) copy-start(bf16[2,256,384]{2,1,0:T(8,128)(2,1)} %param.13) | copy-start | bytes 1179652
  427.6 40.3 %copy-start.4 = (bf16[1,2,32,384]{3,2,1,0:T(8,128)(2,1)S(1)}, bf16[1,2,32,384]{3,2,1,0:T(8,128)(2,1)}, u32[]{:S(2)}) copy-start(bf16[1,2,32,384]{3,2,1,0:T(8,128)(2,1)} %param.12) | copy-start | bytes 147460
  465.0 14.2 %copy-start.1 = (bf16[192,3,384]{2,0,1:T(8,128)(2,1)S(1)}, bf16[192,3,384]{2,0,1:T(8,128)(2,1)}, u32[]{:S(2)}) copy-start(bf16[192,3,384]{2,0,1:T(8,128)(2,1)} %param.15) | copy-start | bytes 1327108
  468.9 9.3 %all-to-all-start.2 = ((bf16[2,1,256,384]{3,2,1,0:T(8,128)(2,1)}), bf16[2,1,256,384]{3,2,1,0:T(8,128)(2,1)S(1)}, u32[]{:S(2)}, u32[]{:S(2)}) async-start(bf16[2,1,256,384]{3,2,1,0:T(8,128)(2,1)} %slice_bitcast_fusion.2), calls=%async_computation.2 | async-start | bytes 786432 | tf_op jit(solution)/shard_map/all_to_all | solution.py:217
Sparse Core Ops, SparseCore 0:
  10.4 81.3 all-gather.7
  93.7 34.1 all-gather.5
  130.3 120.7 all-gather.11
  253.4 84.1 all-gather.13
  339.8 58.8 all-gather.9
  427.8 37.2 reduce-scatter.3

commit v2 on v1

--- a/solution.py
+++ b/solution.py
@@ -130,15 +130,20 @@
     normed = (
         (hidden - average) * lax.rsqrt(variance + epsilon) * (1.0 + modulation[1]) + modulation[0]
     ).astype(jnp.bfloat16)
+    width_rows = qkv_weight.shape[0]
+    qkv_cols = 3 * heads_local * HD
+    in_weight = lax.all_gather(
+        jnp.concatenate([qkv_weight.reshape(width_rows, qkv_cols), up_weight], axis=1),
+        "seq",
+        axis=0,
+        tiled=True,
+    )
+    normed, in_weight = lax.optimization_barrier((normed, in_weight))
     gathered = lax.all_gather(normed, "wblk", axis=2, tiled=True)
     token_rows = gathered.reshape(row_count, D)
-    projected, mlp_units = input_folder(
-        token_rows,
-        (
-            lax.all_gather(qkv_weight, "seq", axis=0, tiled=True),
-            lax.all_gather(up_weight, "seq", axis=0, tiled=True),
-        ),
-    )
+    both = jnp.dot(token_rows, in_weight, preferred_element_type=jnp.float32)
+    projected = both[:, :qkv_cols]
+    mlp_units = both[:, qkv_cols:]
     projected = projected.reshape(prompts, local_len, 3, heads_local, HD)
     image_index = seq_pos * image_rows + jnp.arange(image_rows, dtype=jnp.int32)
     height_pos = jnp.concatenate(
@@ -197,13 +202,13 @@
     attended = returned.reshape(prompts, heads_local, local_len, HD)
     attended = attended.transpose(0, 2, 1, 3).reshape(row_count, heads_local * HD)
     activated = jax.nn.gelu(mlp_units, approximate=True).astype(jnp.bfloat16)
-    branch_terms = output_folder(
-        attended,
-        activated,
-        (
-            lax.all_gather(attn_weight, "seq", axis=1, tiled=True),
-            lax.all_gather(down_weight, "seq", axis=1, tiled=True),
-        ),
+    out_weight = lax.all_gather(
+        jnp.concatenate([attn_weight, down_weight], axis=0), "seq", axis=1, tiled=True
+    )
+    branch_terms = jnp.dot(
+        jnp.concatenate([attended, activated], axis=1),
+        out_weight,
+        preferred_element_type=jnp.float32,
     )
     branch = lax.psum_scatter(
         branch_terms.reshape(prompts, local_len, D).astype(jnp.bfloat16),

time: 488 us -> 441 us (0.904)
  waiting for transfers between devices: 283 us -> 244 us
  blocking collectives: 61.4 us -> 78.9 us
  matrix products: 43 us -> 31.2 us
  local copies, waits for them, and re-layouts: 47.1 us -> 39.3 us
  starting transfers between devices: 20.9 us -> 13.9 us
    all_gather x4 -> x2, waiting for transfers between devices: 114 us -> 58.6 us  [the longest x1 58.6 us: shards(): lax.all_gather(jnp.concatenate([qkv_weight.reshape(width_rows, qkv_cols),...]
    all_to_all x0 -> x1, blocking collectives: none -> 15.2 us  [shards(): returned = lax.all_to_all(mixed, 'seq', 0, 0, tiled=True)]
    all_gather x1, waiting for transfers between devices: 23.6 us -> 36.7 us  [shards(): gathered = lax.all_gather(normed, 'wblk', axis=2, tiled=True)]
    dot_general x3 -> x2, matrix products: 28.2 us -> 17.4 us  [the longest x1 9.27 us: shards(): both = jnp.dot(token_rows, in_weight, preferred_element_type=jnp.float32)]
    reshape x1 -> x2, local copies, waits for them, and re-layouts: 12.4 us -> 3.3 us  [the longest x1 2.11 us: shards(): projected = projected.reshape(prompts, local_len, 3, heads_local, HD)]
    all_to_all x1 -> x0, starting transfers between devices: 6.69 us -> none  [shards(): returned = lax.all_to_all(mixed, 'seq', 0, 0, tiled=True)]
    unnamed x16 -> x30, local copies, waits for them, and re-layouts: 28.2 us -> 29.2 us
    unnamed x7 -> x5, waiting for transfers between devices: 39.6 us -> 39.7 us
  transfers between devices with their start and end apart: 9 -> 6, of which waited for: 7 -> 5; matrix products, arithmetic and copies ran while one was open for 14% -> 11% of each run, Pallas kernels for 0% -> 0%
where the time goes in v2:
time: 441 us; the launch traced here: 440 us
  waiting for transfers between devices  244 us (55%)
  blocking collectives  78.9 us (18%)
  local copies, waits for them, and re-layouts  39.3 us (9%)
  matrix products  31.2 us (7%)
  other arithmetic  18 us (4%)
  between operations  15 us (3%)
  starting transfers between devices  13.9 us (3%)
    all_to_all x1, waiting for transfers between devices, shards(): received = lax.all_to_all(send, 'seq', 0, 0, tiled=True)  104 us
    all_gather x1, waiting for transfers between devices, shards(): lax.all_gather(jnp.concatenate([qkv_weight.reshape(width_rows, qkv_cols),...  58.6 us
    psum x1, blocking collectives, shards(): modulation = lax.psum(mod_terms.reshape(3, dim_local), 'seq')  48.5 us
    unnamed x5, waiting for transfers between devices  39.7 us
    all_gather x1, waiting for transfers between devices, shards(): gathered = lax.all_gather(normed, 'wblk', axis=2, tiled=True)  36.7 us
    unnamed x30, local copies, waits for them, and re-layouts  29.2 us
    all_to_all x1, blocking collectives, shards(): returned = lax.all_to_all(mixed, 'seq', 0, 0, tiled=True)  15.2 us
    psum x1, blocking collectives, shards(): lax.psum((jnp.sum(hidden, axis=-1), jnp.sum(hidden * hidden, axis=-1)), '...  15.1 us
  transfers between devices with their start and end apart: 6, of which 5 were waited for; matrix products, arithmetic and copies ran while one was open for 11% of the time, Pallas kernels for 0%

profile of v2, /device:TPU:2, one launch (start us, length us, event | category | flops | bytes accessed | tf_op | source)
XLA Modules:
  0.0 440.3 jit_solution(17777463775007592388)
XLA Ops:
  7.3 1.2 reshape.288
  8.5 1.8 pad_maximum_fusion.1
  10.3 0.0 all-gather.6.cloned.1.call-start
  11.1 0.1 fusion.47
  11.1 0.8 fusion.55
  11.9 0.2 fusion.29
  12.1 0.3 convert_reduce_fusion
  12.5 15.1 %all-reduce.2 = (f32[2,288]{1,0:T(2,128)S(1)}, f32[2,288]{1,0:T(2,128)S(1)}) all-reduce(f32[2,288]{1,0:T(2,128)S(1)} %get-tuple-element.8, f32[2,288]{1,0:T(2,128)S(1)} %get-tuple-element.7), channel_id=1, replica_groups=mesh['cfg'=2,'seq'=16,'wblk'=8] {'wblk'}, use_global_device_ids=true, to_apply=%region_4.5 | all-reduce | flops 1152 | bytes 9216 | tf_op jit(solution)/shard_map/psum | solution.py:125
  27.6 48.5 %psum.21 = f32[3,384]{1,0:T(4,128)S(1)} all-reduce(f32[3,384]{1,0:T(4,128)S(1)} %bitcast.108), channel_id=1, replica_groups=mesh['cfg'=2,'seq'=16,'wblk'=8] {'seq'}, use_global_device_ids=true, to_apply=%region_0.1 | all-reduce | flops 1152 | bytes 9216 | tf_op jit(solution)/shard_map/psum | solution.py:122
  76.1 1.1 fusion.26
  77.2 58.6 %all-gather.4.cloned.1.call-done = bf16[3072,1536]{1,0:T(8,128)(2,1)} async-done(((bf16[192,1536]{1,0:T(8,128)(2,1)}), bf16[3072,1536]{1,0:T(8,128)(2,1)}) %all-gather.4.cloned.1.call-update) | async-done | bytes 9437200 | tf_op jit(solution)/shard_map/all_gather | solution.py:135
  135.8 0.0 all-gather.8.cloned.1.call-start
  135.8 0.8 pad_maximum_fusion.5
  136.7 0.1 mul.324
  136.8 0.1 mul.305
  137.0 0.1 concatenate.38
  137.1 0.1 concatenate.39
  137.1 0.1 broadcast_multiply_fusion.1
  137.2 0.4 fusion.36
  137.6 36.7 %all-gather.6.cloned.1.call-done = bf16[2,288,3072]{2,1,0:T(8,128)(2,1)} async-done(((bf16[2,288,384]{2,1,0:T(8,128)(2,1)}), bf16[2,288,3072]{2,1,0:T(8,128)(2,1)}) %all-gather.6.cloned.1.call-update) | async-done | bytes 3538960 | tf_op jit(solution)/shard_map/all_gather | solution.py:142
  174.3 9.3 %fusion.62 = f32[576,1536]{1,0:T(8,128)S(1)} fusion(bf16[576,3072]{1,0:T(8,128)(2,1)} %bitcast.110, bf16[3072,1536]{1,0:T(8,128)(2,1)} %all-gather.4.cloned.1.call-done), kind=kOutput, calls=%fused_computation.115 | convolution fusion | flops 5435817984 | bytes 16515072 | tf_op jit(solution)/shard_map/dot_general | solution.py:144
  183.6 1.5 fusion.58
  185.0 2.1 reshape.290
  187.2 1.3 slice.87
  188.4 1.4 fusion.60
  189.8 0.5 copy.35
  190.3 0.5 copy.34
  190.8 0.4 multiply_reduce_fusion
  191.2 0.4 multiply_reduce_fusion.1
  191.6 0.4 multiply_multiply_fusion.1
  191.9 0.4 multiply_multiply_fusion.2
  192.3 0.8 subtract_convert_fusion.1
  193.1 0.6 pad_maximum_fusion.3
  193.7 0.5 copy.24
  194.2 0.6 pad_maximum_fusion.4
  194.8 0.5 copy.27
  195.3 0.2 broadcast_in_dim.23
  195.5 0.2 broadcast_in_dim.29
  195.7 1.7 pad_maximum_fusion
  197.4 10.1 %all-to-all-start = ((bf16[16,648,128]{2,1,0:T(8,128)(2,1)}), bf16[16,648,128]{2,1,0:T(8,128)(2,1)S(1)}, u32[]{:S(2)}, u32[]{:S(2)}) async-start(bf16[16,648,128]{2,1,0:T(8,128)(2,1)} %pad_maximum_fusion), calls=%async_computation | async-start | bytes 5308416 | tf_op jit(solution)/shard_map/all_to_all | solution.py:179
  207.5 0.2 reduce-scatter.4.cloned.1.call-start
  207.8 0.6 dynamic_slice.10
  208.4 0.7 fusion.46
  209.0 103.9 %all-to-all-done = bf16[16,648,128]{2,1,0:T(8,128)(2,1)S(1)} async-done(((bf16[16,648,128]{2,1,0:T(8,128)(2,1)}), bf16[16,648,128]{2,1,0:T(8,128)(2,1)S(1)}, u32[]{:S(2)}, u32[]{:S(2)}) %all-to-all-start) | async-done | bytes 2654240 | tf_op jit(solution)/shard_map/all_to_all | solution.py:179
  313.0 0.2 fusion.59
  313.2 3.5 fusion.61
  316.6 4.2 fusion.1
  320.9 2.8 copy-done.2
  323.7 10.2 %fusion.9 = bf16[1152,128]{1,0:T(8,128)(2,1)S(1)} fusion(bf16[4608,128]{1,0:T(8,128)(2,1)S(1)} %bitcast.89, f32[1152,4608]{1,0:T(8,128)} %copy-done.2, f32[1152]{0:T(1024)S(1)} %get-tuple-element.34, f32[1152]{0:T(1024)S(1)} %fusion.1), kind=kOutput, calls=%fused_computation.11 | convolution fusion | flops 1369866240 | bytes 22717440 | tf_op jit(solution)/shard_map/dot_general | solution.py:197
  333.9 15.2 %all_to_all.19 = bf16[16,72,128]{2,1,0:T(8,128)(2,1)S(1)} all-to-all(bf16[16,72,128]{2,1,0:T(8,128)(2,1)S(1)} %bitcast.96), channel_id=1, replica_groups=mesh['cfg'=2,'seq'=16,'wblk'=8] {'seq'}, dimensions={0} | all-to-all | bytes 589824 | tf_op jit(solution)/shard_map/all_to_all | solution.py:201
  349.1 0.2 copy.28
  349.4 8.1 %convolution_convert_fusion = bf16[576,3072]{1,0:T(8,128)(2,1)} fusion(bf16[1024,3072]{0,1:T(8,128)(2,1)} %all-gather.8.cloned.1.call-done, bf16[576,768]{1,0:T(8,128)(2,1)S(1)} %copy-done.4, bf16[576,256]{1,0:T(8,128)(2,1)S(1)} %bitcast.107), kind=kOutput, calls=%fused_computation.7 | convolution fusion | flops 3628007424 | bytes 11010048 | tf_op jit(solution)/shard_map/dot_general | solution.py:208
  357.6 12.3 %copy.32 = bf16[2,288,3072]{1,0,2:T(2,128)(2,1)} copy(bf16[2,288,3072]{2,1,0:T(8,128)(2,1)} %bitcast.93) | data formatting | bytes 7077888
  369.9 10.2 %reshape.316 = bf16[3072,576]{1,0:T(8,128)(2,1)} reshape(bf16[3072,2,288]{2,1,0:T(2,128)(2,1)} %bitcast.86) | data formatting | bytes 7077888
  380.0 39.6 %reduce-scatter.4.cloned.1.call-done = bf16[384,576]{1,0:T(8,128)(2,1)} async-done(((bf16[3072,576]{1,0:T(8,128)(2,1)}), bf16[384,576]{1,0:T(8,128)(2,1)}) %reduce-scatter.4.cloned.1.call-update) | async-done | bytes 442384
  419.7 2.1 reshape.317
  421.8 0.7 copy.33
  422.5 0.1 fusion.28
  422.7 0.8 slice_bitcast_fusion.2
  423.5 3.5 all-to-all-start.2
  427.0 0.6 slice_bitcast_fusion.3
  427.6 5.2 %all-to-all-done.2 = bf16[2,1,256,384]{3,2,1,0:T(8,128)(2,1)S(1)} async-done(((bf16[2,1,256,384]{3,2,1,0:T(8,128)(2,1)}), bf16[2,1,256,384]{3,2,1,0:T(8,128)(2,1)S(1)}, u32[]{:S(2)}, u32[]{:S(2)}) %all-to-all-start.2) | async-done | bytes 393248 | tf_op jit(solution)/shard_map/all_to_all | solution.py:222
  432.8 0.1 bitcast_convert_fusion
  432.8 1.0 multiply_add_fusion
  (40 shorter events, 0.4 us)
Async XLA Ops:
  7.2 4.8 %copy-start = (bf16[192,3,384]{2,0,1:T(8,128)(2,1)S(1)}, bf16[192,3,384]{2,0,1:T(8,128)(2,1)}, u32[]{:S(2)}) copy-start(bf16[192,3,384]{2,0,1:T(8,128)(2,1)} %param.15) | copy-start | bytes 1327108
  7.2 4.9 %copy-start.5 = (bf16[1,2,32,384]{3,2,1,0:T(8,128)(2,1)S(1)}, bf16[1,2,32,384]{3,2,1,0:T(8,128)(2,1)}, u32[]{:S(2)}) copy-start(bf16[1,2,32,384]{3,2,1,0:T(8,128)(2,1)} %param.12) | copy-start | bytes 147460
  7.2 4.9 %copy-start.3 = (bf16[2,256,384]{2,1,0:T(8,128)(2,1)S(1)}, bf16[2,256,384]{2,1,0:T(8,128)(2,1)}, u32[]{:S(2)}) copy-start(bf16[2,256,384]{2,1,0:T(8,128)(2,1)} %param.13) | copy-start | bytes 1179652
  7.2 128.6 %copy-start.7 = (bf16[256,192]{0,1:T(8,128)(2,1)S(1)}, bf16[256,192]{0,1:T(8,128)(2,1)}, u32[]{:S(2)}) copy-start(bf16[256,192]{0,1:T(8,128)(2,1)} %param.20) | copy-start | bytes 294916
  7.2 128.6 %copy-start.6 = (bf16[768,192]{0,1:T(8,128)(2,1)S(1)}, bf16[768,192]{0,1:T(8,128)(2,1)}, u32[]{:S(2)}) copy-start(bf16[768,192]{0,1:T(8,128)(2,1)} %param.21) | copy-start | bytes 884740
  7.2 128.5 %all-gather.4.cloned.1.call-start = ((), (), s32[]{:S(2)}) async-start(), calls=%async_computation.4 | async-start | bytes 10027008 | tf_op jit(solution)/shard_map/all_gather | solution.py:135
  8.5 128.2 %copy-start.8 = (f32[128]{0:T(128)S(1)}, f32[128]{0:T(128)}, u32[]{:S(2)}) copy-start(f32[128]{0:T(128)} %param.18) | copy-start | bytes 1540
  8.5 128.4 %copy-start.9 = (f32[128]{0:T(128)S(1)}, f32[128]{0:T(128)}, u32[]{:S(2)}) copy-start(f32[128]{0:T(128)} %param.19) | copy-start | bytes 1540
  10.3 164.0 %all-gather.6.cloned.1.call-start = ((), (), s32[]{:S(2)}) async-start(), calls=%async_computation.5 | async-start | bytes 3981312 | tf_op jit(solution)/shard_map/all_gather | solution.py:142
  135.8 213.7 %all-gather.8.cloned.1.call-start = ((), (), s32[]{:S(2)}) async-start(), calls=%async_computation.6 | async-start | bytes 6684672 | tf_op jit(solution)/shard_map/all_gather | solution.py:205
  197.4 10.4 %copy-start.10 = (s32[2]{0:T(128)S(1)}, s32[2]{0:T(128)}, u32[]{:S(2)}) copy-start(s32[2]{0:T(128)} %param.22) | copy-start | bytes 28
  197.4 115.6 %all-to-all-start = ((bf16[16,648,128]{2,1,0:T(8,128)(2,1)}), bf16[16,648,128]{2,1,0:T(8,128)(2,1)S(1)}, u32[]{:S(2)}, u32[]{:S(2)}) async-start(bf16[16,648,128]{2,1,0:T(8,128)(2,1)} %pad_maximum_fusion), calls=%async_computation | async-start | bytes 5308416 | tf_op jit(solution)/shard_map/all_to_all | solution.py:179
  207.5 212.2 %reduce-scatter.4.cloned.1.call-start = ((), (), s32[]{:S(2)}) async-start(), calls=%async_computation.7 | async-start | bytes 4423680
  316.6 7.1 %copy-start.2 = (f32[1152,4608]{1,0:T(8,128)}, f32[1152,4608]{1,0:T(8,128)S(1)}, u32[]{:S(2)}) copy-start(f32[1152,4608]{1,0:T(8,128)S(1)} %get-tuple-element.35) | copy-start | bytes 63700996
  323.7 25.7 %copy-start.4 = (bf16[576,768]{1,0:T(8,128)(2,1)S(1)}, bf16[576,768]{1,0:T(8,128)(2,1)}, u32[]{:S(2)}) copy-start(bf16[576,768]{1,0:T(8,128)(2,1)} %get-tuple-element.17) | copy-start | bytes 2654212
  422.5 11.3 %copy-start.1 = (bf16[192,3,384]{2,0,1:T(8,128)(2,1)S(1)}, bf16[192,3,384]{2,0,1:T(8,128)(2,1)}, u32[]{:S(2)}) copy-start(bf16[192,3,384]{2,0,1:T(8,128)(2,1)} %param.15) | copy-start | bytes 1327108
  423.5 9.3 %all-to-all-start.2 = ((bf16[2,1,256,384]{3,2,1,0:T(8,128)(2,1)}), bf16[2,1,256,384]{3,2,1,0:T(8,128)(2,1)S(1)}, u32[]{:S(2)}, u32[]{:S(2)}) async-start(bf16[2,1,256,384]{3,2,1,0:T(8,128)(2,1)} %slice_bitcast_fusion.2), calls=%async_computation.2 | async-start | bytes 786432 | tf_op jit(solution)/shard_map/all_to_all | solution.py:222
Sparse Core Ops, SparseCore 0:
  10.5 125.2 all-gather.3
  137.6 36.6 all-gather.5
  177.3 143.5 all-gather.7
  380.1 39.4 reduce-scatter.3

commit v3 on v2

--- a/solution.py
+++ b/solution.py
@@ -138,10 +138,15 @@
         axis=0,
         tiled=True,
     )
-    normed, in_weight = lax.optimization_barrier((normed, in_weight))
-    gathered = lax.all_gather(normed, "wblk", axis=2, tiled=True)
-    token_rows = gathered.reshape(row_count, D)
-    both = jnp.dot(token_rows, in_weight, preferred_element_type=jnp.float32)
+    wblk_count = lax.psum(1, "wblk")
+    spread = jnp.broadcast_to(normed.reshape(1, row_count, dim_local), (wblk_count, row_count, dim_local))
+    gathered = lax.all_to_all(spread, "wblk", 0, 0, tiled=True)
+    both = jnp.einsum(
+        "wrf,wfn->rn",
+        gathered,
+        in_weight.reshape(wblk_count, dim_local, -1),
+        preferred_element_type=jnp.float32,
+    )
     projected = both[:, :qkv_cols]
     mlp_units = both[:, qkv_cols:]
     projected = projected.reshape(prompts, local_len, 3, heads_local, HD)
@@ -202,20 +207,20 @@
     attended = returned.reshape(prompts, heads_local, local_len, HD)
     attended = attended.transpose(0, 2, 1, 3).reshape(row_count, heads_local * HD)
     activated = jax.nn.gelu(mlp_units, approximate=True).astype(jnp.bfloat16)
-    out_weight = lax.all_gather(
-        jnp.concatenate([attn_weight, down_weight], axis=0), "seq", axis=1, tiled=True
-    )
-    branch_terms = jnp.dot(
+    out_source, in_weight = lax.optimization_barrier(
+        (jnp.concatenate([attn_weight, down_weight], axis=0), in_weight)
+    )
+    out_weight = lax.all_gather(out_source, "seq", axis=1, tiled=True)
+    terms_by_feature = lax.dot_general(
+        out_weight,
         jnp.concatenate([attended, activated], axis=1),
-        out_weight,
+        (((0,), (1,)), ((), ())),
         preferred_element_type=jnp.float32,
     )
     branch = lax.psum_scatter(
-        branch_terms.reshape(prompts, local_len, D).astype(jnp.bfloat16),
-        "wblk",
-        scatter_dimension=2,
-        tiled=True,
-    ).astype(jnp.float32)
+        terms_by_feature.astype(jnp.bfloat16), "wblk", scatter_dimension=0, tiled=True
+    )
+    branch = branch.T.reshape(prompts, local_len, dim_local).astype(jnp.float32)
     layer_out = hidden + modulation[2] * branch
     text_out = layer_out[:, :text_rows].astype(jnp.bfloat16)[None]
     image_out = layer_out[:, text_rows:]

time: 441 us -> 391 us (0.89)
  waiting for transfers between devices: 244 us -> 198 us
  local copies, waits for them, and re-layouts: 39.3 us -> 24.8 us
  starting transfers between devices: 13.9 us -> 24.4 us
    all_gather x2 -> x1, waiting for transfers between devices: 36.7 us -> 0.02 us  [shards(): out_weight = lax.all_gather(out_source, 'seq', axis=1, tiled=True)]
    unnamed x30 -> x36, local copies, waits for them, and re-layouts: 29.2 us -> 11.3 us
    all_gather x1, waiting for transfers between devices: 58.6 us -> 47.5 us  [shards(): lax.all_gather(jnp.concatenate([qkv_weight.reshape(width_rows, qkv_cols),...]
    all_to_all x1, starting transfers between devices: 10.1 us -> 16 us  [shards(): received = lax.all_to_all(send, 'seq', 0, 0, tiled=True)]
    all_to_all x0 -> x1, starting transfers between devices: none -> 4.62 us  [shards(): gathered = lax.all_to_all(spread, 'wblk', 0, 0, tiled=True)]
    unnamed x5 -> x4, waiting for transfers between devices: 39.7 us -> 41.7 us
  transfers between devices with their start and end apart: 6 -> 6, of which waited for: 5 -> 4; matrix products, arithmetic and copies ran while one was open for 11% -> 13% of each run, Pallas kernels for 0% -> 0%
where the time goes in v3:
time: 391 us
  waiting for transfers between devices  198 us (51%)
  blocking collectives  79.4 us (20%)
  matrix products  31.2 us (8%)
  local copies, waits for them, and re-layouts  24.8 us (6%)
  starting transfers between devices  24.4 us (6%)
  other arithmetic  18 us (5%)
  between operations  15 us (4%)
    all_to_all x1, waiting for transfers between devices, shards(): received = lax.all_to_all(send, 'seq', 0, 0, tiled=True)  103 us
    all_gather x1, waiting for transfers between devices, shards(): lax.all_gather(jnp.concatenate([qkv_weight.reshape(width_rows, qkv_cols),...  47.5 us
    psum x1, blocking collectives, shards(): modulation = lax.psum(mod_terms.reshape(3, dim_local), 'seq')  47.1 us
    unnamed x4, waiting for transfers between devices  41.7 us
    all_to_all x1, blocking collectives, shards(): returned = lax.all_to_all(mixed, 'seq', 0, 0, tiled=True)  17.2 us
    all_to_all x1, starting transfers between devices, shards(): received = lax.all_to_all(send, 'seq', 0, 0, tiled=True)  16 us
    psum x1, blocking collectives, shards(): lax.psum((jnp.sum(hidden, axis=-1), jnp.sum(hidden * hidden, axis=-1)), '...  15.1 us
    unnamed x36, local copies, waits for them, and re-layouts  11.3 us
  transfers between devices with their start and end apart: 6, of which 4 were waited for; matrix products, arithmetic and copies ran while one was open for 13% of the time, Pallas kernels for 0%

profile of v3, /device:TPU:2, one launch (start us, length us, event | category | flops | bytes accessed | tf_op | source)
XLA Modules:
  0.0 390.6 jit_solution(6578100651269434871)
XLA Ops:
  7.3 1.2 reshape.336
  8.4 1.8 pad_maximum_fusion.1
  10.9 1.1 convert_reduce_fusion
  12.0 15.1 %all-reduce.2 = (f32[2,288]{1,0:T(2,128)S(1)}, f32[2,288]{1,0:T(2,128)S(1)}) all-reduce(f32[2,288]{1,0:T(2,128)S(1)} %get-tuple-element.6, f32[2,288]{1,0:T(2,128)S(1)} %get-tuple-element.5), channel_id=1, replica_groups=mesh['cfg'=2,'seq'=16,'wblk'=8] {'wblk'}, use_global_device_ids=true, to_apply=%region_4.5 | all-reduce | flops 1152 | bytes 9216 | tf_op jit(solution)/shard_map/psum | solution.py:125
  27.2 0.1 sub.85
  27.2 0.1 mul.308
  27.4 0.1 fusion.45
  27.4 0.1 fusion.53
  27.6 0.2 fusion.27
  27.8 47.1 %psum.21 = f32[3,384]{1,0:T(4,128)S(1)} all-reduce(f32[3,384]{1,0:T(4,128)S(1)} %bitcast.117), channel_id=1, replica_groups=mesh['cfg'=2,'seq'=16,'wblk'=8] {'seq'}, use_global_device_ids=true, to_apply=%region_0.1 | all-reduce | flops 1152 | bytes 9216 | tf_op jit(solution)/shard_map/psum | solution.py:122
  74.9 0.2 fusion.26
  75.2 2.1 broadcast_in_dim.23
  77.3 4.6 %all-to-all-start = ((bf16[8,576,384]{2,1,0:T(8,128)(2,1)}), bf16[8,576,384]{2,1,0:T(8,128)(2,1)}, u32[]{:S(2)}, u32[]{:S(2)}) async-start(bf16[8,576,384]{2,1,0:T(8,128)(2,1)} %broadcast_in_dim.23), calls=%async_computation | async-start | bytes 7077888 | tf_op jit(solution)/shard_map/all_to_all | solution.py:143
  82.0 0.1 concatenate.40
  82.0 0.1 concatenate.39
  82.1 0.7 mul.335
  82.9 0.8 mul.316
  83.6 0.8 pad_maximum_fusion.3
  84.4 0.1 broadcast_multiply_fusion.1
  84.5 1.0 fusion.34
  85.6 47.5 %all-gather.3.cloned.1.call-done = bf16[3072,1536]{1,0:T(8,128)(2,1)} async-done(((bf16[192,1536]{1,0:T(8,128)(2,1)}), bf16[3072,1536]{1,0:T(8,128)(2,1)}) %all-gather.3.cloned.1.call-update) | async-done | bytes 9437200 | tf_op jit(solution)/shard_map/all_gather | solution.py:135
  133.1 9.3 %convolution_bitcast_fusion = f32[576,1536]{1,0:T(8,128)S(1)} fusion(bf16[8,576,384]{2,1,0:T(8,128)(2,1)} %all-to-all-done, bf16[8,384,1536]{2,1,0:T(8,128)(2,1)} %bitcast.119), kind=kOutput, calls=%fused_computation.8 | convolution fusion | flops 5435817984 | bytes 16515072 | tf_op jit(solution)/shard_map/wrf,wfn->rn/dot_general | solution.py:144
  142.5 1.5 fusion.56
  143.9 2.1 reshape.338
  146.1 1.3 slice.90
  147.4 1.3 fusion.58
  148.7 0.5 copy.33
  149.2 0.5 copy.34
  149.8 0.4 multiply_reduce_fusion.2
  150.1 0.4 multiply_reduce_fusion.1
  150.5 0.4 multiply_multiply_fusion.2
  150.9 0.4 multiply_multiply_fusion.1
  151.3 0.8 subtract_convert_fusion.1
  152.1 0.6 pad_maximum_fusion.4
  152.7 0.5 copy.24
  153.2 0.6 pad_maximum_fusion.5
  153.7 0.5 copy.27
  154.2 0.2 broadcast_in_dim.26
  154.4 0.2 broadcast_in_dim.32
  154.6 1.7 pad_maximum_fusion
  156.3 16.0 %all-to-all-start.1 = ((bf16[16,648,128]{2,1,0:T(8,128)(2,1)}), bf16[16,648,128]{2,1,0:T(8,128)(2,1)S(1)}, u32[]{:S(2)}, u32[]{:S(2)}) async-start(bf16[16,648,128]{2,1,0:T(8,128)(2,1)} %pad_maximum_fusion), calls=%async_computation.1 | async-start | bytes 5308416 | tf_op jit(solution)/shard_map/all_to_all | solution.py:184
  172.3 0.2 reduce-scatter.4.cloned.1.call-start
  172.6 0.6 dynamic_slice.10
  173.1 0.7 fusion.44
  173.8 103.3 %all-to-all-done.1 = bf16[16,648,128]{2,1,0:T(8,128)(2,1)S(1)} async-done(((bf16[16,648,128]{2,1,0:T(8,128)(2,1)}), bf16[16,648,128]{2,1,0:T(8,128)(2,1)S(1)}, u32[]{:S(2)}, u32[]{:S(2)}) %all-to-all-start.1) | async-done | bytes 2654240 | tf_op jit(solution)/shard_map/all_to_all | solution.py:184
  277.2 0.2 fusion.57
  277.3 3.5 fusion.59
  280.8 4.2 %fusion.1 = f32[1152]{0:T(1024)S(1)} fusion(f32[1152,4608]{1,0:T(8,128)S(1)} %get-tuple-element.33, f32[1152]{0:T(1024)S(1)} %get-tuple-element.32), kind=kLoop, calls=%fused_computation.3 | loop fusion | flops 10615680 | bytes 21242880 | tf_op jit(solution)/shard_map/reduce_sum | solution.py:201
  285.1 2.8 copy-done.2
  287.9 10.2 %fusion.9 = bf16[1152,128]{1,0:T(8,128)(2,1)S(1)} fusion(bf16[4608,128]{1,0:T(8,128)(2,1)S(1)} %bitcast.99, f32[1152,4608]{1,0:T(8,128)} %copy-done.2, f32[1152]{0:T(1024)S(1)} %get-tuple-element.32, f32[1152]{0:T(1024)S(1)} %fusion.1), kind=kOutput, calls=%fused_computation.12 | convolution fusion | flops 1369866240 | bytes 22717440 | tf_op jit(solution)/shard_map/dot_general | solution.py:202
  298.1 17.2 %all_to_all.24 = bf16[16,72,128]{2,1,0:T(8,128)(2,1)S(1)} all-to-all(bf16[16,72,128]{2,1,0:T(8,128)(2,1)S(1)} %bitcast.105), channel_id=1, replica_groups=mesh['cfg'=2,'seq'=16,'wblk'=8] {'seq'}, dimensions={0} | all-to-all | bytes 589824 | tf_op jit(solution)/shard_map/all_to_all | solution.py:206
  315.2 0.2 copy.28
  315.6 8.1 %convolution_convert_fusion = bf16[3072,576]{0,1:T(8,128)(2,1)} fusion(bf16[1024,3072]{0,1:T(8,128)(2,1)} %all-gather.5.cloned.1.call-done, bf16[576,768]{1,0:T(8,128)(2,1)S(1)} %copy-done.4, bf16[576,256]{1,0:T(8,128)(2,1)S(1)} %bitcast.116), kind=kOutput, calls=%fused_computation.7 | convolution fusion | flops 3628007424 | bytes 11010048 | tf_op jit(solution)/shard_map/dot_general | solution.py:214
  323.7 6.1 %copy.31 = bf16[3072,576]{1,0:T(8,128)(2,1)} copy(bf16[3072,576]{0,1:T(8,128)(2,1)} %convolution_convert_fusion) | data formatting | bytes 7077888
  329.8 41.6 %reduce-scatter.4.cloned.1.call-done = bf16[384,576]{1,0:T(8,128)(2,1)} async-done(((bf16[3072,576]{1,0:T(8,128)(2,1)}), bf16[384,576]{1,0:T(8,128)(2,1)}) %reduce-scatter.4.cloned.1.call-update) | async-done | bytes 442384
  371.4 1.3 copy.32
  372.7 0.1 convert_element_type.112
  372.8 0.1 add_convert_fusion
  372.9 0.8 slice_bitcast_fusion.2
  373.7 3.5 all-to-all-start.3
  377.2 0.6 slice_bitcast_fusion.3
  377.8 5.2 %all-to-all-done.3 = bf16[2,1,256,384]{3,2,1,0:T(8,128)(2,1)S(1)} async-done(((bf16[2,1,256,384]{3,2,1,0:T(8,128)(2,1)}), bf16[2,1,256,384]{3,2,1,0:T(8,128)(2,1)S(1)}, u32[]{:S(2)}, u32[]{:S(2)}) %all-to-all-start.3) | async-done | bytes 393248 | tf_op jit(solution)/shard_map/all_to_all | solution.py:227
  383.0 0.1 bitcast_convert_fusion
  383.1 1.0 multiply_add_fusion
  (49 shorter events, 0.4 us)
Async XLA Ops:
  7.2 20.4 %copy-start = (bf16[192,3,384]{2,0,1:T(8,128)(2,1)S(1)}, bf16[192,3,384]{2,0,1:T(8,128)(2,1)}, u32[]{:S(2)}) copy-start(bf16[192,3,384]{2,0,1:T(8,128)(2,1)} %param.15) | copy-start | bytes 1327108
  7.2 3.7 copy-start.3
  7.2 67.7 %copy-start.5 = (bf16[1,2,32,384]{3,2,1,0:T(8,128)(2,1)S(1)}, bf16[1,2,32,384]{3,2,1,0:T(8,128)(2,1)}, u32[]{:S(2)}) copy-start(bf16[1,2,32,384]{3,2,1,0:T(8,128)(2,1)} %param.12) | copy-start | bytes 147460
  7.2 20.2 %copy-start.11 = (f32[1,192]{1,0:T(1,128)S(1)}, f32[1,192]{1,0:T(1,128)}, u32[]{:S(2)}) copy-start(f32[1,192]{1,0:T(1,128)} %param.14) | copy-start | bytes 2308
  7.2 125.9 %all-gather.3.cloned.1.call-start = ((), (), s32[]{:S(2)}) async-start(), calls=%async_computation.5 | async-start | bytes 10027008 | tf_op jit(solution)/shard_map/all_gather | solution.py:135
  77.2 4.9 %copy-start.12 = (f32[128]{0:T(128)S(1)}, f32[128]{0:T(128)}, u32[]{:S(2)}) copy-start(f32[128]{0:T(128)} %param.18) | copy-start | bytes 1540
  77.2 5.6 %copy-start.13 = (f32[128]{0:T(128)S(1)}, f32[128]{0:T(128)}, u32[]{:S(2)}) copy-start(f32[128]{0:T(128)} %param.19) | copy-start | bytes 1540
  77.3 6.4 %copy-start.7 = (bf16[768,192]{0,1:T(8,128)(2,1)S(1)}, bf16[768,192]{0,1:T(8,128)(2,1)}, u32[]{:S(2)}) copy-start(bf16[768,192]{0,1:T(8,128)(2,1)} %param.21) | copy-start | bytes 884740
  77.3 6.4 %copy-start.10 = (bf16[256,192]{0,1:T(8,128)(2,1)S(1)}, bf16[256,192]{0,1:T(8,128)(2,1)}, u32[]{:S(2)}) copy-start(bf16[256,192]{0,1:T(8,128)(2,1)} %param.20) | copy-start | bytes 294916
  77.3 55.9 %all-to-all-start = ((bf16[8,576,384]{2,1,0:T(8,128)(2,1)}), bf16[8,576,384]{2,1,0:T(8,128)(2,1)}, u32[]{:S(2)}, u32[]{:S(2)}) async-start(bf16[8,576,384]{2,1,0:T(8,128)(2,1)} %broadcast_in_dim.23), calls=%async_computation | async-start | bytes 7077888 | tf_op jit(solution)/shard_map/all_to_all | solution.py:143
  81.9 233.7 %all-gather.5.cloned.1.call-start = ((), (), s32[]{:S(2)}) async-start(), calls=%async_computation.6 | async-start | bytes 6684672 | tf_op jit(solution)/shard_map/all_gather | solution.py:213
  148.7 1.8 copy-start.9
  148.7 2.2 copy-start.8
  149.7 1.5 copy-start.6
  156.3 16.3 %copy-start.14 = (s32[2]{0:T(128)S(1)}, s32[2]{0:T(128)}, u32[]{:S(2)}) copy-start(s32[2]{0:T(128)} %param.22) | copy-start | bytes 28
  156.3 120.9 %all-to-all-start.1 = ((bf16[16,648,128]{2,1,0:T(8,128)(2,1)}), bf16[16,648,128]{2,1,0:T(8,128)(2,1)S(1)}, u32[]{:S(2)}, u32[]{:S(2)}) async-start(bf16[16,648,128]{2,1,0:T(8,128)(2,1)} %pad_maximum_fusion), calls=%async_computation.1 | async-start | bytes 5308416 | tf_op jit(solution)/shard_map/all_to_all | solution.py:184
  172.3 199.1 %reduce-scatter.4.cloned.1.call-start = ((), (), s32[]{:S(2)}) async-start(), calls=%async_computation.7 | async-start | bytes 4423680
  280.8 7.1 %copy-start.2 = (f32[1152,4608]{1,0:T(8,128)}, f32[1152,4608]{1,0:T(8,128)S(1)}, u32[]{:S(2)}) copy-start(f32[1152,4608]{1,0:T(8,128)S(1)} %get-tuple-element.33) | copy-start | bytes 63700996
  287.9 27.7 %copy-start.4 = (bf16[576,768]{1,0:T(8,128)(2,1)S(1)}, bf16[576,768]{1,0:T(8,128)(2,1)}, u32[]{:S(2)}) copy-start(bf16[576,768]{1,0:T(8,128)(2,1)} %get-tuple-element.15) | copy-start | bytes 2654212
  372.8 11.3 %copy-start.1 = (bf16[192,3,384]{2,0,1:T(8,128)(2,1)S(1)}, bf16[192,3,384]{2,0,1:T(8,128)(2,1)}, u32[]{:S(2)}) copy-start(bf16[192,3,384]{2,0,1:T(8,128)(2,1)} %param.15) | copy-start | bytes 1327108
  373.7 9.3 %all-to-all-start.3 = ((bf16[2,1,256,384]{3,2,1,0:T(8,128)(2,1)}), bf16[2,1,256,384]{3,2,1,0:T(8,128)(2,1)S(1)}, u32[]{:S(2)}, u32[]{:S(2)}) async-start(bf16[2,1,256,384]{3,2,1,0:T(8,128)(2,1)} %slice_bitcast_fusion.2), calls=%async_computation.3 | async-start | bytes 786432 | tf_op jit(solution)/shard_map/all_to_all | solution.py:227
Sparse Core Ops, SparseCore 0:
  10.4 122.6 all-gather.2
  136.1 147.8 all-gather.4
  329.9 41.4 reduce-scatter.3

commit v4 on v3

--- a/solution.py
+++ b/solution.py
@@ -119,7 +119,9 @@
     mod_terms = jnp.dot(
         cond_vec, mod_weight.reshape(dim_seq, 3 * dim_local), preferred_element_type=jnp.float32
     )
-    modulation = lax.psum(mod_terms.reshape(3, dim_local), "seq")
+    seq_count = lax.psum(1, "seq")
+    mod_spread = jnp.broadcast_to(mod_terms.reshape(1, 3, dim_local), (seq_count, 3, dim_local))
+    modulation = jnp.sum(lax.all_to_all(mod_spread, "seq", 0, 0, tiled=True), axis=0)
     local_rows = jnp.concatenate([text_tokens[0], image_tokens], axis=1)
     hidden = local_rows.astype(jnp.float32)
     totals, squares = lax.psum(
@@ -132,23 +134,26 @@
     ).astype(jnp.bfloat16)
     width_rows = qkv_weight.shape[0]
     qkv_cols = 3 * heads_local * HD
-    in_weight = lax.all_gather(
-        jnp.concatenate([qkv_weight.reshape(width_rows, qkv_cols), up_weight], axis=1),
-        "seq",
-        axis=0,
-        tiled=True,
+    qkv_full = lax.all_gather(
+        qkv_weight.reshape(width_rows, qkv_cols), "seq", axis=0, tiled=True
     )
     wblk_count = lax.psum(1, "wblk")
     spread = jnp.broadcast_to(normed.reshape(1, row_count, dim_local), (wblk_count, row_count, dim_local))
     gathered = lax.all_to_all(spread, "wblk", 0, 0, tiled=True)
-    both = jnp.einsum(
+    up_source, gathered = lax.optimization_barrier((up_weight, gathered))
+    up_full = lax.all_gather(up_source, "seq", axis=0, tiled=True)
+    projected = jnp.einsum(
         "wrf,wfn->rn",
         gathered,
-        in_weight.reshape(wblk_count, dim_local, -1),
+        qkv_full.reshape(wblk_count, dim_local, -1),
         preferred_element_type=jnp.float32,
     )
-    projected = both[:, :qkv_cols]
-    mlp_units = both[:, qkv_cols:]
+    mlp_units = jnp.einsum(
+        "wrf,wfn->rn",
+        gathered,
+        up_full.reshape(wblk_count, dim_local, -1),
+        preferred_element_type=jnp.float32,
+    )
     projected = projected.reshape(prompts, local_len, 3, heads_local, HD)
     image_index = seq_pos * image_rows + jnp.arange(image_rows, dtype=jnp.int32)
     height_pos = jnp.concatenate(
@@ -162,7 +167,6 @@
     key_rows = rotate(head_norm(projected[:, :, 1], key_gain), angles).astype(jnp.bfloat16)
     values = projected[:, :, 2].astype(jnp.bfloat16)
     scale_factor = HD ** (-0.5)
-    seq_count = lax.psum(1, "seq")
     pair_count = prompts * heads_local
     subs = seq_count // pair_count
     sub_rows = local_len // subs
@@ -181,6 +185,9 @@
         ],
         axis=1,
     )
+    out_source, send = lax.optimization_barrier(
+        (jnp.concatenate([attn_weight, down_weight], axis=0), send)
+    )
     received = lax.all_to_all(send, "seq", 0, 0, tiled=True)
     key_piece = received[:, :local_len].reshape(seq_count * local_len, HD)
     value_piece = received[:, local_len : 2 * local_len].reshape(seq_count * local_len, HD)
@@ -207,9 +214,6 @@
     attended = returned.reshape(prompts, heads_local, local_len, HD)
     attended = attended.transpose(0, 2, 1, 3).reshape(row_count, heads_local * HD)
     activated = jax.nn.gelu(mlp_units, approximate=True).astype(jnp.bfloat16)
-    out_source, in_weight = lax.optimization_barrier(
-        (jnp.concatenate([attn_weight, down_weight], axis=0), in_weight)
-    )
     out_weight = lax.all_gather(out_source, "seq", axis=1, tiled=True)
     terms_by_feature = lax.dot_general(
         out_weight,

time: 391 us -> 397 us (1.015)
  blocking collectives: 79.4 us -> 60.9 us
  waiting for transfers between devices: 198 us -> 209 us
  starting transfers between devices: 24.4 us -> 34.4 us
  matrix products: 31.2 us -> 36.1 us
    all_gather x1, waiting for transfers between devices: 0.02 us -> 57.2 us  [shards(): out_weight = lax.all_gather(out_source, 'seq', axis=1, tiled=True)]
    psum x1 -> x0, blocking collectives: 47.1 us -> none  [shards(): modulation = lax.psum(mod_terms.reshape(3, dim_local), 'seq')]
    all_gather x1 -> x2, waiting for transfers between devices: 47.5 us -> 3.27 us  [the longest x1 3.25 us: shards(): lax.all_gather(qkv_weight.reshape(width_rows, qkv_cols), 'seq', axis=0, t...]
    all_to_all x1, blocking collectives: 17.2 us -> 46 us  [shards(): gathered = lax.all_to_all(spread, 'wblk', 0, 0, tiled=True)]
    all_to_all x1 -> x2, starting transfers between devices: 4.62 us -> 19.7 us  [the longest x1 11.5 us: shards(): lax.all_to_all(mod_spread, 'seq', 0, 0, tiled=True)]
    all_to_all x1, waiting for transfers between devices: 103 us -> 89.2 us  [shards(): received = lax.all_to_all(send, 'seq', 0, 0, tiled=True)]
    all_to_all x1 -> x2, waiting for transfers between devices: 0.01 us -> 8.87 us  [the longest x1 8.86 us: shards(): returned = lax.all_to_all(mixed, 'seq', 0, 0, tiled=True)]
    reshape x1 -> x2, local copies, waits for them, and re-layouts: 2.11 us -> 7.32 us  [the longest x1 7.09 us: shards(): qkv_full.reshape(wblk_count, dim_local, -1)]
  transfers between devices with their start and end apart: 6 -> 8, of which waited for: 4 -> 6; matrix products, arithmetic and copies ran while one was open for 13% -> 14% of each run, Pallas kernels for 0% -> 0%
where the time goes in v4:
time: 397 us; the launch traced here: 396 us
  waiting for transfers between devices  209 us (53%)
  blocking collectives  60.9 us (15%)
  matrix products  36.1 us (9%)
  starting transfers between devices  34.4 us (9%)
  local copies, waits for them, and re-layouts  25.5 us (6%)
  other arithmetic  15.7 us (4%)
  between operations  14.9 us (4%)
    all_to_all x1, waiting for transfers between devices, shards(): received = lax.all_to_all(send, 'seq', 0, 0, tiled=True)  89.2 us
    all_gather x1, waiting for transfers between devices, shards(): out_weight = lax.all_gather(out_source, 'seq', axis=1, tiled=True)  57.2 us
    all_to_all x1, blocking collectives, shards(): gathered = lax.all_to_all(spread, 'wblk', 0, 0, tiled=True)  46 us
    unnamed x5, waiting for transfers between devices  45.3 us
    psum x1, blocking collectives, shards(): lax.psum((jnp.sum(hidden, axis=-1), jnp.sum(hidden * hidden, axis=-1)), '...  14.8 us
    all_to_all x1, starting transfers between devices, shards(): lax.all_to_all(mod_spread, 'seq', 0, 0, tiled=True)  11.5 us
    all_to_all x1, starting transfers between devices, shards(): received = lax.all_to_all(send, 'seq', 0, 0, tiled=True)  10.9 us
    dot_general x1, matrix products, shards(): jnp.dot(weights.astype(jnp.bfloat16), value_piece, preferred_element_type...  10.8 us
  transfers between devices with their start and end apart: 8, of which 6 were waited for; matrix products, arithmetic and copies ran while one was open for 14% of the time, Pallas kernels for 0%

profile of v4, /device:TPU:2, one launch (start us, length us, event | category | flops | bytes accessed | tf_op | source)
XLA Modules:
  0.0 396.5 jit_solution(9299779750826395407)
XLA Ops:
  7.2 1.9 reshape.346
  9.8 0.1 fusion.54
  9.9 0.8 fusion.62
  10.7 0.2 fusion.36
  10.9 0.7 broadcast_in_dim.24
  11.5 11.5 %all-to-all-start = ((f32[16,3,384]{2,1,0:T(4,128)}), f32[16,3,384]{2,1,0:T(4,128)S(1)}, u32[]{:S(2)}, u32[]{:S(2)}) async-start(f32[16,3,384]{2,1,0:T(4,128)} %broadcast_in_dim.24), calls=%async_computation | async-start | bytes 196608 | tf_op jit(solution)/shard_map/all_to_all | solution.py:124
  23.0 1.3 convert_reduce_fusion
  24.4 14.8 %all-reduce.2 = (f32[2,288]{1,0:T(2,128)S(1)}, f32[2,288]{1,0:T(2,128)S(1)}) all-reduce(f32[2,288]{1,0:T(2,128)S(1)} %get-tuple-element.14, f32[2,288]{1,0:T(2,128)S(1)} %get-tuple-element.13), channel_id=1, replica_groups=mesh['cfg'=2,'seq'=16,'wblk'=8] {'wblk'}, use_global_device_ids=true, to_apply=%region_4.5 | all-reduce | flops 1152 | bytes 9216 | tf_op jit(solution)/shard_map/psum | solution.py:127
  39.2 0.1 mul.307
  39.3 0.1 sub.82
  39.4 1.3 fusion.35
  40.7 0.3 broadcast_in_dim.25
  41.0 46.0 %all_to_all.29 = bf16[8,576,384]{2,1,0:T(8,128)(2,1)} all-to-all(bf16[8,576,384]{2,1,0:T(8,128)(2,1)S(1)} %broadcast_in_dim.25), channel_id=1, replica_groups=mesh['cfg'=2,'seq'=16,'wblk'=8] {'wblk'}, dimensions={0} | all-to-all | bytes 7077888 | tf_op jit(solution)/shard_map/all_to_all | solution.py:142
  87.1 0.0 all-gather.6.cloned.1.call-start
  87.2 0.1 mul.334
  87.3 0.1 mul.315
  87.5 0.1 concatenate.35
  87.6 0.1 concatenate.36
  87.7 0.8 pad_maximum_fusion.2
  88.5 0.1 broadcast_multiply_fusion.1
  88.5 0.4 fusion.43
  88.9 3.3 all-gather.4.cloned.1.call-done
  92.2 7.1 %copy.67 = bf16[8,384,768]{1,0,2:T(8,128)(2,1)} copy(bf16[8,384,768]{2,1,0:T(8,128)(2,1)} %bitcast.115) | data formatting | bytes 9437184 | tf_op jit(solution)/shard_map/reshape | solution.py:148
  99.3 6.9 %fusion.24 = f32[2,288,3,2,128]{4,1,3,2,0:T(8,128)S(1)} fusion(bf16[3,2,128,384,8]{3,4,2,1,0:T(8,128)(2,1)} %bitcast.116, bf16[2,288,384,8,1,1]{2,1,0,3,5,4:T(8,128)(2,1)} %bitcast.119), kind=kOutput, calls=%fused_computation.24 | convolution fusion | flops 2717908992 | bytes 10027008 | tf_op jit(solution)/shard_map/wrf,wfn->rn/dot_general | solution.py:145
  106.2 0.5 multiply_reduce_fusion.2
  106.7 0.5 copy.58
  107.2 0.5 copy.56
  107.8 0.4 multiply_multiply_fusion.1
  108.2 0.4 multiply_multiply_fusion.2
  108.5 0.8 subtract_convert_fusion.1
  109.3 0.6 pad_maximum_fusion.3
  109.9 0.5 copy.57
  110.4 0.6 pad_maximum_fusion.4
  111.0 0.5 copy.59
  111.5 0.2 broadcast_in_dim.28
  111.6 0.2 broadcast_in_dim.34
  111.8 1.7 pad_maximum_fusion
  113.5 10.9 %all-to-all-start.2 = ((bf16[16,648,128]{2,1,0:T(8,128)(2,1)}), bf16[16,648,128]{2,1,0:T(8,128)(2,1)S(1)}, u32[]{:S(2)}, u32[]{:S(2)}) async-start(bf16[16,648,128]{2,1,0:T(8,128)(2,1)} %pad_maximum_fusion), calls=%async_computation.2 | async-start | bytes 5308416 | tf_op jit(solution)/shard_map/all_to_all | solution.py:191
  124.4 0.6 dynamic_slice.10
  125.0 0.7 fusion.53
  125.7 89.2 %all-to-all-done.2 = bf16[16,648,128]{2,1,0:T(8,128)(2,1)S(1)} async-done(((bf16[16,648,128]{2,1,0:T(8,128)(2,1)}), bf16[16,648,128]{2,1,0:T(8,128)(2,1)S(1)}, u32[]{:S(2)}, u32[]{:S(2)}) %all-to-all-start.2) | async-done | bytes 2654240 | tf_op jit(solution)/shard_map/all_to_all | solution.py:191
  215.0 0.2 fusion.65
  215.1 3.5 fusion.66
  218.6 4.2 %fusion.1 = f32[1152]{0:T(1024)S(1)} fusion(f32[1152,4608]{1,0:T(8,128)S(1)} %get-tuple-element.39, f32[1152]{0:T(1024)S(1)} %get-tuple-element.38), kind=kLoop, calls=%fused_computation.3 | loop fusion | flops 10615680 | bytes 21242880 | tf_op jit(solution)/shard_map/reduce_sum | solution.py:208
  222.9 2.8 copy-done.2
  225.7 10.8 %fusion.13 = bf16[1152,128]{1,0:T(8,128)(2,1)} fusion(bf16[4608,128]{1,0:T(8,128)(2,1)S(1)} %bitcast.113, f32[1152,4608]{1,0:T(8,128)} %copy-done.2, f32[1152]{0:T(1024)S(1)} %get-tuple-element.38, f32[1152]{0:T(1024)S(1)} %fusion.1), kind=kOutput, calls=%fused_computation.15 | convolution fusion | flops 1369866240 | bytes 22717440 | tf_op jit(solution)/shard_map/dot_general | solution.py:209
  236.5 8.2 %all-to-all-start.3 = ((bf16[16,72,128]{2,1,0:T(8,128)(2,1)}), bf16[16,72,128]{2,1,0:T(8,128)(2,1)S(1)}, u32[]{:S(2)}, u32[]{:S(2)}) async-start(bf16[16,72,128]{2,1,0:T(8,128)(2,1)} %bitcast.32), calls=%async_computation.3 | async-start | bytes 589824 | tf_op jit(solution)/shard_map/all_to_all | solution.py:213
  244.7 0.3 reduce-scatter.4.cloned.1.call-start
  245.0 6.6 %fusion.23 = bf16[576,768]{1,0:T(8,128)(2,1)S(1)} fusion(bf16[8,576,384]{2,1,0:T(8,128)(2,1)} %all_to_all.29, bf16[8,384,768]{2,1,0:T(8,128)(2,1)} %bitcast.137), kind=kOutput, calls=%fused_computation.23 | convolution fusion | flops 2721890304 | bytes 9142272 | tf_op jit(solution)/shard_map/wrf,wfn->rn/dot_general | solution.py:151
  251.6 8.9 %all-to-all-done.3 = bf16[16,72,128]{2,1,0:T(8,128)(2,1)S(1)} async-done(((bf16[16,72,128]{2,1,0:T(8,128)(2,1)}), bf16[16,72,128]{2,1,0:T(8,128)(2,1)S(1)}, u32[]{:S(2)}, u32[]{:S(2)}) %all-to-all-start.3) | async-done | bytes 294944 | tf_op jit(solution)/shard_map/all_to_all | solution.py:213
  260.5 0.2 copy.60
  260.8 57.2 %all-gather.6.cloned.1.call-done = bf16[1024,3072]{0,1:T(8,128)(2,1)} async-done(((bf16[1024,192]{0,1:T(8,128)(2,1)}), bf16[1024,3072]{0,1:T(8,128)(2,1)}) %all-gather.6.cloned.1.call-update) | async-done | bytes 6291472 | tf_op jit(solution)/shard_map/all_gather | solution.py:217
  317.9 8.1 %convolution_convert_fusion = bf16[3072,576]{0,1:T(8,128)(2,1)} fusion(bf16[1024,3072]{0,1:T(8,128)(2,1)} %all-gather.6.cloned.1.call-done, bf16[576,768]{1,0:T(8,128)(2,1)S(1)} %fusion.23, bf16[576,256]{1,0:T(8,128)(2,1)S(1)} %bitcast.134), kind=kOutput, calls=%fused_computation.10 | convolution fusion | flops 3628007424 | bytes 11010048 | tf_op jit(solution)/shard_map/dot_general | solution.py:218
  326.0 6.1 %copy.68 = bf16[3072,576]{1,0:T(8,128)(2,1)} copy(bf16[3072,576]{0,1:T(8,128)(2,1)} %convolution_convert_fusion) | data formatting | bytes 7077888
  332.1 45.2 %reduce-scatter.4.cloned.1.call-done = bf16[384,576]{1,0:T(8,128)(2,1)} async-done(((bf16[3072,576]{1,0:T(8,128)(2,1)}), bf16[384,576]{1,0:T(8,128)(2,1)}) %reduce-scatter.4.cloned.1.call-update) | async-done | bytes 442384
  377.3 1.3 copy.69
  378.6 0.1 convert_element_type.112
  378.7 0.1 add_convert_fusion
  378.8 0.8 slice_bitcast_fusion.2
  379.6 3.5 all-to-all-start.4
  383.1 0.6 slice_bitcast_fusion.3
  383.8 5.2 %all-to-all-done.4 = bf16[2,1,256,384]{3,2,1,0:T(8,128)(2,1)S(1)} async-done(((bf16[2,1,256,384]{3,2,1,0:T(8,128)(2,1)}), bf16[2,1,256,384]{3,2,1,0:T(8,128)(2,1)S(1)}, u32[]{:S(2)}, u32[]{:S(2)}) %all-to-all-start.4) | async-done | bytes 393248 | tf_op jit(solution)/shard_map/all_to_all | solution.py:231
  388.9 0.1 bitcast_convert_fusion
  389.0 1.0 multiply_add_fusion
  (41 shorter events, 0.5 us)
Async XLA Ops:
  7.2 3.5 copy-start
  7.2 85.0 %all-gather.4.cloned.1.call-start = ((), (), s32[]{:S(2)}) async-start(), calls=%async_computation.6 | async-start | bytes 5013504 | tf_op jit(solution)/shard_map/all_gather | solution.py:137
  11.5 27.8 %all-to-all-start = ((f32[16,3,384]{2,1,0:T(4,128)}), f32[16,3,384]{2,1,0:T(4,128)S(1)}, u32[]{:S(2)}, u32[]{:S(2)}) async-start(f32[16,3,384]{2,1,0:T(4,128)} %broadcast_in_dim.24), calls=%async_computation | async-start | bytes 196608 | tf_op jit(solution)/shard_map/all_to_all | solution.py:124
  23.0 222.0 %all-gather.8.cloned.1.call-start = ((), (), s32[]{:S(2)}) async-start(), calls=%async_computation.8 | async-start | bytes 5013504 | tf_op jit(solution)/shard_map/all_gather | solution.py:144
  41.0 46.2 %copy-start.7 = (f32[128]{0:T(128)S(1)}, f32[128]{0:T(128)}, u32[]{:S(2)}) copy-start(f32[128]{0:T(128)} %param.18) | copy-start | bytes 1540
  41.0 46.3 %copy-start.8 = (f32[128]{0:T(128)S(1)}, f32[128]{0:T(128)}, u32[]{:S(2)}) copy-start(f32[128]{0:T(128)} %param.19) | copy-start | bytes 1540
  41.0 46.6 %copy-start.5 = (bf16[768,192]{0,1:T(8,128)(2,1)S(1)}, bf16[768,192]{0,1:T(8,128)(2,1)}, u32[]{:S(2)}) copy-start(bf16[768,192]{0,1:T(8,128)(2,1)} %param.21) | copy-start | bytes 884740
  41.0 46.6 %copy-start.6 = (bf16[256,192]{0,1:T(8,128)(2,1)S(1)}, bf16[256,192]{0,1:T(8,128)(2,1)}, u32[]{:S(2)}) copy-start(bf16[256,192]{0,1:T(8,128)(2,1)} %param.20) | copy-start | bytes 294916
  87.1 230.8 %all-gather.6.cloned.1.call-start = ((), (), s32[]{:S(2)}) async-start(), calls=%async_computation.7 | async-start | bytes 6684672 | tf_op jit(solution)/shard_map/all_gather | solution.py:217
  113.5 10.9 %copy-start.9 = (s32[2]{0:T(128)S(1)}, s32[2]{0:T(128)}, u32[]{:S(2)}) copy-start(s32[2]{0:T(128)} %param.22) | copy-start | bytes 28
  113.5 101.4 %all-to-all-start.2 = ((bf16[16,648,128]{2,1,0:T(8,128)(2,1)}), bf16[16,648,128]{2,1,0:T(8,128)(2,1)S(1)}, u32[]{:S(2)}, u32[]{:S(2)}) async-start(bf16[16,648,128]{2,1,0:T(8,128)(2,1)} %pad_maximum_fusion), calls=%async_computation.2 | async-start | bytes 5308416 | tf_op jit(solution)/shard_map/all_to_all | solution.py:191
  218.6 7.1 %copy-start.2 = (f32[1152,4608]{1,0:T(8,128)}, f32[1152,4608]{1,0:T(8,128)S(1)}, u32[]{:S(2)}) copy-start(f32[1152,4608]{1,0:T(8,128)S(1)} %get-tuple-element.39) | copy-start | bytes 63700996
  236.5 24.0 %all-to-all-start.3 = ((bf16[16,72,128]{2,1,0:T(8,128)(2,1)}), bf16[16,72,128]{2,1,0:T(8,128)(2,1)S(1)}, u32[]{:S(2)}, u32[]{:S(2)}) async-start(bf16[16,72,128]{2,1,0:T(8,128)(2,1)} %bitcast.32), calls=%async_computation.3 | async-start | bytes 589824 | tf_op jit(solution)/shard_map/all_to_all | solution.py:213
  244.7 132.6 %reduce-scatter.4.cloned.1.call-start = ((), (), s32[]{:S(2)}) async-start(), calls=%async_computation.9 | async-start | bytes 4423680
  332.1 46.6 %copy-start.3 = (bf16[2,256,384]{2,1,0:T(8,128)(2,1)S(1)}, bf16[2,256,384]{2,1,0:T(8,128)(2,1)}, u32[]{:S(2)}) copy-start(bf16[2,256,384]{2,1,0:T(8,128)(2,1)} %param.13) | copy-start | bytes 1179652
  332.1 46.6 %copy-start.4 = (bf16[1,2,32,384]{3,2,1,0:T(8,128)(2,1)S(1)}, bf16[1,2,32,384]{3,2,1,0:T(8,128)(2,1)}, u32[]{:S(2)}) copy-start(bf16[1,2,32,384]{3,2,1,0:T(8,128)(2,1)} %param.12) | copy-start | bytes 147460
  378.6 11.4 %copy-start.1 = (bf16[192,3,384]{2,0,1:T(8,128)(2,1)S(1)}, bf16[192,3,384]{2,0,1:T(8,128)(2,1)}, u32[]{:S(2)}) copy-start(bf16[192,3,384]{2,0,1:T(8,128)(2,1)} %param.15) | copy-start | bytes 1327108
  379.6 9.3 %all-to-all-start.4 = ((bf16[2,1,256,384]{3,2,1,0:T(8,128)(2,1)}), bf16[2,1,256,384]{3,2,1,0:T(8,128)(2,1)S(1)}, u32[]{:S(2)}, u32[]{:S(2)}) async-start(bf16[2,1,256,384]{3,2,1,0:T(8,128)(2,1)} %slice_bitcast_fusion.2), calls=%async_computation.4 | async-start | bytes 786432 | tf_op jit(solution)/shard_map/all_to_all | solution.py:231
Sparse Core Ops, SparseCore 0:
  11.0 81.1 all-gather.3
  94.6 125.0 all-gather.7
  222.7 95.1 all-gather.5
  332.3 45.0 reduce-scatter.3

commit v5 on v4

--- a/solution.py
+++ b/solution.py
@@ -140,8 +140,13 @@
     wblk_count = lax.psum(1, "wblk")
     spread = jnp.broadcast_to(normed.reshape(1, row_count, dim_local), (wblk_count, row_count, dim_local))
     gathered = lax.all_to_all(spread, "wblk", 0, 0, tiled=True)
-    up_source, gathered = lax.optimization_barrier((up_weight, gathered))
-    up_full = lax.all_gather(up_source, "seq", axis=0, tiled=True)
+    up_cols = up_weight.shape[1]
+    tail_source = jnp.concatenate(
+        [up_weight, jnp.concatenate([attn_weight, down_weight], axis=0).T], axis=1
+    )
+    tail_source, gathered = lax.optimization_barrier((tail_source, gathered))
+    tail_full = lax.all_gather(tail_source, "seq", axis=0, tiled=True)
+    up_full = tail_full[:, :up_cols]
     projected = jnp.einsum(
         "wrf,wfn->rn",
         gathered,
@@ -185,9 +190,6 @@
         ],
         axis=1,
     )
-    out_source, send = lax.optimization_barrier(
-        (jnp.concatenate([attn_weight, down_weight], axis=0), send)
-    )
     received = lax.all_to_all(send, "seq", 0, 0, tiled=True)
     key_piece = received[:, :local_len].reshape(seq_count * local_len, HD)
     value_piece = received[:, local_len : 2 * local_len].reshape(seq_count * local_len, HD)
@@ -214,11 +216,10 @@
     attended = returned.reshape(prompts, heads_local, local_len, HD)
     attended = attended.transpose(0, 2, 1, 3).reshape(row_count, heads_local * HD)
     activated = jax.nn.gelu(mlp_units, approximate=True).astype(jnp.bfloat16)
-    out_weight = lax.all_gather(out_source, "seq", axis=1, tiled=True)
     terms_by_feature = lax.dot_general(
-        out_weight,
+        tail_full[:, up_cols:],
         jnp.concatenate([attended, activated], axis=1),
-        (((0,), (1,)), ((), ())),
+        (((1,), (1,)), ((), ())),
         preferred_element_type=jnp.float32,
     )
     branch = lax.psum_scatter(

time: 397 us -> 370 us (0.932)
  waiting for transfers between devices: 209 us -> 185 us
  local copies, waits for them, and re-layouts: 25.5 us -> 30.1 us
  matrix products: 36.1 us -> 31.8 us
    all_gather x2 -> x1, waiting for transfers between devices: 57.2 us -> 11.7 us  [shards(): tail_full = lax.all_gather(tail_source, 'seq', axis=0, tiled=True)]
    all_to_all x1, waiting for transfers between devices: 8.86 us -> 41.6 us  [shards(): gathered = lax.all_to_all(spread, 'wblk', 0, 0, tiled=True)]
    all_to_all x1, waiting for transfers between devices: 89.2 us -> 84.2 us  [shards(): received = lax.all_to_all(send, 'seq', 0, 0, tiled=True)]
    unnamed x5 -> x4, waiting for transfers between devices: 45.3 us -> 41.3 us
    unnamed x23 -> x31, local copies, waits for them, and re-layouts: 10.3 us -> 10.7 us
  transfers between devices with their start and end apart: 8 -> 7, of which waited for: 6 -> 6; matrix products, arithmetic and copies ran while one was open for 14% -> 14% of each run, Pallas kernels for 0% -> 0%
where the time goes in v5:
time: 370 us; the launch traced here: 369 us
  waiting for transfers between devices  185 us (50%)
  blocking collectives  60.7 us (16%)
  matrix products  31.8 us (9%)
  starting transfers between devices  30.9 us (8%)
  local copies, waits for them, and re-layouts  30.1 us (8%)
  other arithmetic  15.9 us (4%)
  between operations  15 us (4%)
    all_to_all x1, waiting for transfers between devices, shards(): received = lax.all_to_all(send, 'seq', 0, 0, tiled=True)  84.2 us
    all_to_all x1, blocking collectives, shards(): returned = lax.all_to_all(mixed, 'seq', 0, 0, tiled=True)  45.9 us
    all_to_all x1, waiting for transfers between devices, shards(): gathered = lax.all_to_all(spread, 'wblk', 0, 0, tiled=True)  41.6 us
    unnamed x4, waiting for transfers between devices  41.3 us
    psum x1, blocking collectives, shards(): lax.psum((jnp.sum(hidden, axis=-1), jnp.sum(hidden * hidden, axis=-1)), '...  14.8 us
    all_gather x1, waiting for transfers between devices, shards(): tail_full = lax.all_gather(tail_source, 'seq', axis=0, tiled=True)  11.7 us
    all_to_all x1, starting transfers between devices, shards(): lax.all_to_all(mod_spread, 'seq', 0, 0, tiled=True)  11.5 us
    all_to_all x1, starting transfers between devices, shards(): received = lax.all_to_all(send, 'seq', 0, 0, tiled=True)  11 us
  transfers between devices with their start and end apart: 7, of which 6 were waited for; matrix products, arithmetic and copies ran while one was open for 14% of the time, Pallas kernels for 0%

profile of v5, /device:TPU:2, one launch (start us, length us, event | category | flops | bytes accessed | tf_op | source)
XLA Modules:
  0.0 369.4 jit_solution(15512662710965867674)
XLA Ops:
  7.2 1.9 reshape.346
  9.8 0.1 fusion.59
  9.9 0.8 fusion.67
  10.7 0.2 fusion.41
  10.9 0.7 broadcast_in_dim.24
  11.5 11.5 %all-to-all-start = ((f32[16,3,384]{2,1,0:T(4,128)}), f32[16,3,384]{2,1,0:T(4,128)S(1)}, u32[]{:S(2)}, u32[]{:S(2)}) async-start(f32[16,3,384]{2,1,0:T(4,128)} %broadcast_in_dim.24), calls=%async_computation | async-start | bytes 196608 | tf_op jit(solution)/shard_map/all_to_all | solution.py:124
  23.0 1.3 convert_reduce_fusion
  24.3 14.8 %all-reduce.2 = (f32[2,288]{1,0:T(2,128)S(1)}, f32[2,288]{1,0:T(2,128)S(1)}) all-reduce(f32[2,288]{1,0:T(2,128)S(1)} %get-tuple-element.10, f32[2,288]{1,0:T(2,128)S(1)} %get-tuple-element.9), channel_id=1, replica_groups=mesh['cfg'=2,'seq'=16,'wblk'=8] {'wblk'}, use_global_device_ids=true, to_apply=%region_4.5 | all-reduce | flops 1152 | bytes 9216 | tf_op jit(solution)/shard_map/psum | solution.py:127
  39.2 0.1 mul.307
  39.2 0.1 sub.82
  39.4 1.2 fusion.40
  40.6 2.1 broadcast_in_dim.25
  42.7 4.7 %all-to-all-start.1 = ((bf16[8,576,384]{2,1,0:T(8,128)(2,1)}), bf16[8,576,384]{2,1,0:T(8,128)(2,1)}, u32[]{:S(2)}, u32[]{:S(2)}) async-start(bf16[8,576,384]{2,1,0:T(8,128)(2,1)} %broadcast_in_dim.25), calls=%async_computation.1 | async-start | bytes 7077888 | tf_op jit(solution)/shard_map/all_to_all | solution.py:142
  47.5 0.9 pad_maximum_fusion.1
  48.4 41.6 %all-to-all-done.1 = bf16[8,576,384]{2,1,0:T(8,128)(2,1)} async-done(((bf16[8,576,384]{2,1,0:T(8,128)(2,1)}), bf16[8,576,384]{2,1,0:T(8,128)(2,1)}, u32[]{:S(2)}, u32[]{:S(2)}) %all-to-all-start.1) | async-done | bytes 3538976 | tf_op jit(solution)/shard_map/all_to_all | solution.py:142
  90.1 0.1 mul.335
  90.2 0.1 mul.316
  90.4 0.1 concatenate.39
  90.4 0.1 concatenate.40
  90.5 0.1 broadcast_multiply_fusion.1
  90.6 0.4 fusion.48
  91.0 1.2 all-gather.5.cloned.1.call-done
  92.2 7.1 %copy.67 = bf16[8,384,768]{1,0,2:T(8,128)(2,1)} copy(bf16[8,384,768]{2,1,0:T(8,128)(2,1)} %bitcast.116) | data formatting | bytes 9437184 | tf_op jit(solution)/shard_map/reshape | solution.py:153
  99.3 6.9 %fusion.29 = f32[2,288,3,2,128]{4,1,3,2,0:T(8,128)S(1)} fusion(bf16[3,2,128,384,8]{3,4,2,1,0:T(8,128)(2,1)} %bitcast.117, bf16[2,288,384,8,1,1]{2,1,0,3,5,4:T(8,128)(2,1)} %bitcast.10), kind=kOutput, calls=%fused_computation.26 | convolution fusion | flops 2717908992 | bytes 10027008 | tf_op jit(solution)/shard_map/wrf,wfn->rn/dot_general | solution.py:150
  106.3 0.5 multiply_reduce_fusion.2
  106.8 0.5 copy.58
  107.3 0.5 copy.56
  107.8 0.4 multiply_multiply_fusion.1
  108.2 0.4 multiply_multiply_fusion.2
  108.6 0.8 subtract_convert_fusion.1
  109.4 0.6 pad_maximum_fusion.3
  110.0 0.5 copy.57
  110.4 0.6 pad_maximum_fusion.4
  111.0 0.5 copy.59
  111.5 0.2 broadcast_in_dim.29
  111.7 0.2 broadcast_in_dim.35
  111.8 1.7 pad_maximum_fusion
  113.5 11.0 %all-to-all-start.2 = ((bf16[16,648,128]{2,1,0:T(8,128)(2,1)}), bf16[16,648,128]{2,1,0:T(8,128)(2,1)S(1)}, u32[]{:S(2)}, u32[]{:S(2)}) async-start(bf16[16,648,128]{2,1,0:T(8,128)(2,1)} %pad_maximum_fusion), calls=%async_computation.2 | async-start | bytes 5308416 | tf_op jit(solution)/shard_map/all_to_all | solution.py:193
  124.5 0.2 reduce-scatter.4.cloned.1.call-start
  124.8 0.6 dynamic_slice.10
  125.4 0.7 fusion.58
  126.1 84.2 %all-to-all-done.2 = bf16[16,648,128]{2,1,0:T(8,128)(2,1)S(1)} async-done(((bf16[16,648,128]{2,1,0:T(8,128)(2,1)}), bf16[16,648,128]{2,1,0:T(8,128)(2,1)S(1)}, u32[]{:S(2)}, u32[]{:S(2)}) %all-to-all-start.2) | async-done | bytes 2654240 | tf_op jit(solution)/shard_map/all_to_all | solution.py:193
  210.3 0.2 fusion.70
  210.5 3.5 fusion.71
  214.0 4.2 %fusion.1 = f32[1152]{0:T(1024)S(1)} fusion(f32[1152,4608]{1,0:T(8,128)S(1)} %get-tuple-element.35, f32[1152]{0:T(1024)S(1)} %get-tuple-element.34), kind=kLoop, calls=%fused_computation.3 | loop fusion | flops 10615680 | bytes 21242880 | tf_op jit(solution)/shard_map/reduce_sum | solution.py:210
  218.2 3.2 copy-done.2
  221.4 10.5 %fusion.18 = bf16[1152,128]{1,0:T(8,128)(2,1)S(1)} fusion(bf16[4608,128]{1,0:T(8,128)(2,1)S(1)} %bitcast.114, f32[1152,4608]{1,0:T(8,128)} %copy-done.2, f32[1152]{0:T(1024)S(1)} %get-tuple-element.34, f32[1152]{0:T(1024)S(1)} %fusion.1), kind=kOutput, calls=%fused_computation.17 | convolution fusion | flops 1369866240 | bytes 22717440 | tf_op jit(solution)/shard_map/dot_general | solution.py:211
  231.9 45.9 %all_to_all.29 = bf16[16,72,128]{2,1,0:T(8,128)(2,1)S(1)} all-to-all(bf16[16,72,128]{2,1,0:T(8,128)(2,1)S(1)} %bitcast.127), channel_id=1, replica_groups=mesh['cfg'=2,'seq'=16,'wblk'=8] {'seq'}, dimensions={0} | all-to-all | bytes 589824 | tf_op jit(solution)/shard_map/all_to_all | solution.py:215
  277.8 0.2 copy.60
  278.1 11.7 %all-gather.3.cloned.1.call-done = bf16[3072,1792]{1,0:T(8,128)(2,1)} async-done(((bf16[192,1792]{1,0:T(8,128)(2,1)}), bf16[3072,1792]{1,0:T(8,128)(2,1)}) %all-gather.3.cloned.1.call-update) | async-done | bytes 11010064 | tf_op jit(solution)/shard_map/all_gather | solution.py:148
  289.8 2.3 slice-done.3
  292.1 5.4 %fusion.28 = bf16[576,768]{1,0:T(8,128)(2,1)S(1)} fusion(bf16[8,576,384]{2,1,0:T(8,128)(2,1)} %all-to-all-done.1, bf16[8,384,768]{2,1,0:T(8,128)(2,1)S(1)} %bitcast.120), kind=kOutput, calls=%fused_computation.25 | convolution fusion | flops 2721890304 | bytes 9142272 | tf_op jit(solution)/shard_map/wrf,wfn->rn/dot_general | solution.py:156
  297.6 5.4 %fusion.11 = bf16[3072,576]{0,1:T(8,128)(2,1)} fusion(bf16[3072,1792]{1,0:T(8,128)(2,1)S(1)} %bitcast.119, bf16[576,768]{1,0:T(8,128)(2,1)S(1)} %fusion.28, bf16[576,256]{1,0:T(8,128)(2,1)S(1)} %bitcast.138), kind=kOutput, calls=%fused_computation.12 | convolution fusion | flops 3628007424 | bytes 11010048 | tf_op jit(solution)/shard_map/dot_general | solution.py:219
  303.0 6.1 %copy.68 = bf16[3072,576]{1,0:T(8,128)(2,1)} copy(bf16[3072,576]{0,1:T(8,128)(2,1)} %fusion.11) | data formatting | bytes 7077888
  309.1 41.2 %reduce-scatter.4.cloned.1.call-done = bf16[384,576]{1,0:T(8,128)(2,1)} async-done(((bf16[3072,576]{1,0:T(8,128)(2,1)}), bf16[384,576]{1,0:T(8,128)(2,1)}) %reduce-scatter.4.cloned.1.call-update) | async-done | bytes 442384
  350.3 1.3 copy.69
  351.6 0.1 convert_element_type.112
  351.7 0.1 add_convert_fusion
  351.8 0.8 slice_bitcast_fusion.2
  352.6 3.5 all-to-all-start.4
  356.1 0.6 slice_bitcast_fusion.3
  356.7 5.2 %all-to-all-done.4 = bf16[2,1,256,384]{3,2,1,0:T(8,128)(2,1)S(1)} async-done(((bf16[2,1,256,384]{3,2,1,0:T(8,128)(2,1)}), bf16[2,1,256,384]{3,2,1,0:T(8,128)(2,1)S(1)}, u32[]{:S(2)}, u32[]{:S(2)}) %all-to-all-start.4) | async-done | bytes 393248 | tf_op jit(solution)/shard_map/all_to_all | solution.py:232
  361.9 0.1 bitcast_convert_fusion
  362.0 1.0 multiply_add_fusion
  (50 shorter events, 0.5 us)
Async XLA Ops:
  7.2 3.5 copy-start
  7.2 85.0 %all-gather.5.cloned.1.call-start = ((), (), s32[]{:S(2)}) async-start(), calls=%async_computation.7 | async-start | bytes 5013504 | tf_op jit(solution)/shard_map/all_gather | solution.py:137
  11.5 27.8 %all-to-all-start = ((f32[16,3,384]{2,1,0:T(4,128)}), f32[16,3,384]{2,1,0:T(4,128)S(1)}, u32[]{:S(2)}, u32[]{:S(2)}) async-start(f32[16,3,384]{2,1,0:T(4,128)} %broadcast_in_dim.24), calls=%async_computation | async-start | bytes 196608 | tf_op jit(solution)/shard_map/all_to_all | solution.py:124
  42.7 4.7 %copy-start.5 = (bf16[768,192]{0,1:T(8,128)(2,1)S(1)}, bf16[768,192]{0,1:T(8,128)(2,1)}, u32[]{:S(2)}) copy-start(bf16[768,192]{0,1:T(8,128)(2,1)} %param.21) | copy-start | bytes 884740
  42.7 4.7 %copy-start.7 = (bf16[256,192]{0,1:T(8,128)(2,1)S(1)}, bf16[256,192]{0,1:T(8,128)(2,1)}, u32[]{:S(2)}) copy-start(bf16[256,192]{0,1:T(8,128)(2,1)} %param.20) | copy-start | bytes 294916
  42.7 4.8 %copy-start.6 = (bf16[192,768]{1,0:T(8,128)(2,1)S(1)}, bf16[192,768]{1,0:T(8,128)(2,1)}, u32[]{:S(2)}) copy-start(bf16[192,768]{1,0:T(8,128)(2,1)} %param.17) | copy-start | bytes 884740
  42.7 47.3 %copy-start.8 = (f32[128]{0:T(128)S(1)}, f32[128]{0:T(128)}, u32[]{:S(2)}) copy-start(f32[128]{0:T(128)} %param.18) | copy-start | bytes 1540
  42.7 47.5 %copy-start.9 = (f32[128]{0:T(128)S(1)}, f32[128]{0:T(128)}, u32[]{:S(2)}) copy-start(f32[128]{0:T(128)} %param.19) | copy-start | bytes 1540
  42.7 47.3 %all-to-all-start.1 = ((bf16[8,576,384]{2,1,0:T(8,128)(2,1)}), bf16[8,576,384]{2,1,0:T(8,128)(2,1)}, u32[]{:S(2)}, u32[]{:S(2)}) async-start(bf16[8,576,384]{2,1,0:T(8,128)(2,1)} %broadcast_in_dim.25), calls=%async_computation.1 | async-start | bytes 7077888 | tf_op jit(solution)/shard_map/all_to_all | solution.py:142
  47.4 242.4 %all-gather.3.cloned.1.call-start = ((), (), s32[]{:S(2)}) async-start(), calls=%async_computation.6 | async-start | bytes 11698176 | tf_op jit(solution)/shard_map/all_gather | solution.py:148
  113.5 11.3 %copy-start.10 = (s32[2]{0:T(128)S(1)}, s32[2]{0:T(128)}, u32[]{:S(2)}) copy-start(s32[2]{0:T(128)} %param.22) | copy-start | bytes 28
  113.5 96.7 %all-to-all-start.2 = ((bf16[16,648,128]{2,1,0:T(8,128)(2,1)}), bf16[16,648,128]{2,1,0:T(8,128)(2,1)S(1)}, u32[]{:S(2)}, u32[]{:S(2)}) async-start(bf16[16,648,128]{2,1,0:T(8,128)(2,1)} %pad_maximum_fusion), calls=%async_computation.2 | async-start | bytes 5308416 | tf_op jit(solution)/shard_map/all_to_all | solution.py:193
  124.5 225.7 %reduce-scatter.4.cloned.1.call-start = ((), (), s32[]{:S(2)}) async-start(), calls=%async_computation.8 | async-start | bytes 4423680
  213.9 7.5 %copy-start.2 = (f32[1152,4608]{1,0:T(8,128)}, f32[1152,4608]{1,0:T(8,128)S(1)}, u32[]{:S(2)}) copy-start(f32[1152,4608]{1,0:T(8,128)S(1)} %get-tuple-element.35) | copy-start | bytes 63700996
  289.8 2.3 slice-start.3
  289.8 7.8 %slice-start = ((s8[11010048]{0:T(1024)(128)(4,1)}), s8[4194304]{0:T(1024)(128)(4,1)S(1)}, s32[]{:S(2)}) async-start(s8[11010048]{0:T(1024)(128)(4,1)} %bitcast.118), calls=%async_computation.9 | async-start | bytes 8388608
  292.1 5.5 %slice-start.1 = ((s8[11010048]{0:T(1024)(128)(4,1)}), s8[4194304]{0:T(1024)(128)(4,1)S(1)}, s32[]{:S(2)}) async-start(s8[11010048]{0:T(1024)(128)(4,1)} %bitcast.118), calls=%async_computation.10 | async-start | bytes 8388608
  292.1 5.5 %slice-start.2 = ((s8[11010048]{0:T(1024)(128)(4,1)}), s8[2621440]{0:T(1024)(128)(4,1)S(1)}, s32[]{:S(2)}) async-start(s8[11010048]{0:T(1024)(128)(4,1)} %bitcast.118), calls=%async_computation.11 | async-start | bytes 5242880
  309.1 42.6 %copy-start.3 = (bf16[2,256,384]{2,1,0:T(8,128)(2,1)S(1)}, bf16[2,256,384]{2,1,0:T(8,128)(2,1)}, u32[]{:S(2)}) copy-start(bf16[2,256,384]{2,1,0:T(8,128)(2,1)} %param.13) | copy-start | bytes 1179652
  309.1 42.6 %copy-start.4 = (bf16[1,2,32,384]{3,2,1,0:T(8,128)(2,1)S(1)}, bf16[1,2,32,384]{3,2,1,0:T(8,128)(2,1)}, u32[]{:S(2)}) copy-start(bf16[1,2,32,384]{3,2,1,0:T(8,128)(2,1)} %param.12) | copy-start | bytes 147460
  351.6 11.4 %copy-start.1 = (bf16[192,3,384]{2,0,1:T(8,128)(2,1)S(1)}, bf16[192,3,384]{2,0,1:T(8,128)(2,1)}, u32[]{:S(2)}) copy-start(bf16[192,3,384]{2,0,1:T(8,128)(2,1)} %param.15) | copy-start | bytes 1327108
  352.6 9.3 %all-to-all-start.4 = ((bf16[2,1,256,384]{3,2,1,0:T(8,128)(2,1)}), bf16[2,1,256,384]{3,2,1,0:T(8,128)(2,1)S(1)}, u32[]{:S(2)}, u32[]{:S(2)}) async-start(bf16[2,1,256,384]{3,2,1,0:T(8,128)(2,1)} %slice_bitcast_fusion.2), calls=%async_computation.4 | async-start | bytes 786432 | tf_op jit(solution)/shard_map/all_to_all | solution.py:232
Sparse Core Ops, SparseCore 0:
  11.0 81.1 all-gather.4
  94.6 195.1 all-gather.2
  309.2 41.0 reduce-scatter.3

commit v6 on v5

--- a/solution.py
+++ b/solution.py
@@ -216,16 +216,24 @@
     attended = returned.reshape(prompts, heads_local, local_len, HD)
     attended = attended.transpose(0, 2, 1, 3).reshape(row_count, heads_local * HD)
     activated = jax.nn.gelu(mlp_units, approximate=True).astype(jnp.bfloat16)
-    terms_by_feature = lax.dot_general(
-        tail_full[:, up_cols:],
-        jnp.concatenate([attended, activated], axis=1),
-        (((1,), (1,)), ((), ())),
-        preferred_element_type=jnp.float32,
-    )
-    branch = lax.psum_scatter(
-        terms_by_feature.astype(jnp.bfloat16), "wblk", scatter_dimension=0, tiled=True
-    )
-    branch = branch.T.reshape(prompts, local_len, dim_local).astype(jnp.float32)
+    out_weight_t = tail_full[:, up_cols:]
+    mixed_rows = jnp.concatenate([attended, activated], axis=1)
+    first_rows = mixed_rows[:local_len]
+    second_rows = mixed_rows[local_len:]
+    first_terms = lax.dot_general(
+        out_weight_t, first_rows, (((1,), (1,)), ((), ())), preferred_element_type=jnp.float32
+    )
+    second_terms = lax.dot_general(
+        out_weight_t, second_rows, (((1,), (1,)), ((), ())), preferred_element_type=jnp.float32
+    )
+    first_branch = lax.psum_scatter(
+        first_terms.astype(jnp.bfloat16), "wblk", scatter_dimension=0, tiled=True
+    ).astype(jnp.float32)
+    second_parts = lax.all_to_all(
+        second_terms.astype(jnp.bfloat16).reshape(wblk_count, dim_local, -1), "wblk", 0, 0, tiled=True
+    )
+    second_branch = jnp.sum(second_parts.astype(jnp.float32), axis=0)
+    branch = jnp.stack([first_branch.T, second_branch.T])
     layer_out = hidden + modulation[2] * branch
     text_out = layer_out[:, :text_rows].astype(jnp.bfloat16)[None]
     image_out = layer_out[:, text_rows:]

time: 370 us -> 373 us (level)
  blocking collectives: 60.7 us -> 96.8 us
  waiting for transfers between devices: 185 us -> 153 us
    all_to_all x0 -> x1, blocking collectives: none -> 36.1 us  [shards(): lax.all_to_all(second_terms.astype(jnp.bfloat16).reshape(wblk_count, dim_...]
    unnamed x4, waiting for transfers between devices: 41.3 us -> 8.73 us
    unnamed x31 -> x33, local copies, waits for them, and re-layouts: 10.7 us -> 7.79 us
  transfers between devices with their start and end apart: 7 -> 7, of which waited for: 6 -> 6; matrix products, arithmetic and copies ran while one was open for 14% -> 15% of each run, Pallas kernels for 0% -> 0%
where the time goes in v6:
time: 373 us; the launch traced here: 372 us
  waiting for transfers between devices  153 us (41%)
  blocking collectives  96.8 us (26%)
  matrix products  33.3 us (9%)
  starting transfers between devices  30.9 us (8%)
  local copies, waits for them, and re-layouts  27.4 us (7%)
  other arithmetic  15.9 us (4%)
  between operations  15 us (4%)
    all_to_all x1, waiting for transfers between devices, shards(): received = lax.all_to_all(send, 'seq', 0, 0, tiled=True)  84.3 us
    all_to_all x1, blocking collectives, shards(): returned = lax.all_to_all(mixed, 'seq', 0, 0, tiled=True)  45.8 us
    all_to_all x1, waiting for transfers between devices, shards(): gathered = lax.all_to_all(spread, 'wblk', 0, 0, tiled=True)  41.6 us
    all_to_all x1, blocking collectives, shards(): lax.all_to_all(second_terms.astype(jnp.bfloat16).reshape(wblk_count, dim_...  36.1 us
    psum x1, blocking collectives, shards(): lax.psum((jnp.sum(hidden, axis=-1), jnp.sum(hidden * hidden, axis=-1)), '...  14.8 us
    all_gather x1, waiting for transfers between devices, shards(): tail_full = lax.all_gather(tail_source, 'seq', axis=0, tiled=True)  11.7 us
    all_to_all x1, starting transfers between devices, shards(): lax.all_to_all(mod_spread, 'seq', 0, 0, tiled=True)  11.5 us
    all_to_all x1, starting transfers between devices, shards(): received = lax.all_to_all(send, 'seq', 0, 0, tiled=True)  11 us
  transfers between devices with their start and end apart: 7, of which 6 were waited for; matrix products, arithmetic and copies ran while one was open for 15% of the time, Pallas kernels for 0%

profile of v6, /device:TPU:2, one launch (start us, length us, event | category | flops | bytes accessed | tf_op | source)
XLA Modules:
  0.0 372.3 jit_solution(17623773927569451466)
XLA Ops:
  7.2 1.9 reshape.346
  9.9 0.8 fusion.74
  10.7 0.2 fusion.48
  10.9 0.7 broadcast_in_dim.24
  11.6 11.5 %all-to-all-start = ((f32[16,3,384]{2,1,0:T(4,128)}), f32[16,3,384]{2,1,0:T(4,128)S(1)}, u32[]{:S(2)}, u32[]{:S(2)}) async-start(f32[16,3,384]{2,1,0:T(4,128)} %broadcast_in_dim.24), calls=%async_computation | async-start | bytes 196608 | tf_op jit(solution)/shard_map/all_to_all | solution.py:124
  23.0 1.3 convert_reduce_fusion.1
  24.3 14.8 %all-reduce.2 = (f32[2,288]{1,0:T(2,128)S(1)}, f32[2,288]{1,0:T(2,128)S(1)}) all-reduce(f32[2,288]{1,0:T(2,128)S(1)} %get-tuple-element.10, f32[2,288]{1,0:T(2,128)S(1)} %get-tuple-element.9), channel_id=1, replica_groups=mesh['cfg'=2,'seq'=16,'wblk'=8] {'wblk'}, use_global_device_ids=true, to_apply=%region_4.5 | all-reduce | flops 1152 | bytes 9216 | tf_op jit(solution)/shard_map/psum | solution.py:127
  39.2 0.1 mul.307
  39.3 0.1 sub.82
  39.4 1.0 fusion.44
  40.5 2.1 broadcast_in_dim.25
  42.6 4.6 %all-to-all-start.1 = ((bf16[8,576,384]{2,1,0:T(8,128)(2,1)}), bf16[8,576,384]{2,1,0:T(8,128)(2,1)}, u32[]{:S(2)}, u32[]{:S(2)}) async-start(bf16[8,576,384]{2,1,0:T(8,128)(2,1)} %broadcast_in_dim.25), calls=%async_computation.1 | async-start | bytes 7077888 | tf_op jit(solution)/shard_map/all_to_all | solution.py:142
  47.3 0.9 pad_maximum_fusion.1
  48.2 41.6 %all-to-all-done.1 = bf16[8,576,384]{2,1,0:T(8,128)(2,1)} async-done(((bf16[8,576,384]{2,1,0:T(8,128)(2,1)}), bf16[8,576,384]{2,1,0:T(8,128)(2,1)}, u32[]{:S(2)}, u32[]{:S(2)}) %all-to-all-start.1) | async-done | bytes 3538976 | tf_op jit(solution)/shard_map/all_to_all | solution.py:142
  89.8 0.1 mul.335
  90.0 0.1 mul.316
  90.3 0.1 broadcast_multiply_fusion.1
  90.4 0.4 fusion.55
  90.8 1.4 all-gather.5.cloned.1.call-done
  92.2 7.1 %copy.73 = bf16[8,384,768]{1,0,2:T(8,128)(2,1)} copy(bf16[8,384,768]{2,1,0:T(8,128)(2,1)} %bitcast.127) | data formatting | bytes 9437184 | tf_op jit(solution)/shard_map/reshape | solution.py:153
  99.3 6.9 %fusion.34 = f32[2,288,3,2,128]{4,1,3,2,0:T(8,128)S(1)} fusion(bf16[3,2,128,384,8]{3,4,2,1,0:T(8,128)(2,1)} %bitcast.128, bf16[2,288,384,8,1,1]{2,1,0,3,5,4:T(8,128)(2,1)} %bitcast.10), kind=kOutput, calls=%fused_computation.31 | convolution fusion | flops 2717908992 | bytes 10027008 | tf_op jit(solution)/shard_map/wrf,wfn->rn/dot_general | solution.py:150
  106.3 0.5 multiply_reduce_fusion.2
  106.8 0.5 copy.62
  107.3 0.5 copy.60
  107.8 0.4 multiply_multiply_fusion.1
  108.2 0.4 multiply_multiply_fusion.2
  108.6 0.8 subtract_convert_fusion.1
  109.4 0.6 pad_maximum_fusion.5
  110.0 0.5 copy.61
  110.5 0.6 pad_maximum_fusion.6
  111.0 0.5 copy.63
  111.5 0.2 broadcast_in_dim.29
  111.7 0.2 broadcast_in_dim.35
  111.9 1.7 pad_maximum_fusion
  113.6 11.0 %all-to-all-start.2 = ((bf16[16,648,128]{2,1,0:T(8,128)(2,1)}), bf16[16,648,128]{2,1,0:T(8,128)(2,1)S(1)}, u32[]{:S(2)}, u32[]{:S(2)}) async-start(bf16[16,648,128]{2,1,0:T(8,128)(2,1)} %pad_maximum_fusion), calls=%async_computation.2 | async-start | bytes 5308416 | tf_op jit(solution)/shard_map/all_to_all | solution.py:193
  124.6 0.2 reduce-scatter.4.cloned.1.call-start
  124.9 0.6 dynamic_slice.10
  125.4 0.7 fusion.65
  126.1 84.3 %all-to-all-done.2 = bf16[16,648,128]{2,1,0:T(8,128)(2,1)S(1)} async-done(((bf16[16,648,128]{2,1,0:T(8,128)(2,1)}), bf16[16,648,128]{2,1,0:T(8,128)(2,1)S(1)}, u32[]{:S(2)}, u32[]{:S(2)}) %all-to-all-start.2) | async-done | bytes 2654240 | tf_op jit(solution)/shard_map/all_to_all | solution.py:193
  210.4 0.2 fusion.78
  210.6 3.5 fusion.79
  214.1 4.2 %fusion.1 = f32[1152]{0:T(1024)S(1)} fusion(f32[1152,4608]{1,0:T(8,128)S(1)} %get-tuple-element.35, f32[1152]{0:T(1024)S(1)} %get-tuple-element.34), kind=kLoop, calls=%fused_computation.3 | loop fusion | flops 10615680 | bytes 21242880 | tf_op jit(solution)/shard_map/reduce_sum | solution.py:210
  218.3 3.2 copy-done.2
  221.5 10.5 %fusion.23 = bf16[1152,128]{1,0:T(8,128)(2,1)S(1)} fusion(bf16[4608,128]{1,0:T(8,128)(2,1)S(1)} %bitcast.125, f32[1152,4608]{1,0:T(8,128)} %copy-done.2, f32[1152]{0:T(1024)S(1)} %get-tuple-element.34, f32[1152]{0:T(1024)S(1)} %fusion.1), kind=kOutput, calls=%fused_computation.21 | convolution fusion | flops 1369866240 | bytes 22717440 | tf_op jit(solution)/shard_map/dot_general | solution.py:211
  232.0 45.8 %all_to_all.34 = bf16[16,72,128]{2,1,0:T(8,128)(2,1)S(1)} all-to-all(bf16[16,72,128]{2,1,0:T(8,128)(2,1)S(1)} %bitcast.139), channel_id=1, replica_groups=mesh['cfg'=2,'seq'=16,'wblk'=8] {'seq'}, dimensions={0} | all-to-all | bytes 589824 | tf_op jit(solution)/shard_map/all_to_all | solution.py:215
  277.8 0.2 copy.64
  278.1 11.7 %all-gather.3.cloned.1.call-done = bf16[3072,1792]{1,0:T(8,128)(2,1)} async-done(((bf16[192,1792]{1,0:T(8,128)(2,1)}), bf16[3072,1792]{1,0:T(8,128)(2,1)}) %all-gather.3.cloned.1.call-update) | async-done | bytes 11010064 | tf_op jit(solution)/shard_map/all_gather | solution.py:148
  289.8 2.3 slice-done.3
  292.1 5.4 %fusion.33 = bf16[576,768]{1,0:T(8,128)(2,1)S(1)} fusion(bf16[8,576,384]{2,1,0:T(8,128)(2,1)} %all-to-all-done.1, bf16[8,384,768]{2,1,0:T(8,128)(2,1)S(1)} %bitcast.131), kind=kOutput, calls=%fused_computation.29 | convolution fusion | flops 2721890304 | bytes 9142272 | tf_op jit(solution)/shard_map/wrf,wfn->rn/dot_general | solution.py:156
  297.6 0.9 copy-done.11
  298.5 2.0 fusion.13
  300.5 2.4 copy.74
  303.0 4.9 %fusion.16 = bf16[3072,288]{0,1:T(8,128)(2,1)S(1)} fusion(bf16[3072,1792]{1,0:T(8,128)(2,1)} %all-gather.3.cloned.1.call-done, bf16[576,768]{1,0:T(8,128)(2,1)} %copy-done.11, bf16[576,256]{1,0:T(8,128)(2,1)S(1)} %bitcast.151), kind=kOutput, calls=%fused_computation.15 | convolution fusion | flops 1814003712 | bytes 9240576 | tf_op jit(solution)/shard_map/dot_general | solution.py:226
  307.9 0.2 copy.104
  308.1 36.1 %all_to_all.35 = bf16[8,384,288]{1,2,0:T(8,128)(2,1)S(1)} all-to-all(bf16[8,384,288]{1,2,0:T(8,128)(2,1)S(1)} %bitcast.124), channel_id=1, replica_groups=mesh['cfg'=2,'seq'=16,'wblk'=8] {'wblk'}, dimensions={0} | all-to-all | bytes 3538944 | tf_op jit(solution)/shard_map/all_to_all | solution.py:232
  344.2 0.2 convert_reduce_fusion
  344.4 8.7 %reduce-scatter.4.cloned.1.call-done = bf16[384,288]{1,0:T(8,128)(2,1)} async-done(((bf16[3072,288]{1,0:T(8,128)(2,1)}), bf16[384,288]{1,0:T(8,128)(2,1)}) %reduce-scatter.4.cloned.1.call-update) | async-done | bytes 221200
  353.1 1.1 copy.75
  354.3 0.1 fusion.40
  354.4 0.8 slice_bitcast_fusion.2
  355.2 3.5 all-to-all-start.5
  358.8 0.6 slice_bitcast_fusion.3
  359.4 5.4 %all-to-all-done.5 = bf16[2,1,256,384]{3,2,1,0:T(8,128)(2,1)S(1)} async-done(((bf16[2,1,256,384]{3,2,1,0:T(8,128)(2,1)}), bf16[2,1,256,384]{3,2,1,0:T(8,128)(2,1)S(1)}, u32[]{:S(2)}, u32[]{:S(2)}) %all-to-all-start.5) | async-done | bytes 393248 | tf_op jit(solution)/shard_map/all_to_all | solution.py:240
  364.8 1.0 multiply_add_fusion
  (56 shorter events, 0.8 us)
Async XLA Ops:
  7.2 3.5 copy-start
  7.2 32.2 %copy-start.3 = (bf16[2,256,384]{2,1,0:T(8,128)(2,1)S(1)}, bf16[2,256,384]{2,1,0:T(8,128)(2,1)}, u32[]{:S(2)}) copy-start(bf16[2,256,384]{2,1,0:T(8,128)(2,1)} %param.13) | copy-start | bytes 1179652
  7.2 85.0 %all-gather.5.cloned.1.call-start = ((), (), s32[]{:S(2)}) async-start(), calls=%async_computation.8 | async-start | bytes 5013504 | tf_op jit(solution)/shard_map/all_gather | solution.py:137
  11.6 27.8 %all-to-all-start = ((f32[16,3,384]{2,1,0:T(4,128)}), f32[16,3,384]{2,1,0:T(4,128)S(1)}, u32[]{:S(2)}, u32[]{:S(2)}) async-start(f32[16,3,384]{2,1,0:T(4,128)} %broadcast_in_dim.24), calls=%async_computation | async-start | bytes 196608 | tf_op jit(solution)/shard_map/all_to_all | solution.py:124
  42.6 4.7 %copy-start.5 = (bf16[768,192]{0,1:T(8,128)(2,1)S(1)}, bf16[768,192]{0,1:T(8,128)(2,1)}, u32[]{:S(2)}) copy-start(bf16[768,192]{0,1:T(8,128)(2,1)} %param.21) | copy-start | bytes 884740
  42.6 4.7 %copy-start.7 = (bf16[256,192]{0,1:T(8,128)(2,1)S(1)}, bf16[256,192]{0,1:T(8,128)(2,1)}, u32[]{:S(2)}) copy-start(bf16[256,192]{0,1:T(8,128)(2,1)} %param.20) | copy-start | bytes 294916
  42.6 4.8 %copy-start.6 = (bf16[192,768]{1,0:T(8,128)(2,1)S(1)}, bf16[192,768]{1,0:T(8,128)(2,1)}, u32[]{:S(2)}) copy-start(bf16[192,768]{1,0:T(8,128)(2,1)} %param.17) | copy-start | bytes 884740
  42.6 47.3 %all-to-all-start.1 = ((bf16[8,576,384]{2,1,0:T(8,128)(2,1)}), bf16[8,576,384]{2,1,0:T(8,128)(2,1)}, u32[]{:S(2)}, u32[]{:S(2)}) async-start(bf16[8,576,384]{2,1,0:T(8,128)(2,1)} %broadcast_in_dim.25), calls=%async_computation.1 | async-start | bytes 7077888 | tf_op jit(solution)/shard_map/all_to_all | solution.py:142
  47.2 42.6 %copy-start.8 = (f32[128]{0:T(128)S(1)}, f32[128]{0:T(128)}, u32[]{:S(2)}) copy-start(f32[128]{0:T(128)} %param.18) | copy-start | bytes 1540
  47.2 42.8 %copy-start.9 = (f32[128]{0:T(128)S(1)}, f32[128]{0:T(128)}, u32[]{:S(2)}) copy-start(f32[128]{0:T(128)} %param.19) | copy-start | bytes 1540
  47.2 242.6 %all-gather.3.cloned.1.call-start = ((), (), s32[]{:S(2)}) async-start(), calls=%async_computation.7 | async-start | bytes 11698176 | tf_op jit(solution)/shard_map/all_gather | solution.py:148
  113.6 11.3 %copy-start.10 = (s32[2]{0:T(128)S(1)}, s32[2]{0:T(128)}, u32[]{:S(2)}) copy-start(s32[2]{0:T(128)} %param.22) | copy-start | bytes 28
  113.6 96.8 %all-to-all-start.2 = ((bf16[16,648,128]{2,1,0:T(8,128)(2,1)}), bf16[16,648,128]{2,1,0:T(8,128)(2,1)S(1)}, u32[]{:S(2)}, u32[]{:S(2)}) async-start(bf16[16,648,128]{2,1,0:T(8,128)(2,1)} %pad_maximum_fusion), calls=%async_computation.2 | async-start | bytes 5308416 | tf_op jit(solution)/shard_map/all_to_all | solution.py:193
  124.6 228.5 %reduce-scatter.4.cloned.1.call-start = ((), (), s32[]{:S(2)}) async-start(), calls=%async_computation.9 | async-start | bytes 2654208
  214.1 7.5 %copy-start.2 = (f32[1152,4608]{1,0:T(8,128)}, f32[1152,4608]{1,0:T(8,128)S(1)}, u32[]{:S(2)}) copy-start(f32[1152,4608]{1,0:T(8,128)S(1)} %get-tuple-element.35) | copy-start | bytes 63700996
  289.8 2.3 slice-start.3
  289.8 8.7 %slice-start = ((s8[11010048]{0:T(1024)(128)(4,1)}), s8[4194304]{0:T(1024)(128)(4,1)S(1)}, s32[]{:S(2)}) async-start(s8[11010048]{0:T(1024)(128)(4,1)} %bitcast.129), calls=%async_computation.10 | async-start | bytes 8388608
  292.1 6.4 %slice-start.1 = ((s8[11010048]{0:T(1024)(128)(4,1)}), s8[4194304]{0:T(1024)(128)(4,1)S(1)}, s32[]{:S(2)}) async-start(s8[11010048]{0:T(1024)(128)(4,1)} %bitcast.129), calls=%async_computation.11 | async-start | bytes 8388608
  292.1 6.4 %slice-start.2 = ((s8[11010048]{0:T(1024)(128)(4,1)}), s8[2621440]{0:T(1024)(128)(4,1)S(1)}, s32[]{:S(2)}) async-start(s8[11010048]{0:T(1024)(128)(4,1)} %bitcast.129), calls=%async_computation.12 | async-start | bytes 5242880
  297.6 0.9 copy-start.11
  308.0 46.2 %copy-start.4 = (bf16[1,2,32,384]{3,2,1,0:T(8,128)(2,1)S(1)}, bf16[1,2,32,384]{3,2,1,0:T(8,128)(2,1)}, u32[]{:S(2)}) copy-start(bf16[1,2,32,384]{3,2,1,0:T(8,128)(2,1)} %param.12) | copy-start | bytes 147460
  354.3 11.5 %copy-start.1 = (bf16[192,3,384]{2,0,1:T(8,128)(2,1)S(1)}, bf16[192,3,384]{2,0,1:T(8,128)(2,1)}, u32[]{:S(2)}) copy-start(bf16[192,3,384]{2,0,1:T(8,128)(2,1)} %param.15) | copy-start | bytes 1327108
  355.2 9.6 %all-to-all-start.5 = ((bf16[2,1,256,384]{3,2,1,0:T(8,128)(2,1)}), bf16[2,1,256,384]{3,2,1,0:T(8,128)(2,1)S(1)}, u32[]{:S(2)}, u32[]{:S(2)}) async-start(bf16[2,1,256,384]{3,2,1,0:T(8,128)(2,1)} %slice_bitcast_fusion.2), calls=%async_computation.5 | async-start | bytes 786432 | tf_op jit(solution)/shard_map/all_to_all | solution.py:240
Sparse Core Ops, SparseCore 0:
  11.0 81.1 all-gather.4
  94.6 195.1 all-gather.2
  303.1 49.9 reduce-scatter.3

commit v7 on v5

--- a/solution.py
+++ b/solution.py
@@ -216,16 +216,16 @@
     attended = returned.reshape(prompts, heads_local, local_len, HD)
     attended = attended.transpose(0, 2, 1, 3).reshape(row_count, heads_local * HD)
     activated = jax.nn.gelu(mlp_units, approximate=True).astype(jnp.bfloat16)
-    terms_by_feature = lax.dot_general(
-        tail_full[:, up_cols:],
+    block_terms = jnp.einsum(
+        "bjk,rk->brj",
+        tail_full[:, up_cols:].reshape(wblk_count, dim_local, -1),
         jnp.concatenate([attended, activated], axis=1),
-        (((1,), (1,)), ((), ())),
         preferred_element_type=jnp.float32,
     )
     branch = lax.psum_scatter(
-        terms_by_feature.astype(jnp.bfloat16), "wblk", scatter_dimension=0, tiled=True
-    )
-    branch = branch.T.reshape(prompts, local_len, dim_local).astype(jnp.float32)
+        block_terms.astype(jnp.bfloat16), "wblk", scatter_dimension=0, tiled=True
+    )
+    branch = branch.reshape(prompts, local_len, dim_local).astype(jnp.float32)
     layer_out = hidden + modulation[2] * branch
     text_out = layer_out[:, :text_rows].astype(jnp.bfloat16)[None]
     image_out = layer_out[:, text_rows:]

time: 370 us -> 365 us (0.986)
  local copies, waits for them, and re-layouts: 30.1 us -> 25.5 us
    unnamed x4 -> x3, waiting for transfers between devices: 41.3 us -> 0.05 us
    reduce_scatter x0 -> x1, waiting for transfers between devices: none -> 40.3 us  [shards(): lax.psum_scatter(block_terms.astype(jnp.bfloat16), 'wblk', scatter_dimens...]
    unnamed x31 -> x23, local copies, waits for them, and re-layouts: 10.7 us -> 3.32 us
where the time goes in v7:
time: 365 us
  waiting for transfers between devices  184 us (50%)
  blocking collectives  60.9 us (17%)
  matrix products  31.5 us (9%)
  starting transfers between devices  30.9 us (8%)
  local copies, waits for them, and re-layouts  25.5 us (7%)
  other arithmetic  16.9 us (5%)
  between operations  14.9 us (4%)
    all_to_all x1, waiting for transfers between devices, shards(): received = lax.all_to_all(send, 'seq', 0, 0, tiled=True)  84.1 us
    all_to_all x1, blocking collectives, shards(): returned = lax.all_to_all(mixed, 'seq', 0, 0, tiled=True)  46.1 us
    all_to_all x1, waiting for transfers between devices, shards(): gathered = lax.all_to_all(spread, 'wblk', 0, 0, tiled=True)  41.6 us
    reduce_scatter x1, waiting for transfers between devices, shards(): lax.psum_scatter(block_terms.astype(jnp.bfloat16), 'wblk', scatter_dimens...  40.3 us
    psum x1, blocking collectives, shards(): lax.psum((jnp.sum(hidden, axis=-1), jnp.sum(hidden * hidden, axis=-1)), '...  14.8 us
    all_gather x1, waiting for transfers between devices, shards(): tail_full = lax.all_gather(tail_source, 'seq', axis=0, tiled=True)  11.6 us
    all_to_all x1, starting transfers between devices, shards(): lax.all_to_all(mod_spread, 'seq', 0, 0, tiled=True)  11.5 us
    all_to_all x1, starting transfers between devices, shards(): received = lax.all_to_all(send, 'seq', 0, 0, tiled=True)  11 us
  transfers between devices with their start and end apart: 7, of which 6 were waited for; matrix products, arithmetic and copies ran while one was open for 14% of the time, Pallas kernels for 0%

profile of v7, /device:TPU:2, one launch (start us, length us, event | category | flops | bytes accessed | tf_op | source)
XLA Modules:
  0.0 364.6 jit_solution(7836679243326904469)
XLA Ops:
  7.2 0.0 all-gather.3.cloned.1.call-start
  7.2 1.9 reshape.349
  9.8 0.1 fusion.55
  9.9 0.8 fusion.63
  10.7 0.2 fusion.37
  10.9 0.7 broadcast_in_dim.24
  11.5 11.5 %all-to-all-start = ((f32[16,3,384]{2,1,0:T(4,128)}), f32[16,3,384]{2,1,0:T(4,128)S(1)}, u32[]{:S(2)}, u32[]{:S(2)}) async-start(f32[16,3,384]{2,1,0:T(4,128)} %broadcast_in_dim.24), calls=%async_computation | async-start | bytes 196608 | tf_op jit(solution)/shard_map/all_to_all | solution.py:124
  23.0 1.3 convert_reduce_fusion
  24.3 14.8 %all-reduce.2 = (f32[2,288]{1,0:T(2,128)S(1)}, f32[2,288]{1,0:T(2,128)S(1)}) all-reduce(f32[2,288]{1,0:T(2,128)S(1)} %get-tuple-element.10, f32[2,288]{1,0:T(2,128)S(1)} %get-tuple-element.9), channel_id=1, replica_groups=mesh['cfg'=2,'seq'=16,'wblk'=8] {'wblk'}, use_global_device_ids=true, to_apply=%region_4.5 | all-reduce | flops 1152 | bytes 9216 | tf_op jit(solution)/shard_map/psum | solution.py:127
  39.2 0.1 mul.308
  39.2 0.1 sub.85
  39.4 1.2 fusion.36
  40.6 2.1 broadcast_in_dim.26
  42.7 4.6 %all-to-all-start.1 = ((bf16[8,576,384]{2,1,0:T(8,128)(2,1)}), bf16[8,576,384]{2,1,0:T(8,128)(2,1)}, u32[]{:S(2)}, u32[]{:S(2)}) async-start(bf16[8,576,384]{2,1,0:T(8,128)(2,1)} %broadcast_in_dim.26), calls=%async_computation.1 | async-start | bytes 7077888 | tf_op jit(solution)/shard_map/all_to_all | solution.py:142
  47.4 0.0 all-gather.5.cloned.1.call-start
  47.5 0.9 pad_maximum_fusion.1
  48.4 41.6 %all-to-all-done.1 = bf16[8,576,384]{2,1,0:T(8,128)(2,1)} async-done(((bf16[8,576,384]{2,1,0:T(8,128)(2,1)}), bf16[8,576,384]{2,1,0:T(8,128)(2,1)}, u32[]{:S(2)}, u32[]{:S(2)}) %all-to-all-start.1) | async-done | bytes 3538976 | tf_op jit(solution)/shard_map/all_to_all | solution.py:142
  90.0 0.1 mul.335
  90.2 0.1 mul.316
  90.3 0.1 concatenate.39
  90.4 0.1 concatenate.40
  90.5 0.1 broadcast_multiply_fusion.1
  90.6 0.4 fusion.44
  91.0 1.2 all-gather.3.cloned.1.call-done
  92.2 7.1 %copy.67 = bf16[8,384,768]{1,0,2:T(8,128)(2,1)} copy(bf16[8,384,768]{2,1,0:T(8,128)(2,1)} %bitcast.123) | data formatting | bytes 9437184 | tf_op jit(solution)/shard_map/reshape | solution.py:153
  99.3 6.9 %fusion.24 = f32[2,288,3,2,128]{4,1,3,2,0:T(8,128)S(1)} fusion(bf16[3,2,128,384,8]{3,4,2,1,0:T(8,128)(2,1)} %bitcast.124, bf16[2,288,384,8,1,1]{2,1,0,3,5,4:T(8,128)(2,1)} %bitcast.10), kind=kOutput, calls=%fused_computation.24 | convolution fusion | flops 2717908992 | bytes 10027008 | tf_op jit(solution)/shard_map/wrf,wfn->rn/dot_general | solution.py:150
  106.3 0.5 multiply_reduce_fusion.2
  106.8 0.5 copy.58
  107.3 0.5 copy.56
  107.8 0.4 multiply_multiply_fusion.1
  108.2 0.4 multiply_multiply_fusion.2
  108.5 0.8 subtract_convert_fusion.1
  109.4 0.6 pad_maximum_fusion.3
  109.9 0.5 copy.57
  110.4 0.6 pad_maximum_fusion.4
  111.0 0.5 copy.59
  111.5 0.2 broadcast_in_dim.29
  111.7 0.2 broadcast_in_dim.35
  111.8 1.7 pad_maximum_fusion
  113.5 11.0 %all-to-all-start.2 = ((bf16[16,648,128]{2,1,0:T(8,128)(2,1)}), bf16[16,648,128]{2,1,0:T(8,128)(2,1)S(1)}, u32[]{:S(2)}, u32[]{:S(2)}) async-start(bf16[16,648,128]{2,1,0:T(8,128)(2,1)} %pad_maximum_fusion), calls=%async_computation.2 | async-start | bytes 5308416 | tf_op jit(solution)/shard_map/all_to_all | solution.py:193
  124.6 0.2 reduce-scatter.2.cloned.1.call-start
  124.8 0.6 dynamic_slice.10
  125.4 0.7 fusion.54
  126.1 84.1 %all-to-all-done.2 = bf16[16,648,128]{2,1,0:T(8,128)(2,1)S(1)} async-done(((bf16[16,648,128]{2,1,0:T(8,128)(2,1)}), bf16[16,648,128]{2,1,0:T(8,128)(2,1)S(1)}, u32[]{:S(2)}, u32[]{:S(2)}) %all-to-all-start.2) | async-done | bytes 2654240 | tf_op jit(solution)/shard_map/all_to_all | solution.py:193
  210.2 0.2 fusion.66
  210.4 3.5 fusion.67
  213.9 4.2 %fusion.1 = f32[1152]{0:T(1024)S(1)} fusion(f32[1152,4608]{1,0:T(8,128)S(1)} %get-tuple-element.35, f32[1152]{0:T(1024)S(1)} %get-tuple-element.34), kind=kLoop, calls=%fused_computation.3 | loop fusion | flops 10615680 | bytes 21242880 | tf_op jit(solution)/shard_map/reduce_sum | solution.py:210
  218.1 3.2 copy-done.2
  221.3 10.5 %fusion.13 = bf16[1152,128]{1,0:T(8,128)(2,1)S(1)} fusion(bf16[4608,128]{1,0:T(8,128)(2,1)S(1)} %bitcast.121, f32[1152,4608]{1,0:T(8,128)} %copy-done.2, f32[1152]{0:T(1024)S(1)} %get-tuple-element.34, f32[1152]{0:T(1024)S(1)} %fusion.1), kind=kOutput, calls=%fused_computation.15 | convolution fusion | flops 1369866240 | bytes 22717440 | tf_op jit(solution)/shard_map/dot_general | solution.py:211
  231.8 46.1 %all_to_all.29 = bf16[16,72,128]{2,1,0:T(8,128)(2,1)S(1)} all-to-all(bf16[16,72,128]{2,1,0:T(8,128)(2,1)S(1)} %bitcast.130), channel_id=1, replica_groups=mesh['cfg'=2,'seq'=16,'wblk'=8] {'seq'}, dimensions={0} | all-to-all | bytes 589824 | tf_op jit(solution)/shard_map/all_to_all | solution.py:215
  277.9 0.2 copy.60
  278.2 11.6 %all-gather.5.cloned.1.call-done = bf16[3072,1792]{1,0:T(8,128)(2,1)} async-done(((bf16[192,1792]{1,0:T(8,128)(2,1)}), bf16[3072,1792]{1,0:T(8,128)(2,1)}) %all-gather.5.cloned.1.call-update) | async-done | bytes 11010064 | tf_op jit(solution)/shard_map/all_gather | solution.py:148
  289.8 2.3 slice-done
  292.1 5.2 %fusion.23 = bf16[576,768]{1,0:T(8,128)(2,1)S(1)} fusion(bf16[8,576,384]{2,1,0:T(8,128)(2,1)} %all-to-all-done.1, bf16[8,384,768]{2,1,0:T(8,128)(2,1)S(1)} %bitcast.119), kind=kOutput, calls=%fused_computation.23 | convolution fusion | flops 2721890304 | bytes 9142272 | tf_op jit(solution)/shard_map/wrf,wfn->rn/dot_general | solution.py:156
  297.3 2.8 slice-done.1
  300.1 5.3 %convert_bitcast_fusion = bf16[8,576,384]{2,1,0:T(8,128)(2,1)} fusion(bf16[8,384,1024]{2,1,0:T(8,128)(2,1)S(1)} %bitcast.120, bf16[576,768]{1,0:T(8,128)(2,1)S(1)} %fusion.23, bf16[576,256]{1,0:T(8,128)(2,1)S(1)} %bitcast.142), kind=kOutput, calls=%fused_computation.11 | convolution fusion | flops 3628007424 | bytes 11010048 | tf_op jit(solution)/shard_map/bjk,rk->brj/dot_general | solution.py:219
  305.5 40.3 %reduce-scatter.2.cloned.1.call-done = bf16[1,576,384]{2,1,0:T(8,128)(2,1)} async-done(((bf16[8,576,384]{2,1,0:T(8,128)(2,1)}), bf16[1,576,384]{2,1,0:T(8,128)(2,1)}) %reduce-scatter.2.cloned.1.call-update) | async-done | bytes 442384 | tf_op jit(solution)/shard_map/reduce_scatter | solution.py:225
  345.8 1.2 fusion.32
  346.9 0.8 slice_bitcast_fusion.2
  347.7 3.5 all-to-all-start.4
  351.3 0.6 slice_bitcast_fusion.3
  351.9 5.2 %all-to-all-done.4 = bf16[2,1,256,384]{3,2,1,0:T(8,128)(2,1)S(1)} async-done(((bf16[2,1,256,384]{3,2,1,0:T(8,128)(2,1)}), bf16[2,1,256,384]{3,2,1,0:T(8,128)(2,1)S(1)}, u32[]{:S(2)}, u32[]{:S(2)}) %all-to-all-start.4) | async-done | bytes 393248 | tf_op jit(solution)/shard_map/all_to_all | solution.py:232
  357.1 0.1 bitcast_convert_fusion
  357.1 1.0 multiply_add_fusion
  (42 shorter events, 0.4 us)
Async XLA Ops:
  7.2 3.5 copy-start
  7.2 85.0 %all-gather.3.cloned.1.call-start = ((), (), s32[]{:S(2)}) async-start(), calls=%async_computation.6 | async-start | bytes 5013504 | tf_op jit(solution)/shard_map/all_gather | solution.py:137
  11.5 27.8 %all-to-all-start = ((f32[16,3,384]{2,1,0:T(4,128)}), f32[16,3,384]{2,1,0:T(4,128)S(1)}, u32[]{:S(2)}, u32[]{:S(2)}) async-start(f32[16,3,384]{2,1,0:T(4,128)} %broadcast_in_dim.24), calls=%async_computation | async-start | bytes 196608 | tf_op jit(solution)/shard_map/all_to_all | solution.py:124
  42.7 4.7 %copy-start.5 = (bf16[768,192]{0,1:T(8,128)(2,1)S(1)}, bf16[768,192]{0,1:T(8,128)(2,1)}, u32[]{:S(2)}) copy-start(bf16[768,192]{0,1:T(8,128)(2,1)} %param.21) | copy-start | bytes 884740
  42.7 4.7 %copy-start.7 = (bf16[256,192]{0,1:T(8,128)(2,1)S(1)}, bf16[256,192]{0,1:T(8,128)(2,1)}, u32[]{:S(2)}) copy-start(bf16[256,192]{0,1:T(8,128)(2,1)} %param.20) | copy-start | bytes 294916
  42.7 4.8 %copy-start.6 = (bf16[192,768]{1,0:T(8,128)(2,1)S(1)}, bf16[192,768]{1,0:T(8,128)(2,1)}, u32[]{:S(2)}) copy-start(bf16[192,768]{1,0:T(8,128)(2,1)} %param.17) | copy-start | bytes 884740
  42.7 47.3 %copy-start.8 = (f32[128]{0:T(128)S(1)}, f32[128]{0:T(128)}, u32[]{:S(2)}) copy-start(f32[128]{0:T(128)} %param.18) | copy-start | bytes 1540
  42.7 47.5 %copy-start.9 = (f32[128]{0:T(128)S(1)}, f32[128]{0:T(128)}, u32[]{:S(2)}) copy-start(f32[128]{0:T(128)} %param.19) | copy-start | bytes 1540
  42.7 47.3 %all-to-all-start.1 = ((bf16[8,576,384]{2,1,0:T(8,128)(2,1)}), bf16[8,576,384]{2,1,0:T(8,128)(2,1)}, u32[]{:S(2)}, u32[]{:S(2)}) async-start(bf16[8,576,384]{2,1,0:T(8,128)(2,1)} %broadcast_in_dim.26), calls=%async_computation.1 | async-start | bytes 7077888 | tf_op jit(solution)/shard_map/all_to_all | solution.py:142
  47.4 242.4 %all-gather.5.cloned.1.call-start = ((), (), s32[]{:S(2)}) async-start(), calls=%async_computation.7 | async-start | bytes 11698176 | tf_op jit(solution)/shard_map/all_gather | solution.py:148
  113.5 11.3 %copy-start.10 = (s32[2]{0:T(128)S(1)}, s32[2]{0:T(128)}, u32[]{:S(2)}) copy-start(s32[2]{0:T(128)} %param.22) | copy-start | bytes 28
  113.5 96.6 %all-to-all-start.2 = ((bf16[16,648,128]{2,1,0:T(8,128)(2,1)}), bf16[16,648,128]{2,1,0:T(8,128)(2,1)S(1)}, u32[]{:S(2)}, u32[]{:S(2)}) async-start(bf16[16,648,128]{2,1,0:T(8,128)(2,1)} %pad_maximum_fusion), calls=%async_computation.2 | async-start | bytes 5308416 | tf_op jit(solution)/shard_map/all_to_all | solution.py:193
  124.6 221.2 %reduce-scatter.2.cloned.1.call-start = ((), (), s32[]{:S(2)}) async-start(), calls=%async_computation.8 | async-start | bytes 3981312 | tf_op jit(solution)/shard_map/reduce_scatter | solution.py:225
  213.9 7.5 %copy-start.2 = (f32[1152,4608]{1,0:T(8,128)}, f32[1152,4608]{1,0:T(8,128)S(1)}, u32[]{:S(2)}) copy-start(f32[1152,4608]{1,0:T(8,128)S(1)} %get-tuple-element.35) | copy-start | bytes 63700996
  289.8 2.3 slice-start
  297.3 2.8 slice-start.1
  305.4 40.4 %copy-start.3 = (bf16[2,256,384]{2,1,0:T(8,128)(2,1)S(1)}, bf16[2,256,384]{2,1,0:T(8,128)(2,1)}, u32[]{:S(2)}) copy-start(bf16[2,256,384]{2,1,0:T(8,128)(2,1)} %param.13) | copy-start | bytes 1179652
  305.4 40.4 %copy-start.4 = (bf16[1,2,32,384]{3,2,1,0:T(8,128)(2,1)S(1)}, bf16[1,2,32,384]{3,2,1,0:T(8,128)(2,1)}, u32[]{:S(2)}) copy-start(bf16[1,2,32,384]{3,2,1,0:T(8,128)(2,1)} %param.12) | copy-start | bytes 147460
  305.4 52.6 %copy-start.1 = (bf16[192,3,384]{2,0,1:T(8,128)(2,1)S(1)}, bf16[192,3,384]{2,0,1:T(8,128)(2,1)}, u32[]{:S(2)}) copy-start(bf16[192,3,384]{2,0,1:T(8,128)(2,1)} %param.15) | copy-start | bytes 1327108
  347.7 9.3 %all-to-all-start.4 = ((bf16[2,1,256,384]{3,2,1,0:T(8,128)(2,1)}), bf16[2,1,256,384]{3,2,1,0:T(8,128)(2,1)S(1)}, u32[]{:S(2)}, u32[]{:S(2)}) async-start(bf16[2,1,256,384]{3,2,1,0:T(8,128)(2,1)} %slice_bitcast_fusion.2), calls=%async_computation.5 | async-start | bytes 786432 | tf_op jit(solution)/shard_map/all_to_all | solution.py:232
Sparse Core Ops, SparseCore 0:
  11.0 81.1 all-gather.2
  94.6 195.1 all-gather.4
  305.6 40.1 reduce-scatter.1

commit v8 on v7

--- a/solution.py
+++ b/solution.py
@@ -229,11 +229,15 @@
     layer_out = hidden + modulation[2] * branch
     text_out = layer_out[:, :text_rows].astype(jnp.bfloat16)[None]
     image_out = layer_out[:, text_rows:]
-    paired = lax.all_to_all(
-        image_out[:, None].astype(jnp.bfloat16), "cfg", split_axis=0, concat_axis=1, tiled=True
-    ).astype(jnp.float32)
-    velocity = paired[:, 1] + guidance * (paired[:, 0] - paired[:, 1])
     own_prompts = prompts // 2
+    rounded_out = image_out.astype(jnp.bfloat16)
+    kept = lax.dynamic_slice_in_dim(rounded_out, cfg_pos * own_prompts, own_prompts, 0)
+    given = lax.dynamic_slice_in_dim(rounded_out, (1 - cfg_pos) * own_prompts, own_prompts, 0)
+    taken = lax.ppermute(given, "cfg", [(0, 1), (1, 0)]).astype(jnp.float32)
+    kept = kept.astype(jnp.float32)
+    conditional = jnp.where(cfg_pos == 0, kept, taken)
+    unconditional = jnp.where(cfg_pos == 0, taken, kept)
+    velocity = unconditional + guidance * (conditional - unconditional)
     latent = lax.dynamic_slice_in_dim(image_tokens, cfg_pos * own_prompts, own_prompts, 0).astype(
         jnp.float32
     )

time: 365 us -> 361 us (0.989)
    all_to_all x1 -> x0, waiting for transfers between devices: 5.18 us -> none  [shards(): lax.all_to_all(image_out[:, None].astype(jnp.bfloat16), 'cfg', split_axis...]
where the time goes in v8:
time: 361 us; the launch traced here: 360 us
  waiting for transfers between devices  182 us (50%)
  blocking collectives  60.9 us (17%)
  matrix products  31.5 us (9%)
  starting transfers between devices  29.2 us (8%)
  local copies, waits for them, and re-layouts  24.8 us (7%)
  other arithmetic  16.9 us (5%)
  between operations  14.9 us (4%)
    all_to_all x1, waiting for transfers between devices, shards(): received = lax.all_to_all(send, 'seq', 0, 0, tiled=True)  84.1 us
    all_to_all x1, blocking collectives, shards(): returned = lax.all_to_all(mixed, 'seq', 0, 0, tiled=True)  46.1 us
    all_to_all x1, waiting for transfers between devices, shards(): gathered = lax.all_to_all(spread, 'wblk', 0, 0, tiled=True)  41.6 us
    reduce_scatter x1, waiting for transfers between devices, shards(): lax.psum_scatter(block_terms.astype(jnp.bfloat16), 'wblk', scatter_dimens...  40.3 us
    psum x1, blocking collectives, shards(): lax.psum((jnp.sum(hidden, axis=-1), jnp.sum(hidden * hidden, axis=-1)), '...  14.8 us
    all_gather x1, waiting for transfers between devices, shards(): tail_full = lax.all_gather(tail_source, 'seq', axis=0, tiled=True)  11.6 us
    all_to_all x1, starting transfers between devices, shards(): lax.all_to_all(mod_spread, 'seq', 0, 0, tiled=True)  11.5 us
    all_to_all x1, starting transfers between devices, shards(): received = lax.all_to_all(send, 'seq', 0, 0, tiled=True)  11 us
  transfers between devices with their start and end apart: 7, of which 6 were waited for; matrix products, arithmetic and copies ran while one was open for 14% of the time, Pallas kernels for 0%

profile of v8, /device:TPU:2, one launch (start us, length us, event | category | flops | bytes accessed | tf_op | source)
XLA Modules:
  0.0 360.3 jit_solution(17261281872503916280)
XLA Ops:
  7.2 0.0 all-gather.3.cloned.1.call-start
  7.2 1.9 reshape.279
  9.1 0.0 all-gather.3.cloned.1.call-update
  9.8 0.1 fusion.55
  9.9 0.8 fusion.63
  10.7 0.2 fusion.37
  10.9 0.7 broadcast_in_dim.24
  11.5 11.5 %all-to-all-start = ((f32[16,3,384]{2,1,0:T(4,128)}), f32[16,3,384]{2,1,0:T(4,128)S(1)}, u32[]{:S(2)}, u32[]{:S(2)}) async-start(f32[16,3,384]{2,1,0:T(4,128)} %broadcast_in_dim.24), calls=%async_computation | async-start | bytes 196608 | tf_op jit(solution)/shard_map/all_to_all | solution.py:124
  23.0 1.3 convert_reduce_fusion
  24.3 14.8 %all-reduce.2 = (f32[2,288]{1,0:T(2,128)S(1)}, f32[2,288]{1,0:T(2,128)S(1)}) all-reduce(f32[2,288]{1,0:T(2,128)S(1)} %get-tuple-element.10, f32[2,288]{1,0:T(2,128)S(1)} %get-tuple-element.9), channel_id=1, replica_groups=mesh['cfg'=2,'seq'=16,'wblk'=8] {'wblk'}, use_global_device_ids=true, to_apply=%region_4.5 | all-reduce | flops 1152 | bytes 9216 | tf_op jit(solution)/shard_map/psum | solution.py:127
  39.2 0.1 mul.288
  39.2 0.1 sub.76
  39.4 1.2 fusion.36
  40.6 2.1 broadcast_in_dim.26
  42.7 4.7 %all-to-all-start.1 = ((bf16[8,576,384]{2,1,0:T(8,128)(2,1)}), bf16[8,576,384]{2,1,0:T(8,128)(2,1)}, u32[]{:S(2)}, u32[]{:S(2)}) async-start(bf16[8,576,384]{2,1,0:T(8,128)(2,1)} %broadcast_in_dim.26), calls=%async_computation.1 | async-start | bytes 7077888 | tf_op jit(solution)/shard_map/all_to_all | solution.py:142
  47.4 0.0 all-gather.5.cloned.1.call-start
  47.5 0.9 pad_maximum_fusion.1
  48.4 41.6 %all-to-all-done.1 = bf16[8,576,384]{2,1,0:T(8,128)(2,1)} async-done(((bf16[8,576,384]{2,1,0:T(8,128)(2,1)}), bf16[8,576,384]{2,1,0:T(8,128)(2,1)}, u32[]{:S(2)}, u32[]{:S(2)}) %all-to-all-start.1) | async-done | bytes 3538976 | tf_op jit(solution)/shard_map/all_to_all | solution.py:142
  90.0 0.0 all-gather.5.cloned.1.call-update
  90.0 0.1 mul.315
  90.2 0.1 mul.296
  90.3 0.1 concatenate.39
  90.4 0.1 concatenate.40
  90.5 0.1 broadcast_multiply_fusion.1
  90.6 0.4 fusion.44
  91.0 1.2 all-gather.3.cloned.1.call-done
  92.2 7.1 %copy.67 = bf16[8,384,768]{1,0,2:T(8,128)(2,1)} copy(bf16[8,384,768]{2,1,0:T(8,128)(2,1)} %bitcast.104) | data formatting | bytes 9437184 | tf_op jit(solution)/shard_map/reshape | solution.py:153
  99.3 6.9 %fusion.24 = f32[2,288,3,2,128]{4,1,3,2,0:T(8,128)S(1)} fusion(bf16[3,2,128,384,8]{3,4,2,1,0:T(8,128)(2,1)} %bitcast.105, bf16[2,288,384,8,1,1]{2,1,0,3,5,4:T(8,128)(2,1)} %bitcast.10), kind=kOutput, calls=%fused_computation.24 | convolution fusion | flops 2717908992 | bytes 10027008 | tf_op jit(solution)/shard_map/wrf,wfn->rn/dot_general | solution.py:150
  106.3 0.5 multiply_reduce_fusion.2
  106.8 0.5 copy.58
  107.3 0.5 copy.56
  107.8 0.4 multiply_multiply_fusion.1
  108.2 0.4 multiply_multiply_fusion.2
  108.6 0.8 subtract_convert_fusion.1
  109.4 0.6 pad_maximum_fusion.3
  110.0 0.5 copy.57
  110.5 0.6 pad_maximum_fusion.4
  111.0 0.5 copy.59
  111.5 0.2 broadcast_in_dim.29
  111.7 0.2 broadcast_in_dim.35
  111.8 1.7 pad_maximum_fusion
  113.6 11.0 %all-to-all-start.2 = ((bf16[16,648,128]{2,1,0:T(8,128)(2,1)}), bf16[16,648,128]{2,1,0:T(8,128)(2,1)S(1)}, u32[]{:S(2)}, u32[]{:S(2)}) async-start(bf16[16,648,128]{2,1,0:T(8,128)(2,1)} %pad_maximum_fusion), calls=%async_computation.2 | async-start | bytes 5308416 | tf_op jit(solution)/shard_map/all_to_all | solution.py:193
  124.6 0.2 reduce-scatter.2.cloned.1.call-start
  124.8 0.6 dynamic_slice.16
  125.4 0.7 fusion.54
  126.1 84.1 %all-to-all-done.2 = bf16[16,648,128]{2,1,0:T(8,128)(2,1)S(1)} async-done(((bf16[16,648,128]{2,1,0:T(8,128)(2,1)}), bf16[16,648,128]{2,1,0:T(8,128)(2,1)S(1)}, u32[]{:S(2)}, u32[]{:S(2)}) %all-to-all-start.2) | async-done | bytes 2654240 | tf_op jit(solution)/shard_map/all_to_all | solution.py:193
  210.3 0.2 fusion.66
  210.4 3.5 fusion.67
  213.9 4.2 %fusion.1 = f32[1152]{0:T(1024)S(1)} fusion(f32[1152,4608]{1,0:T(8,128)S(1)} %get-tuple-element.35, f32[1152]{0:T(1024)S(1)} %get-tuple-element.34), kind=kLoop, calls=%fused_computation.3 | loop fusion | flops 10615680 | bytes 21242880 | tf_op jit(solution)/shard_map/reduce_sum | solution.py:210
  218.1 3.2 copy-done.2
  221.4 10.5 %fusion.13 = bf16[1152,128]{1,0:T(8,128)(2,1)S(1)} fusion(bf16[4608,128]{1,0:T(8,128)(2,1)S(1)} %bitcast.102, f32[1152,4608]{1,0:T(8,128)} %copy-done.2, f32[1152]{0:T(1024)S(1)} %get-tuple-element.34, f32[1152]{0:T(1024)S(1)} %fusion.1), kind=kOutput, calls=%fused_computation.15 | convolution fusion | flops 1369866240 | bytes 22717440 | tf_op jit(solution)/shard_map/dot_general | solution.py:211
  231.9 46.1 %all_to_all.20 = bf16[16,72,128]{2,1,0:T(8,128)(2,1)S(1)} all-to-all(bf16[16,72,128]{2,1,0:T(8,128)(2,1)S(1)} %bitcast.111), channel_id=1, replica_groups=mesh['cfg'=2,'seq'=16,'wblk'=8] {'seq'}, dimensions={0} | all-to-all | bytes 589824 | tf_op jit(solution)/shard_map/all_to_all | solution.py:215
  277.9 0.2 copy.60
  278.2 11.6 %all-gather.5.cloned.1.call-done = bf16[3072,1792]{1,0:T(8,128)(2,1)} async-done(((bf16[192,1792]{1,0:T(8,128)(2,1)}), bf16[3072,1792]{1,0:T(8,128)(2,1)}) %all-gather.5.cloned.1.call-update) | async-done | bytes 11010064 | tf_op jit(solution)/shard_map/all_gather | solution.py:148
  289.8 2.3 slice-done
  292.1 5.2 %fusion.23 = bf16[576,768]{1,0:T(8,128)(2,1)S(1)} fusion(bf16[8,576,384]{2,1,0:T(8,128)(2,1)} %all-to-all-done.1, bf16[8,384,768]{2,1,0:T(8,128)(2,1)S(1)} %bitcast.100), kind=kOutput, calls=%fused_computation.23 | convolution fusion | flops 2721890304 | bytes 9142272 | tf_op jit(solution)/shard_map/wrf,wfn->rn/dot_general | solution.py:156
  297.3 2.8 slice-done.1
  300.1 5.3 %convert_bitcast_fusion = bf16[8,576,384]{2,1,0:T(8,128)(2,1)} fusion(bf16[8,384,1024]{2,1,0:T(8,128)(2,1)S(1)} %bitcast.101, bf16[576,768]{1,0:T(8,128)(2,1)S(1)} %fusion.23, bf16[576,256]{1,0:T(8,128)(2,1)S(1)} %bitcast.123), kind=kOutput, calls=%fused_computation.11 | convolution fusion | flops 3628007424 | bytes 11010048 | tf_op jit(solution)/shard_map/bjk,rk->brj/dot_general | solution.py:219
  305.5 40.3 %reduce-scatter.2.cloned.1.call-done = bf16[1,576,384]{2,1,0:T(8,128)(2,1)} async-done(((bf16[8,576,384]{2,1,0:T(8,128)(2,1)}), bf16[1,576,384]{2,1,0:T(8,128)(2,1)}) %reduce-scatter.2.cloned.1.call-update) | async-done | bytes 442384 | tf_op jit(solution)/shard_map/reduce_scatter | solution.py:225
  345.8 1.2 fusion.32
  347.0 1.7 collective-permute-start
  348.8 0.6 slice_bitcast_fusion
  349.4 3.4 collective-permute-done
  352.8 1.0 multiply_add_fusion
  (42 shorter events, 0.4 us)
Async XLA Ops:
  7.2 3.5 copy-start
  7.2 85.0 %all-gather.3.cloned.1.call-start = ((), (), s32[]{:S(2)}) async-start(), calls=%async_computation.5 | async-start | bytes 5013504 | tf_op jit(solution)/shard_map/all_gather | solution.py:137
  11.5 27.8 %all-to-all-start = ((f32[16,3,384]{2,1,0:T(4,128)}), f32[16,3,384]{2,1,0:T(4,128)S(1)}, u32[]{:S(2)}, u32[]{:S(2)}) async-start(f32[16,3,384]{2,1,0:T(4,128)} %broadcast_in_dim.24), calls=%async_computation | async-start | bytes 196608 | tf_op jit(solution)/shard_map/all_to_all | solution.py:124
  42.7 4.7 %copy-start.5 = (bf16[768,192]{0,1:T(8,128)(2,1)S(1)}, bf16[768,192]{0,1:T(8,128)(2,1)}, u32[]{:S(2)}) copy-start(bf16[768,192]{0,1:T(8,128)(2,1)} %param.21) | copy-start | bytes 884740
  42.7 4.7 %copy-start.7 = (bf16[256,192]{0,1:T(8,128)(2,1)S(1)}, bf16[256,192]{0,1:T(8,128)(2,1)}, u32[]{:S(2)}) copy-start(bf16[256,192]{0,1:T(8,128)(2,1)} %param.20) | copy-start | bytes 294916
  42.7 4.8 %copy-start.6 = (bf16[192,768]{1,0:T(8,128)(2,1)S(1)}, bf16[192,768]{1,0:T(8,128)(2,1)}, u32[]{:S(2)}) copy-start(bf16[192,768]{1,0:T(8,128)(2,1)} %param.17) | copy-start | bytes 884740
  42.7 47.3 %copy-start.8 = (f32[128]{0:T(128)S(1)}, f32[128]{0:T(128)}, u32[]{:S(2)}) copy-start(f32[128]{0:T(128)} %param.18) | copy-start | bytes 1540
  42.7 47.5 %copy-start.9 = (f32[128]{0:T(128)S(1)}, f32[128]{0:T(128)}, u32[]{:S(2)}) copy-start(f32[128]{0:T(128)} %param.19) | copy-start | bytes 1540
  42.7 47.3 %all-to-all-start.1 = ((bf16[8,576,384]{2,1,0:T(8,128)(2,1)}), bf16[8,576,384]{2,1,0:T(8,128)(2,1)}, u32[]{:S(2)}, u32[]{:S(2)}) async-start(bf16[8,576,384]{2,1,0:T(8,128)(2,1)} %broadcast_in_dim.26), calls=%async_computation.1 | async-start | bytes 7077888 | tf_op jit(solution)/shard_map/all_to_all | solution.py:142
  47.4 242.4 %all-gather.5.cloned.1.call-start = ((), (), s32[]{:S(2)}) async-start(), calls=%async_computation.6 | async-start | bytes 11698176 | tf_op jit(solution)/shard_map/all_gather | solution.py:148
  113.6 11.3 %copy-start.10 = (s32[2]{0:T(128)S(1)}, s32[2]{0:T(128)}, u32[]{:S(2)}) copy-start(s32[2]{0:T(128)} %param.22) | copy-start | bytes 28
  113.6 96.7 %all-to-all-start.2 = ((bf16[16,648,128]{2,1,0:T(8,128)(2,1)}), bf16[16,648,128]{2,1,0:T(8,128)(2,1)S(1)}, u32[]{:S(2)}, u32[]{:S(2)}) async-start(bf16[16,648,128]{2,1,0:T(8,128)(2,1)} %pad_maximum_fusion), calls=%async_computation.2 | async-start | bytes 5308416 | tf_op jit(solution)/shard_map/all_to_all | solution.py:193
  124.6 221.2 %reduce-scatter.2.cloned.1.call-start = ((), (), s32[]{:S(2)}) async-start(), calls=%async_computation.7 | async-start | bytes 3981312 | tf_op jit(solution)/shard_map/reduce_scatter | solution.py:225
  213.9 7.5 %copy-start.2 = (f32[1152,4608]{1,0:T(8,128)}, f32[1152,4608]{1,0:T(8,128)S(1)}, u32[]{:S(2)}) copy-start(f32[1152,4608]{1,0:T(8,128)S(1)} %get-tuple-element.35) | copy-start | bytes 63700996
  289.8 2.3 slice-start
  297.3 2.8 slice-start.1
  305.4 40.4 %copy-start.3 = (bf16[2,256,384]{2,1,0:T(8,128)(2,1)S(1)}, bf16[2,256,384]{2,1,0:T(8,128)(2,1)}, u32[]{:S(2)}) copy-start(bf16[2,256,384]{2,1,0:T(8,128)(2,1)} %param.13) | copy-start | bytes 1179652
  305.4 40.4 %copy-start.4 = (bf16[1,2,32,384]{3,2,1,0:T(8,128)(2,1)S(1)}, bf16[1,2,32,384]{3,2,1,0:T(8,128)(2,1)}, u32[]{:S(2)}) copy-start(bf16[1,2,32,384]{3,2,1,0:T(8,128)(2,1)} %param.12) | copy-start | bytes 147460
  305.4 48.4 %copy-start.1 = (bf16[192,3,384]{2,0,1:T(8,128)(2,1)S(1)}, bf16[192,3,384]{2,0,1:T(8,128)(2,1)}, u32[]{:S(2)}) copy-start(bf16[192,3,384]{2,0,1:T(8,128)(2,1)} %param.15) | copy-start | bytes 1327108
  347.0 5.8 %collective-permute-start = (bf16[1,256,384]{2,1,0:T(8,128)(2,1)S(1)}, bf16[1,256,384]{2,1,0:T(8,128)(2,1)S(1)}, u32[]{:S(2)}, u32[]{:S(2)}) collective-permute-start(bf16[1,256,384]{2,1,0:T(8,128)(2,1)S(1)} %constant_dynamic-slice_fusion), channel_id=1, source_target_pairs={{0,128},{128,0},{1,129},{129,1},{2,130},{130,2},{3,131},{131,3},{4... | collective-permute-start | bytes 589832 | tf_op jit(solution)/shard_map/ppermute | solution.py:236
Sparse Core Ops, SparseCore 0:
  11.0 81.1 all-gather.2
  94.6 195.1 all-gather.4
  305.6 40.1 reduce-scatter.1

commit v9 on v8

--- a/solution.py
+++ b/solution.py
@@ -146,7 +146,9 @@
     )
     tail_source, gathered = lax.optimization_barrier((tail_source, gathered))
     tail_full = lax.all_gather(tail_source, "seq", axis=0, tiled=True)
-    up_full = tail_full[:, :up_cols]
+    up_full, out_weight_t = lax.optimization_barrier(
+        (tail_full[:, :up_cols], tail_full[:, up_cols:])
+    )
     projected = jnp.einsum(
         "wrf,wfn->rn",
         gathered,
@@ -218,7 +220,7 @@
     activated = jax.nn.gelu(mlp_units, approximate=True).astype(jnp.bfloat16)
     block_terms = jnp.einsum(
         "bjk,rk->brj",
-        tail_full[:, up_cols:].reshape(wblk_count, dim_local, -1),
+        out_weight_t.reshape(wblk_count, dim_local, -1),
         jnp.concatenate([attended, activated], axis=1),
         preferred_element_type=jnp.float32,
     )

time: 361 us -> 358 us (level)
  no operation moved by 1% of the time
where the time goes in v9:
time: 358 us
  waiting for transfers between devices  182 us (51%)
  blocking collectives  60.9 us (17%)
  matrix products  31.7 us (9%)
  starting transfers between devices  29.2 us (8%)
  local copies, waits for them, and re-layouts  22 us (6%)
  other arithmetic  16.9 us (5%)
  between operations  14.9 us (4%)
    all_to_all x1, waiting for transfers between devices, shards(): received = lax.all_to_all(send, 'seq', 0, 0, tiled=True)  84.1 us
    all_to_all x1, blocking collectives, shards(): returned = lax.all_to_all(mixed, 'seq', 0, 0, tiled=True)  46.1 us
    all_to_all x1, waiting for transfers between devices, shards(): gathered = lax.all_to_all(spread, 'wblk', 0, 0, tiled=True)  41.6 us
    reduce_scatter x1, waiting for transfers between devices, shards(): lax.psum_scatter(block_terms.astype(jnp.bfloat16), 'wblk', scatter_dimens...  40.3 us
    psum x1, blocking collectives, shards(): lax.psum((jnp.sum(hidden, axis=-1), jnp.sum(hidden * hidden, axis=-1)), '...  14.8 us
    all_gather x1, waiting for transfers between devices, shards(): tail_full = lax.all_gather(tail_source, 'seq', axis=0, tiled=True)  11.6 us
    all_to_all x1, starting transfers between devices, shards(): lax.all_to_all(mod_spread, 'seq', 0, 0, tiled=True)  11.5 us
    all_to_all x1, starting transfers between devices, shards(): received = lax.all_to_all(send, 'seq', 0, 0, tiled=True)  11 us
  transfers between devices with their start and end apart: 7, of which 6 were waited for; matrix products, arithmetic and copies ran while one was open for 14% of the time, Pallas kernels for 0%

profile of v9, /device:TPU:2, one launch (start us, length us, event | category | flops | bytes accessed | tf_op | source)
XLA Modules:
  0.0 357.7 jit_solution(6790954558333753336)
XLA Ops:
  7.2 0.0 all-gather.3.cloned.1.call-start
  7.2 1.9 reshape.279
  9.1 0.0 all-gather.3.cloned.1.call-update
  9.8 0.1 fusion.55
  9.9 0.8 fusion.63
  10.7 0.2 fusion.37
  10.9 0.7 broadcast_in_dim.24
  11.5 11.5 %all-to-all-start = ((f32[16,3,384]{2,1,0:T(4,128)}), f32[16,3,384]{2,1,0:T(4,128)S(1)}, u32[]{:S(2)}, u32[]{:S(2)}) async-start(f32[16,3,384]{2,1,0:T(4,128)} %broadcast_in_dim.24), calls=%async_computation | async-start | bytes 196608 | tf_op jit(solution)/shard_map/all_to_all | solution.py:124
  23.0 1.3 convert_reduce_fusion
  24.3 14.8 %all-reduce.2 = (f32[2,288]{1,0:T(2,128)S(1)}, f32[2,288]{1,0:T(2,128)S(1)}) all-reduce(f32[2,288]{1,0:T(2,128)S(1)} %get-tuple-element.14, f32[2,288]{1,0:T(2,128)S(1)} %get-tuple-element.13), channel_id=1, replica_groups=mesh['cfg'=2,'seq'=16,'wblk'=8] {'wblk'}, use_global_device_ids=true, to_apply=%region_4.5 | all-reduce | flops 1152 | bytes 9216 | tf_op jit(solution)/shard_map/psum | solution.py:127
  39.2 0.1 mul.288
  39.2 0.1 sub.76
  39.4 1.2 fusion.36
  40.6 2.1 broadcast_in_dim.26
  42.7 4.7 %all-to-all-start.1 = ((bf16[8,576,384]{2,1,0:T(8,128)(2,1)}), bf16[8,576,384]{2,1,0:T(8,128)(2,1)}, u32[]{:S(2)}, u32[]{:S(2)}) async-start(bf16[8,576,384]{2,1,0:T(8,128)(2,1)} %broadcast_in_dim.26), calls=%async_computation.1 | async-start | bytes 7077888 | tf_op jit(solution)/shard_map/all_to_all | solution.py:142
  47.4 0.0 all-gather.5.cloned.1.call-start
  47.5 0.9 pad_maximum_fusion.1
  48.4 41.6 %all-to-all-done.1 = bf16[8,576,384]{2,1,0:T(8,128)(2,1)} async-done(((bf16[8,576,384]{2,1,0:T(8,128)(2,1)}), bf16[8,576,384]{2,1,0:T(8,128)(2,1)}, u32[]{:S(2)}, u32[]{:S(2)}) %all-to-all-start.1) | async-done | bytes 3538976 | tf_op jit(solution)/shard_map/all_to_all | solution.py:142
  90.0 0.0 all-gather.5.cloned.1.call-update
  90.0 0.1 mul.315
  90.2 0.1 mul.296
  90.3 0.1 concatenate.39
  90.4 0.1 concatenate.40
  90.5 0.1 broadcast_multiply_fusion.1
  90.6 0.4 fusion.44
  91.0 1.2 all-gather.3.cloned.1.call-done
  92.2 7.1 %copy.67 = bf16[8,384,768]{1,0,2:T(8,128)(2,1)} copy(bf16[8,384,768]{2,1,0:T(8,128)(2,1)} %bitcast.104) | data formatting | bytes 9437184 | tf_op jit(solution)/shard_map/reshape | solution.py:155
  99.3 6.9 %fusion.24 = f32[2,288,3,2,128]{4,1,3,2,0:T(8,128)S(1)} fusion(bf16[3,2,128,384,8]{3,4,2,1,0:T(8,128)(2,1)} %bitcast.105, bf16[2,288,384,8,1,1]{2,1,0,3,5,4:T(8,128)(2,1)} %bitcast.10), kind=kOutput, calls=%fused_computation.24 | convolution fusion | flops 2717908992 | bytes 10027008 | tf_op jit(solution)/shard_map/wrf,wfn->rn/dot_general | solution.py:152
  106.3 0.5 multiply_reduce_fusion.2
  106.8 0.5 copy.58
  107.3 0.5 copy.56
  107.8 0.4 multiply_multiply_fusion.1
  108.2 0.4 multiply_multiply_fusion.2
  108.6 0.8 subtract_convert_fusion.1
  109.4 0.6 pad_maximum_fusion.3
  110.0 0.5 copy.57
  110.5 0.6 pad_maximum_fusion.4
  111.0 0.5 copy.59
  111.5 0.2 broadcast_in_dim.29
  111.7 0.2 broadcast_in_dim.35
  111.8 1.7 pad_maximum_fusion
  113.6 11.0 %all-to-all-start.2 = ((bf16[16,648,128]{2,1,0:T(8,128)(2,1)}), bf16[16,648,128]{2,1,0:T(8,128)(2,1)S(1)}, u32[]{:S(2)}, u32[]{:S(2)}) async-start(bf16[16,648,128]{2,1,0:T(8,128)(2,1)} %pad_maximum_fusion), calls=%async_computation.2 | async-start | bytes 5308416 | tf_op jit(solution)/shard_map/all_to_all | solution.py:195
  124.6 0.2 reduce-scatter.2.cloned.1.call-start
  124.8 0.6 dynamic_slice.16
  125.4 0.7 fusion.54
  126.1 84.1 %all-to-all-done.2 = bf16[16,648,128]{2,1,0:T(8,128)(2,1)S(1)} async-done(((bf16[16,648,128]{2,1,0:T(8,128)(2,1)}), bf16[16,648,128]{2,1,0:T(8,128)(2,1)S(1)}, u32[]{:S(2)}, u32[]{:S(2)}) %all-to-all-start.2) | async-done | bytes 2654240 | tf_op jit(solution)/shard_map/all_to_all | solution.py:195
  210.3 0.2 fusion.66
  210.4 3.5 fusion.67
  213.9 4.2 %fusion.1 = f32[1152]{0:T(1024)S(1)} fusion(f32[1152,4608]{1,0:T(8,128)S(1)} %get-tuple-element.39, f32[1152]{0:T(1024)S(1)} %get-tuple-element.38), kind=kLoop, calls=%fused_computation.3 | loop fusion | flops 10615680 | bytes 21242880 | tf_op jit(solution)/shard_map/reduce_sum | solution.py:212
  218.1 3.2 copy-done.2
  221.4 10.5 %fusion.13 = bf16[1152,128]{1,0:T(8,128)(2,1)S(1)} fusion(bf16[4608,128]{1,0:T(8,128)(2,1)S(1)} %bitcast.102, f32[1152,4608]{1,0:T(8,128)} %copy-done.2, f32[1152]{0:T(1024)S(1)} %get-tuple-element.38, f32[1152]{0:T(1024)S(1)} %fusion.1), kind=kOutput, calls=%fused_computation.15 | convolution fusion | flops 1369866240 | bytes 22717440 | tf_op jit(solution)/shard_map/dot_general | solution.py:213
  231.9 46.1 %all_to_all.20 = bf16[16,72,128]{2,1,0:T(8,128)(2,1)S(1)} all-to-all(bf16[16,72,128]{2,1,0:T(8,128)(2,1)S(1)} %bitcast.111), channel_id=1, replica_groups=mesh['cfg'=2,'seq'=16,'wblk'=8] {'seq'}, dimensions={0} | all-to-all | bytes 589824 | tf_op jit(solution)/shard_map/all_to_all | solution.py:217
  277.9 0.2 copy.60
  278.2 11.6 %all-gather.5.cloned.1.call-done = bf16[3072,1792]{1,0:T(8,128)(2,1)} async-done(((bf16[192,1792]{1,0:T(8,128)(2,1)}), bf16[3072,1792]{1,0:T(8,128)(2,1)}) %all-gather.5.cloned.1.call-update) | async-done | bytes 11010064 | tf_op jit(solution)/shard_map/all_gather | solution.py:148
  289.8 2.3 slice-done.1
  292.1 5.3 %fusion.23 = bf16[576,768]{1,0:T(8,128)(2,1)S(1)} fusion(bf16[8,576,384]{2,1,0:T(8,128)(2,1)} %all-to-all-done.1, bf16[8,384,768]{2,1,0:T(8,128)(2,1)S(1)} %bitcast.101), kind=kOutput, calls=%fused_computation.23 | convolution fusion | flops 2721890304 | bytes 9142272 | tf_op jit(solution)/shard_map/wrf,wfn->rn/dot_general | solution.py:158
  297.4 5.4 %convert_bitcast_fusion = bf16[8,576,384]{2,1,0:T(8,128)(2,1)} fusion(bf16[8,384,1024]{2,1,0:T(8,128)(2,1)S(1)} %bitcast.100, bf16[576,768]{1,0:T(8,128)(2,1)S(1)} %fusion.23, bf16[576,256]{1,0:T(8,128)(2,1)S(1)} %bitcast.123), kind=kOutput, calls=%fused_computation.11 | convolution fusion | flops 3628007424 | bytes 11010048 | tf_op jit(solution)/shard_map/bjk,rk->brj/dot_general | solution.py:221
  302.8 0.0 reduce-scatter.2.cloned.1.call-update
  302.9 40.3 %reduce-scatter.2.cloned.1.call-done = bf16[1,576,384]{2,1,0:T(8,128)(2,1)} async-done(((bf16[8,576,384]{2,1,0:T(8,128)(2,1)}), bf16[1,576,384]{2,1,0:T(8,128)(2,1)}) %reduce-scatter.2.cloned.1.call-update) | async-done | bytes 442384 | tf_op jit(solution)/shard_map/reduce_scatter | solution.py:227
  343.2 1.2 fusion.32
  344.4 1.7 collective-permute-start
  346.1 0.6 slice_bitcast_fusion
  346.8 3.4 collective-permute-done
  350.2 1.0 multiply_add_fusion
  (42 shorter events, 0.4 us)
Async XLA Ops:
  7.2 3.5 copy-start
  7.2 85.0 %all-gather.3.cloned.1.call-start = ((), (), s32[]{:S(2)}) async-start(), calls=%async_computation.5 | async-start | bytes 5013504 | tf_op jit(solution)/shard_map/all_gather | solution.py:137
  11.5 27.8 %all-to-all-start = ((f32[16,3,384]{2,1,0:T(4,128)}), f32[16,3,384]{2,1,0:T(4,128)S(1)}, u32[]{:S(2)}, u32[]{:S(2)}) async-start(f32[16,3,384]{2,1,0:T(4,128)} %broadcast_in_dim.24), calls=%async_computation | async-start | bytes 196608 | tf_op jit(solution)/shard_map/all_to_all | solution.py:124
  42.7 4.7 %copy-start.5 = (bf16[768,192]{0,1:T(8,128)(2,1)S(1)}, bf16[768,192]{0,1:T(8,128)(2,1)}, u32[]{:S(2)}) copy-start(bf16[768,192]{0,1:T(8,128)(2,1)} %param.21) | copy-start | bytes 884740
  42.7 4.7 %copy-start.7 = (bf16[256,192]{0,1:T(8,128)(2,1)S(1)}, bf16[256,192]{0,1:T(8,128)(2,1)}, u32[]{:S(2)}) copy-start(bf16[256,192]{0,1:T(8,128)(2,1)} %param.20) | copy-start | bytes 294916
  42.7 4.8 %copy-start.6 = (bf16[192,768]{1,0:T(8,128)(2,1)S(1)}, bf16[192,768]{1,0:T(8,128)(2,1)}, u32[]{:S(2)}) copy-start(bf16[192,768]{1,0:T(8,128)(2,1)} %param.17) | copy-start | bytes 884740
  42.7 47.3 %copy-start.8 = (f32[128]{0:T(128)S(1)}, f32[128]{0:T(128)}, u32[]{:S(2)}) copy-start(f32[128]{0:T(128)} %param.18) | copy-start | bytes 1540
  42.7 47.5 %copy-start.9 = (f32[128]{0:T(128)S(1)}, f32[128]{0:T(128)}, u32[]{:S(2)}) copy-start(f32[128]{0:T(128)} %param.19) | copy-start | bytes 1540
  42.7 47.3 %all-to-all-start.1 = ((bf16[8,576,384]{2,1,0:T(8,128)(2,1)}), bf16[8,576,384]{2,1,0:T(8,128)(2,1)}, u32[]{:S(2)}, u32[]{:S(2)}) async-start(bf16[8,576,384]{2,1,0:T(8,128)(2,1)} %broadcast_in_dim.26), calls=%async_computation.1 | async-start | bytes 7077888 | tf_op jit(solution)/shard_map/all_to_all | solution.py:142
  47.4 242.4 %all-gather.5.cloned.1.call-start = ((), (), s32[]{:S(2)}) async-start(), calls=%async_computation.6 | async-start | bytes 11698176 | tf_op jit(solution)/shard_map/all_gather | solution.py:148
  113.6 11.3 %copy-start.10 = (s32[2]{0:T(128)S(1)}, s32[2]{0:T(128)}, u32[]{:S(2)}) copy-start(s32[2]{0:T(128)} %param.22) | copy-start | bytes 28
  113.6 96.7 %all-to-all-start.2 = ((bf16[16,648,128]{2,1,0:T(8,128)(2,1)}), bf16[16,648,128]{2,1,0:T(8,128)(2,1)S(1)}, u32[]{:S(2)}, u32[]{:S(2)}) async-start(bf16[16,648,128]{2,1,0:T(8,128)(2,1)} %pad_maximum_fusion), calls=%async_computation.2 | async-start | bytes 5308416 | tf_op jit(solution)/shard_map/all_to_all | solution.py:195
  124.6 218.6 %reduce-scatter.2.cloned.1.call-start = ((), (), s32[]{:S(2)}) async-start(), calls=%async_computation.7 | async-start | bytes 3981312 | tf_op jit(solution)/shard_map/reduce_scatter | solution.py:227
  213.9 7.5 %copy-start.2 = (f32[1152,4608]{1,0:T(8,128)}, f32[1152,4608]{1,0:T(8,128)S(1)}, u32[]{:S(2)}) copy-start(f32[1152,4608]{1,0:T(8,128)S(1)} %get-tuple-element.39) | copy-start | bytes 63700996
  289.8 2.3 slice-start.1
  292.1 5.3 %slice-start = ((bf16[3072,1792]{1,0:T(8,128)(2,1)}), bf16[3072,1024]{1,0:T(8,128)(2,1)S(1)}, s32[]{:S(2)}) async-start(bf16[3072,1792]{1,0:T(8,128)(2,1)} %all-gather.5.cloned.1.call-done), calls=%async_computation.8 | async-start | bytes 12582912 | tf_op jit(solution)/shard_map/slice | solution.py:150
  302.8 40.4 %copy-start.3 = (bf16[2,256,384]{2,1,0:T(8,128)(2,1)S(1)}, bf16[2,256,384]{2,1,0:T(8,128)(2,1)}, u32[]{:S(2)}) copy-start(bf16[2,256,384]{2,1,0:T(8,128)(2,1)} %param.13) | copy-start | bytes 1179652
  302.8 40.4 %copy-start.4 = (bf16[1,2,32,384]{3,2,1,0:T(8,128)(2,1)S(1)}, bf16[1,2,32,384]{3,2,1,0:T(8,128)(2,1)}, u32[]{:S(2)}) copy-start(bf16[1,2,32,384]{3,2,1,0:T(8,128)(2,1)} %param.12) | copy-start | bytes 147460
  302.8 48.4 %copy-start.1 = (bf16[192,3,384]{2,0,1:T(8,128)(2,1)S(1)}, bf16[192,3,384]{2,0,1:T(8,128)(2,1)}, u32[]{:S(2)}) copy-start(bf16[192,3,384]{2,0,1:T(8,128)(2,1)} %param.15) | copy-start | bytes 1327108
  344.4 5.8 %collective-permute-start = (bf16[1,256,384]{2,1,0:T(8,128)(2,1)S(1)}, bf16[1,256,384]{2,1,0:T(8,128)(2,1)S(1)}, u32[]{:S(2)}, u32[]{:S(2)}) collective-permute-start(bf16[1,256,384]{2,1,0:T(8,128)(2,1)S(1)} %constant_dynamic-slice_fusion), channel_id=1, source_target_pairs={{0,128},{128,0},{1,129},{129,1},{2,130},{130,2},{3,131},{131,3},{4... | collective-permute-start | bytes 589832 | tf_op jit(solution)/shard_map/ppermute | solution.py:238
Sparse Core Ops, SparseCore 0:
  11.0 81.1 all-gather.2
  94.6 195.1 all-gather.4
  302.9 40.1 reduce-scatter.1

commit v10 on v9

--- a/solution.py
+++ b/solution.py
@@ -138,8 +138,8 @@
         qkv_weight.reshape(width_rows, qkv_cols), "seq", axis=0, tiled=True
     )
     wblk_count = lax.psum(1, "wblk")
-    spread = jnp.broadcast_to(normed.reshape(1, row_count, dim_local), (wblk_count, row_count, dim_local))
-    gathered = lax.all_to_all(spread, "wblk", 0, 0, tiled=True)
+    spread = jnp.broadcast_to(normed.reshape(row_count, 1, dim_local), (row_count, wblk_count, dim_local))
+    gathered = lax.all_to_all(spread, "wblk", 1, 1, tiled=True).reshape(row_count, D)
     up_cols = up_weight.shape[1]
     tail_source = jnp.concatenate(
         [up_weight, jnp.concatenate([attn_weight, down_weight], axis=0).T], axis=1
@@ -150,15 +150,15 @@
         (tail_full[:, :up_cols], tail_full[:, up_cols:])
     )
     projected = jnp.einsum(
-        "wrf,wfn->rn",
+        "rk,kn->rn",
         gathered,
-        qkv_full.reshape(wblk_count, dim_local, -1),
+        qkv_full,
         preferred_element_type=jnp.float32,
     )
     mlp_units = jnp.einsum(
-        "wrf,wfn->rn",
+        "rk,kn->rn",
         gathered,
-        up_full.reshape(wblk_count, dim_local, -1),
+        up_full,
         preferred_element_type=jnp.float32,
     )
     projected = projected.reshape(prompts, local_len, 3, heads_local, HD)

time: 358 us -> 357 us (level)
  blocking collectives: 60.9 us -> 43 us
  waiting for transfers between devices: 182 us -> 198 us
    all_gather x1, waiting for transfers between devices: 11.6 us -> 31 us  [shards(): tail_full = lax.all_gather(tail_source, 'seq', axis=0, tiled=True)]
    all_to_all x1, blocking collectives: 46.1 us -> 28.2 us  [shards(): returned = lax.all_to_all(mixed, 'seq', 0, 0, tiled=True)]
  transfers between devices with their start and end apart: 7 -> 7, of which waited for: 6 -> 5; matrix products, arithmetic and copies ran while one was open for 14% -> 15% of each run, Pallas kernels for 0% -> 0%
where the time goes in v10:
time: 357 us; the launch traced here: 356 us
  waiting for transfers between devices  198 us (55%)
  blocking collectives  43 us (12%)
  matrix products  30.3 us (8%)
  starting transfers between devices  28 us (8%)
  local copies, waits for them, and re-layouts  25 us (7%)
  other arithmetic  16.8 us (5%)
  between operations  14.9 us (4%)
    all_to_all x1, waiting for transfers between devices, shards(): received = lax.all_to_all(send, 'seq', 0, 0, tiled=True)  82.2 us
    all_to_all x1, waiting for transfers between devices, shards(): lax.all_to_all(spread, 'wblk', 1, 1, tiled=True).reshape(row_count, D)  41.6 us
    reduce_scatter x1, waiting for transfers between devices, shards(): lax.psum_scatter(block_terms.astype(jnp.bfloat16), 'wblk', scatter_dimens...  40 us
    all_gather x1, waiting for transfers between devices, shards(): tail_full = lax.all_gather(tail_source, 'seq', axis=0, tiled=True)  31 us
    all_to_all x1, blocking collectives, shards(): returned = lax.all_to_all(mixed, 'seq', 0, 0, tiled=True)  28.2 us
    psum x1, blocking collectives, shards(): lax.psum((jnp.sum(hidden, axis=-1), jnp.sum(hidden * hidden, axis=-1)), '...  14.8 us
    all_to_all x1, starting transfers between devices, shards(): lax.all_to_all(mod_spread, 'seq', 0, 0, tiled=True)  11.5 us
    dot_general x1, matrix products, shards(): jnp.dot(weights.astype(jnp.bfloat16), value_piece, preferred_element_type...  10.6 us
  transfers between devices with their start and end apart: 7, of which 5 were waited for; matrix products, arithmetic and copies ran while one was open for 15% of the time, Pallas kernels for 0%

profile of v10, /device:TPU:2, one launch (start us, length us, event | category | flops | bytes accessed | tf_op | source)
XLA Modules:
  0.0 356.4 jit_solution(5952095517683835310)
XLA Ops:
  7.2 1.9 reshape.270
  9.8 0.1 fusion.46
  9.9 0.8 fusion.54
  10.7 0.2 fusion.28
  10.9 0.7 broadcast_in_dim.24
  11.6 11.5 %all-to-all-start = ((f32[16,3,384]{2,1,0:T(4,128)}), f32[16,3,384]{2,1,0:T(4,128)S(1)}, u32[]{:S(2)}, u32[]{:S(2)}) async-start(f32[16,3,384]{2,1,0:T(4,128)} %broadcast_in_dim.24), calls=%async_computation | async-start | bytes 196608 | tf_op jit(solution)/shard_map/all_to_all | solution.py:124
  23.0 1.3 convert_reduce_fusion
  24.3 14.8 %all-reduce.2 = (f32[2,288]{1,0:T(2,128)S(1)}, f32[2,288]{1,0:T(2,128)S(1)}) all-reduce(f32[2,288]{1,0:T(2,128)S(1)} %get-tuple-element.12, f32[2,288]{1,0:T(2,128)S(1)} %get-tuple-element.11), channel_id=1, replica_groups=mesh['cfg'=2,'seq'=16,'wblk'=8] {'wblk'}, use_global_device_ids=true, to_apply=%region_4.5 | all-reduce | flops 1152 | bytes 9216 | tf_op jit(solution)/shard_map/psum | solution.py:127
  39.2 0.1 mul.288
  39.3 0.1 sub.76
  39.4 1.0 fusion.27
  40.5 2.1 broadcast_in_dim.26
  42.6 4.6 %all-to-all-start.1 = ((bf16[576,8,384]{2,0,1:T(8,128)(2,1)}), bf16[576,8,384]{2,0,1:T(8,128)(2,1)}, u32[]{:S(2)}, u32[]{:S(2)}) async-start(bf16[576,8,384]{2,0,1:T(8,128)(2,1)} %broadcast_in_dim.26), calls=%async_computation.1 | async-start | bytes 7077888 | tf_op jit(solution)/shard_map/all_to_all | solution.py:142
  47.2 0.0 all-gather.5.cloned.1.call-start
  47.4 0.9 pad_maximum_fusion.1
  48.3 41.6 %all-to-all-done.1 = bf16[576,8,384]{2,0,1:T(8,128)(2,1)} async-done(((bf16[576,8,384]{2,0,1:T(8,128)(2,1)}), bf16[576,8,384]{2,0,1:T(8,128)(2,1)}, u32[]{:S(2)}, u32[]{:S(2)}) %all-to-all-start.1) | async-done | bytes 3538976 | tf_op jit(solution)/shard_map/all_to_all | solution.py:142
  89.9 4.4 %copy.66 = bf16[8,72,8,384]{3,2,0,1:T(8,128)(2,1)} copy(bf16[8,72,8,384]{3,2,1,0:T(8,128)(2,1)} %bitcast.42) | data formatting | bytes 7077888 | tf_op jit(solution)/shard_map/reshape | solution.py:142
  94.3 0.1 mul.315
  94.5 0.1 mul.296
  94.7 0.1 concatenate.39
  94.7 0.1 concatenate.40
  94.8 0.1 broadcast_multiply_fusion.1
  94.9 0.4 fusion.35
  95.3 7.6 %fusion.60 = f32[576,768]{1,0:T(8,128)} fusion(bf16[576,3072]{1,0:T(8,128)(2,1)} %bitcast.91, bf16[3072,768]{1,0:T(8,128)(2,1)} %all-gather.3.cloned.1.call-done), kind=kOutput, calls=%fused_computation.113 | convolution fusion | flops 2717908992 | bytes 10027008 | tf_op jit(solution)/shard_map/rk,kn->rn/dot_general | solution.py:152
  102.9 2.2 reshape.271
  105.1 0.2 slice.77
  105.3 1.2 fusion.58
  106.5 1.4 copy.62
  107.9 0.5 copy.61
  108.4 0.4 multiply_reduce_fusion.1
  108.8 0.4 multiply_reduce_fusion.2
  109.2 0.4 multiply_multiply_fusion.1
  109.5 0.4 multiply_multiply_fusion.2
  109.9 0.8 subtract_convert_fusion.1
  110.7 0.6 pad_maximum_fusion.3
  111.3 0.5 copy.50
  111.8 0.6 pad_maximum_fusion.4
  112.4 0.5 copy.53
  112.9 0.2 broadcast_in_dim.29
  113.1 0.2 broadcast_in_dim.35
  113.3 1.7 pad_maximum_fusion
  115.0 10.0 %all-to-all-start.2 = ((bf16[16,648,128]{2,1,0:T(8,128)(2,1)}), bf16[16,648,128]{2,1,0:T(8,128)(2,1)S(1)}, u32[]{:S(2)}, u32[]{:S(2)}) async-start(bf16[16,648,128]{2,1,0:T(8,128)(2,1)} %pad_maximum_fusion), calls=%async_computation.2 | async-start | bytes 5308416 | tf_op jit(solution)/shard_map/all_to_all | solution.py:195
  125.0 0.2 reduce-scatter.2.cloned.1.call-start
  125.2 0.6 dynamic_slice.16
  125.8 0.7 fusion.45
  126.5 82.2 %all-to-all-done.2 = bf16[16,648,128]{2,1,0:T(8,128)(2,1)S(1)} async-done(((bf16[16,648,128]{2,1,0:T(8,128)(2,1)}), bf16[16,648,128]{2,1,0:T(8,128)(2,1)S(1)}, u32[]{:S(2)}, u32[]{:S(2)}) %all-to-all-start.2) | async-done | bytes 2654240 | tf_op jit(solution)/shard_map/all_to_all | solution.py:195
  208.7 0.2 fusion.57
  208.9 3.5 fusion.59
  212.4 4.2 %fusion.1 = f32[1152]{0:T(1024)S(1)} fusion(f32[1152,4608]{1,0:T(8,128)S(1)} %get-tuple-element.37, f32[1152]{0:T(1024)S(1)} %get-tuple-element.36), kind=kLoop, calls=%fused_computation.3 | loop fusion | flops 10615680 | bytes 21242880 | tf_op jit(solution)/shard_map/reduce_sum | solution.py:212
  216.6 3.2 copy-done.2
  219.9 10.6 %fusion.9 = bf16[1152,128]{1,0:T(8,128)(2,1)S(1)} fusion(bf16[4608,128]{1,0:T(8,128)(2,1)S(1)} %bitcast.87, f32[1152,4608]{1,0:T(8,128)} %copy-done.2, f32[1152]{0:T(1024)S(1)} %get-tuple-element.36, f32[1152]{0:T(1024)S(1)} %fusion.1), kind=kOutput, calls=%fused_computation.11 | convolution fusion | flops 1369866240 | bytes 22717440 | tf_op jit(solution)/shard_map/dot_general | solution.py:213
  230.4 28.2 %all_to_all.20 = bf16[16,72,128]{2,1,0:T(8,128)(2,1)S(1)} all-to-all(bf16[16,72,128]{2,1,0:T(8,128)(2,1)S(1)} %bitcast.94), channel_id=1, replica_groups=mesh['cfg'=2,'seq'=16,'wblk'=8] {'seq'}, dimensions={0} | all-to-all | bytes 589824 | tf_op jit(solution)/shard_map/all_to_all | solution.py:217
  258.6 0.2 copy.54
  258.9 31.0 %all-gather.5.cloned.1.call-done = bf16[3072,1792]{1,0:T(8,128)(2,1)} async-done(((bf16[192,1792]{1,0:T(8,128)(2,1)}), bf16[3072,1792]{1,0:T(8,128)(2,1)}) %all-gather.5.cloned.1.call-update) | async-done | bytes 11010064 | tf_op jit(solution)/shard_map/all_gather | solution.py:148
  289.8 2.3 slice-done.1
  292.2 1.1 copy-done.4
  293.3 3.1 fusion.19
  296.4 5.4 %convert_bitcast_fusion = bf16[8,576,384]{2,1,0:T(8,128)(2,1)} fusion(bf16[8,384,1024]{2,1,0:T(8,128)(2,1)S(1)} %bitcast.84, bf16[576,768]{1,0:T(8,128)(2,1)S(1)} %fusion.19, bf16[576,256]{1,0:T(8,128)(2,1)S(1)} %bitcast.106), kind=kOutput, calls=%fused_computation.7 | convolution fusion | flops 3628007424 | bytes 11010048 | tf_op jit(solution)/shard_map/bjk,rk->brj/dot_general | solution.py:221
  301.9 40.0 %reduce-scatter.2.cloned.1.call-done = bf16[1,576,384]{2,1,0:T(8,128)(2,1)} async-done(((bf16[8,576,384]{2,1,0:T(8,128)(2,1)}), bf16[1,576,384]{2,1,0:T(8,128)(2,1)}) %reduce-scatter.2.cloned.1.call-update) | async-done | bytes 442384 | tf_op jit(solution)/shard_map/reduce_scatter | solution.py:227
  341.9 1.1 fusion.23
  343.1 1.5 collective-permute-start
  344.7 0.6 slice_bitcast_fusion
  345.3 3.6 %collective-permute-done = bf16[1,256,384]{2,1,0:T(8,128)(2,1)S(1)} collective-permute-done((bf16[1,256,384]{2,1,0:T(8,128)(2,1)S(1)}, bf16[1,256,384]{2,1,0:T(8,128)(2,1)S(1)}, u32[]{:S(2)}, u32[]{:S(2)}) %collective-permute-start) | collective-permute-done | bytes 196640 | tf_op jit(solution)/shard_map/ppermute | solution.py:238
  348.9 1.0 multiply_add_fusion
  (48 shorter events, 0.5 us)
Async XLA Ops:
  7.2 3.5 copy-start
  7.2 32.2 %copy-start.3 = (bf16[2,256,384]{2,1,0:T(8,128)(2,1)S(1)}, bf16[2,256,384]{2,1,0:T(8,128)(2,1)}, u32[]{:S(2)}) copy-start(bf16[2,256,384]{2,1,0:T(8,128)(2,1)} %param.13) | copy-start | bytes 1179652
  7.2 88.1 %all-gather.3.cloned.1.call-start = ((), (), s32[]{:S(2)}) async-start(), calls=%async_computation.5 | async-start | bytes 5013504 | tf_op jit(solution)/shard_map/all_gather | solution.py:137
  11.6 27.8 %all-to-all-start = ((f32[16,3,384]{2,1,0:T(4,128)}), f32[16,3,384]{2,1,0:T(4,128)S(1)}, u32[]{:S(2)}, u32[]{:S(2)}) async-start(f32[16,3,384]{2,1,0:T(4,128)} %broadcast_in_dim.24), calls=%async_computation | async-start | bytes 196608 | tf_op jit(solution)/shard_map/all_to_all | solution.py:124
  42.6 4.7 %copy-start.6 = (bf16[768,192]{0,1:T(8,128)(2,1)S(1)}, bf16[768,192]{0,1:T(8,128)(2,1)}, u32[]{:S(2)}) copy-start(bf16[768,192]{0,1:T(8,128)(2,1)} %param.21) | copy-start | bytes 884740
  42.6 4.7 %copy-start.8 = (bf16[256,192]{0,1:T(8,128)(2,1)S(1)}, bf16[256,192]{0,1:T(8,128)(2,1)}, u32[]{:S(2)}) copy-start(bf16[256,192]{0,1:T(8,128)(2,1)} %param.20) | copy-start | bytes 294916
  42.6 4.8 %copy-start.7 = (bf16[192,768]{1,0:T(8,128)(2,1)S(1)}, bf16[192,768]{1,0:T(8,128)(2,1)}, u32[]{:S(2)}) copy-start(bf16[192,768]{1,0:T(8,128)(2,1)} %param.17) | copy-start | bytes 884740
  42.6 47.3 %all-to-all-start.1 = ((bf16[576,8,384]{2,0,1:T(8,128)(2,1)}), bf16[576,8,384]{2,0,1:T(8,128)(2,1)}, u32[]{:S(2)}, u32[]{:S(2)}) async-start(bf16[576,8,384]{2,0,1:T(8,128)(2,1)} %broadcast_in_dim.26), calls=%async_computation.1 | async-start | bytes 7077888 | tf_op jit(solution)/shard_map/all_to_all | solution.py:142
  47.2 242.6 %all-gather.5.cloned.1.call-start = ((), (), s32[]{:S(2)}) async-start(), calls=%async_computation.6 | async-start | bytes 11698176 | tf_op jit(solution)/shard_map/all_gather | solution.py:148
  89.9 4.5 %copy-start.9 = (f32[128]{0:T(128)S(1)}, f32[128]{0:T(128)}, u32[]{:S(2)}) copy-start(f32[128]{0:T(128)} %param.18) | copy-start | bytes 1540
  89.9 4.6 %copy-start.10 = (f32[128]{0:T(128)S(1)}, f32[128]{0:T(128)}, u32[]{:S(2)}) copy-start(f32[128]{0:T(128)} %param.19) | copy-start | bytes 1540
  115.0 10.3 %copy-start.11 = (s32[2]{0:T(128)S(1)}, s32[2]{0:T(128)}, u32[]{:S(2)}) copy-start(s32[2]{0:T(128)} %param.22) | copy-start | bytes 28
  115.0 93.7 %all-to-all-start.2 = ((bf16[16,648,128]{2,1,0:T(8,128)(2,1)}), bf16[16,648,128]{2,1,0:T(8,128)(2,1)S(1)}, u32[]{:S(2)}, u32[]{:S(2)}) async-start(bf16[16,648,128]{2,1,0:T(8,128)(2,1)} %pad_maximum_fusion), calls=%async_computation.2 | async-start | bytes 5308416 | tf_op jit(solution)/shard_map/all_to_all | solution.py:195
  125.0 216.9 %reduce-scatter.2.cloned.1.call-start = ((), (), s32[]{:S(2)}) async-start(), calls=%async_computation.7 | async-start | bytes 3981312 | tf_op jit(solution)/shard_map/reduce_scatter | solution.py:227
  212.4 7.5 %copy-start.2 = (f32[1152,4608]{1,0:T(8,128)}, f32[1152,4608]{1,0:T(8,128)S(1)}, u32[]{:S(2)}) copy-start(f32[1152,4608]{1,0:T(8,128)S(1)} %get-tuple-element.37) | copy-start | bytes 63700996
  289.8 2.3 slice-start.1
  289.8 3.5 copy-start.4
  293.3 3.1 slice-start
  301.8 40.1 %copy-start.5 = (bf16[1,2,32,384]{3,2,1,0:T(8,128)(2,1)S(1)}, bf16[1,2,32,384]{3,2,1,0:T(8,128)(2,1)}, u32[]{:S(2)}) copy-start(bf16[1,2,32,384]{3,2,1,0:T(8,128)(2,1)} %param.12) | copy-start | bytes 147460
  301.8 48.1 %copy-start.1 = (bf16[192,3,384]{2,0,1:T(8,128)(2,1)S(1)}, bf16[192,3,384]{2,0,1:T(8,128)(2,1)}, u32[]{:S(2)}) copy-start(bf16[192,3,384]{2,0,1:T(8,128)(2,1)} %param.15) | copy-start | bytes 1327108
  343.1 5.8 %collective-permute-start = (bf16[1,256,384]{2,1,0:T(8,128)(2,1)S(1)}, bf16[1,256,384]{2,1,0:T(8,128)(2,1)S(1)}, u32[]{:S(2)}, u32[]{:S(2)}) collective-permute-start(bf16[1,256,384]{2,1,0:T(8,128)(2,1)S(1)} %constant_dynamic-slice_fusion), channel_id=1, source_target_pairs={{0,128},{128,0},{1,129},{129,1},{2,130},{130,2},{3,131},{131,3},{4... | collective-permute-start | bytes 589832 | tf_op jit(solution)/shard_map/ppermute | solution.py:238
Sparse Core Ops, SparseCore 0:
  11.0 81.1 all-gather.2
  94.6 195.1 all-gather.4
  301.9 39.9 reduce-scatter.1

commit v11 on v10

--- a/solution.py
+++ b/solution.py
@@ -134,16 +134,20 @@
     ).astype(jnp.bfloat16)
     width_rows = qkv_weight.shape[0]
     qkv_cols = 3 * heads_local * HD
-    qkv_full = lax.all_gather(
-        qkv_weight.reshape(width_rows, qkv_cols), "seq", axis=0, tiled=True
+    head_full = lax.all_gather(
+        jnp.concatenate([qkv_weight.reshape(width_rows, qkv_cols), attn_weight.T], axis=1),
+        "seq",
+        axis=0,
+        tiled=True,
+    )
+    qkv_full, attn_weight_t = lax.optimization_barrier(
+        (head_full[:, :qkv_cols], head_full[:, qkv_cols:])
     )
     wblk_count = lax.psum(1, "wblk")
     spread = jnp.broadcast_to(normed.reshape(row_count, 1, dim_local), (row_count, wblk_count, dim_local))
     gathered = lax.all_to_all(spread, "wblk", 1, 1, tiled=True).reshape(row_count, D)
     up_cols = up_weight.shape[1]
-    tail_source = jnp.concatenate(
-        [up_weight, jnp.concatenate([attn_weight, down_weight], axis=0).T], axis=1
-    )
+    tail_source = jnp.concatenate([up_weight, down_weight.T], axis=1)
     tail_source, gathered = lax.optimization_barrier((tail_source, gathered))
     tail_full = lax.all_gather(tail_source, "seq", axis=0, tiled=True)
     up_full, out_weight_t = lax.optimization_barrier(
@@ -220,8 +224,13 @@
     activated = jax.nn.gelu(mlp_units, approximate=True).astype(jnp.bfloat16)
     block_terms = jnp.einsum(
         "bjk,rk->brj",
+        attn_weight_t.reshape(wblk_count, dim_local, -1),
+        attended,
+        preferred_element_type=jnp.float32,
+    ) + jnp.einsum(
+        "bjk,rk->brj",
         out_weight_t.reshape(wblk_count, dim_local, -1),
-        jnp.concatenate([attended, activated], axis=1),
+        activated,
         preferred_element_type=jnp.float32,
     )
     branch = lax.psum_scatter(

time: 357 us -> 376 us (1.053)
  waiting for transfers between devices: 198 us -> 179 us
  blocking collectives: 43 us -> 59.8 us
  matrix products: 30.3 us -> 39 us
  local copies, waits for them, and re-layouts: 25 us -> 32.2 us
  starting transfers between devices: 28 us -> 31.9 us
    all_gather x1, waiting for transfers between devices: 31 us -> 0.02 us  [shards(): tail_full = lax.all_gather(tail_source, 'seq', axis=0, tiled=True)]
    all_to_all x1, blocking collectives: 28.2 us -> 45 us  [shards(): returned = lax.all_to_all(mixed, 'seq', 0, 0, tiled=True)]
    dot_general x1, matrix products: 5.36 us -> 15.1 us  [shards(): jnp.einsum('bjk,rk->brj', out_weight_t.reshape(wblk_count, dim_local, -1)...]
    all_gather x1, waiting for transfers between devices: 0.02 us -> 7.96 us  [shards(): lax.all_gather(jnp.concatenate([qkv_weight.reshape(width_rows, qkv_cols),...]
    slice x2 -> x1, local copies, waits for them, and re-layouts: 0.01 us -> 7.91 us  [shards(): tail_full[:, up_cols:]]
    all_to_all x1, starting transfers between devices: 10 us -> 13.8 us  [shards(): received = lax.all_to_all(send, 'seq', 0, 0, tiled=True)]
  transfers between devices with their start and end apart: 7 -> 7, of which waited for: 5 -> 5; matrix products, arithmetic and copies ran while one was open for 15% -> 13% of each run, Pallas kernels for 0% -> 0%
where the time goes in v11:
time: 376 us; the launch traced here: 375 us
  waiting for transfers between devices  179 us (48%)
  blocking collectives  59.8 us (16%)
  matrix products  39 us (10%)
  local copies, waits for them, and re-layouts  32.2 us (9%)
  starting transfers between devices  31.9 us (8%)
  other arithmetic  18.4 us (5%)
  between operations  14.9 us (4%)
    all_to_all x1, waiting for transfers between devices, shards(): received = lax.all_to_all(send, 'seq', 0, 0, tiled=True)  85 us
    all_to_all x1, blocking collectives, shards(): returned = lax.all_to_all(mixed, 'seq', 0, 0, tiled=True)  45 us
    all_to_all x1, waiting for transfers between devices, shards(): lax.all_to_all(spread, 'wblk', 1, 1, tiled=True).reshape(row_count, D)  41.7 us
    reduce_scatter x1, waiting for transfers between devices, shards(): lax.psum_scatter(block_terms.astype(jnp.bfloat16), 'wblk', scatter_dimens...  40.5 us
    dot_general x1, matrix products, shards(): jnp.einsum('bjk,rk->brj', out_weight_t.reshape(wblk_count, dim_local, -1)...  15.1 us
    psum x1, blocking collectives, shards(): lax.psum((jnp.sum(hidden, axis=-1), jnp.sum(hidden * hidden, axis=-1)), '...  14.8 us
    all_to_all x1, starting transfers between devices, shards(): received = lax.all_to_all(send, 'seq', 0, 0, tiled=True)  13.8 us
    all_to_all x1, starting transfers between devices, shards(): lax.all_to_all(mod_spread, 'seq', 0, 0, tiled=True)  11.5 us
  transfers between devices with their start and end apart: 7, of which 5 were waited for; matrix products, arithmetic and copies ran while one was open for 13% of the time, Pallas kernels for 0%

profile of v11, /device:TPU:2, one launch (start us, length us, event | category | flops | bytes accessed | tf_op | source)
XLA Modules:
  0.0 375.0 jit_solution(10894734934829988417)
XLA Ops:
  7.2 1.2 reshape.273
  8.4 1.7 pad_maximum_fusion.3
  10.9 0.8 fusion.59
  11.7 0.2 fusion.33
  11.9 0.7 broadcast_in_dim.24
  12.5 11.5 %all-to-all-start = ((f32[16,3,384]{2,1,0:T(4,128)}), f32[16,3,384]{2,1,0:T(4,128)S(1)}, u32[]{:S(2)}, u32[]{:S(2)}) async-start(f32[16,3,384]{2,1,0:T(4,128)} %broadcast_in_dim.24), calls=%async_computation | async-start | bytes 196608 | tf_op jit(solution)/shard_map/all_to_all | solution.py:124
  24.0 1.3 convert_reduce_fusion
  25.3 14.8 %all-reduce.2 = (f32[2,288]{1,0:T(2,128)S(1)}, f32[2,288]{1,0:T(2,128)S(1)}) all-reduce(f32[2,288]{1,0:T(2,128)S(1)} %get-tuple-element.16, f32[2,288]{1,0:T(2,128)S(1)} %get-tuple-element.15), channel_id=1, replica_groups=mesh['cfg'=2,'seq'=16,'wblk'=8] {'wblk'}, use_global_device_ids=true, to_apply=%region_4.5 | all-reduce | flops 1152 | bytes 9216 | tf_op jit(solution)/shard_map/psum | solution.py:127
  40.2 0.1 mul.288
  40.2 0.1 sub.76
  40.4 1.0 fusion.28
  41.4 2.1 broadcast_in_dim.26
  43.6 4.6 %all-to-all-start.1 = ((bf16[576,8,384]{2,0,1:T(8,128)(2,1)}), bf16[576,8,384]{2,0,1:T(8,128)(2,1)}, u32[]{:S(2)}, u32[]{:S(2)}) async-start(bf16[576,8,384]{2,0,1:T(8,128)(2,1)} %broadcast_in_dim.26), calls=%async_computation.1 | async-start | bytes 7077888 | tf_op jit(solution)/shard_map/all_to_all | solution.py:148
  48.2 0.8 pad_maximum_fusion.1
  49.1 41.7 %all-to-all-done.1 = bf16[576,8,384]{2,0,1:T(8,128)(2,1)} async-done(((bf16[576,8,384]{2,0,1:T(8,128)(2,1)}), bf16[576,8,384]{2,0,1:T(8,128)(2,1)}, u32[]{:S(2)}, u32[]{:S(2)}) %all-to-all-start.1) | async-done | bytes 3538976 | tf_op jit(solution)/shard_map/all_to_all | solution.py:148
  90.8 4.5 %copy.66 = bf16[8,72,8,384]{3,2,0,1:T(8,128)(2,1)} copy(bf16[8,72,8,384]{3,2,1,0:T(8,128)(2,1)} %bitcast.44) | data formatting | bytes 7077888 | tf_op jit(solution)/shard_map/reshape | solution.py:148
  95.4 0.1 mul.315
  95.5 0.1 mul.296
  95.7 0.1 concatenate.36
  95.8 0.1 broadcast_multiply_fusion.1
  95.9 0.4 fusion.40
  96.3 8.0 %all-gather.3.cloned.1.call-done = bf16[3072,1024]{1,0:T(8,128)(2,1)} async-done(((bf16[192,1024]{1,0:T(8,128)(2,1)}), bf16[3072,1024]{1,0:T(8,128)(2,1)}) %all-gather.3.cloned.1.call-update) | async-done | bytes 6291472 | tf_op jit(solution)/shard_map/all_gather | solution.py:137
  104.3 2.3 slice-done
  106.6 1.1 copy-done.4
  107.7 4.1 %fusion.71 = f32[576,768]{1,0:T(8,128)} fusion(bf16[576,3072]{1,0:T(8,128)(2,1)S(1)} %bitcast.93, bf16[3072,768]{1,0:T(8,128)(2,1)S(1)} %slice-done), kind=kOutput, calls=%fused_computation.121 | convolution fusion | flops 2717908992 | bytes 10027008 | tf_op jit(solution)/shard_map/rk,kn->rn/dot_general | solution.py:156
  111.9 2.2 reshape.274
  114.1 0.2 slice.87
  114.3 1.2 fusion.67
  115.5 1.4 copy.62
  116.9 0.5 copy.61
  117.4 0.4 multiply_reduce_fusion.1
  117.8 0.4 multiply_reduce_fusion.2
  118.2 0.4 multiply_multiply_fusion.1
  118.5 0.4 multiply_multiply_fusion.2
  118.9 0.8 subtract_convert_fusion.1
  119.7 0.6 pad_maximum_fusion.4
  120.3 0.5 copy.50
  120.8 0.6 pad_maximum_fusion.5
  121.4 0.5 copy.53
  121.9 0.2 broadcast_in_dim.29
  122.1 0.2 broadcast_in_dim.35
  122.2 1.7 pad_maximum_fusion
  123.9 13.8 %all-to-all-start.2 = ((bf16[16,648,128]{2,1,0:T(8,128)(2,1)}), bf16[16,648,128]{2,1,0:T(8,128)(2,1)S(1)}, u32[]{:S(2)}, u32[]{:S(2)}) async-start(bf16[16,648,128]{2,1,0:T(8,128)(2,1)} %pad_maximum_fusion), calls=%async_computation.2 | async-start | bytes 5308416 | tf_op jit(solution)/shard_map/all_to_all | solution.py:199
  137.8 0.2 reduce-scatter.2.cloned.1.call-start
  138.1 0.6 dynamic_slice.16
  138.6 0.7 fusion.50
  139.3 85.0 %all-to-all-done.2 = bf16[16,648,128]{2,1,0:T(8,128)(2,1)S(1)} async-done(((bf16[16,648,128]{2,1,0:T(8,128)(2,1)}), bf16[16,648,128]{2,1,0:T(8,128)(2,1)S(1)}, u32[]{:S(2)}, u32[]{:S(2)}) %all-to-all-start.2) | async-done | bytes 2654240 | tf_op jit(solution)/shard_map/all_to_all | solution.py:199
  224.3 0.2 fusion.66
  224.5 3.5 fusion.68
  228.0 4.2 %fusion.1 = f32[1152]{0:T(1024)S(1)} fusion(f32[1152,4608]{1,0:T(8,128)S(1)} %get-tuple-element.43, f32[1152]{0:T(1024)S(1)} %get-tuple-element.42), kind=kLoop, calls=%fused_computation.3 | loop fusion | flops 10615680 | bytes 21242880 | tf_op jit(solution)/shard_map/reduce_sum | solution.py:216
  232.2 3.0 copy-done.2
  235.3 10.1 %fusion.10 = bf16[1152,128]{1,0:T(8,128)(2,1)S(1)} fusion(bf16[4608,128]{1,0:T(8,128)(2,1)S(1)} %bitcast.87, f32[1152,4608]{1,0:T(8,128)} %copy-done.2, f32[1152]{0:T(1024)S(1)} %get-tuple-element.42, f32[1152]{0:T(1024)S(1)} %fusion.1), kind=kOutput, calls=%fused_computation.12 | convolution fusion | flops 1369866240 | bytes 22717440 | tf_op jit(solution)/shard_map/dot_general | solution.py:217
  245.4 45.0 %all_to_all.20 = bf16[16,72,128]{2,1,0:T(8,128)(2,1)S(1)} all-to-all(bf16[16,72,128]{2,1,0:T(8,128)(2,1)S(1)} %bitcast.95), channel_id=1, replica_groups=mesh['cfg'=2,'seq'=16,'wblk'=8] {'seq'}, dimensions={0} | all-to-all | bytes 589824 | tf_op jit(solution)/shard_map/all_to_all | solution.py:221
  290.3 0.2 copy.78
  290.6 0.2 reshape.303
  290.8 7.9 %fusion.65 = (bf16[3072,768]{1,0:T(8,128)(2,1)}, bf16[3072,768]{1,0:T(8,128)(2,1)}) fusion(bf16[3072,1536]{1,0:T(8,128)(2,1)} %all-gather.5.cloned.1.call-done), kind=kLoop, calls=%fused_computation.115 | loop fusion | bytes 18874368 | tf_op jit(solution)/shard_map/slice | solution.py:154
  298.7 15.1 %fusion.23 = f32[576,8,384]{2,0,1:T(8,128)} fusion(bf16[8,384,768]{2,1,0:T(8,128)(2,1)} %bitcast.91, bf16[576,3072]{1,0:T(8,128)(2,1)} %bitcast.92, bf16[3072,768]{1,0:T(8,128)(2,1)} %get-tuple-element.13), kind=kOutput, calls=%fused_computation.24 | convolution fusion | flops 5439799296 | bytes 20054016 | tf_op jit(solution)/shard_map/bjk,rk->brj/dot_general | solution.py:230
  313.8 6.0 %fusion.6 = bf16[8,576,384]{2,1,0:T(8,128)(2,1)} fusion(f32[576,8,384]{2,0,1:T(8,128)} %fusion.23, bf16[576,256,1]{1,0,2:T(8,128)(2,1)S(1)} %reshape.303, bf16[8,384,256]{2,1,0:T(8,128)(2,1)S(1)} %bitcast.86), kind=kOutput, calls=%fused_computation.8 | convolution fusion | flops 909508608 | bytes 12484608 | tf_op jit(solution)/shard_map/bjk,rk->brj/dot_general | solution.py:225
  319.9 40.5 %reduce-scatter.2.cloned.1.call-done = bf16[1,576,384]{2,1,0:T(8,128)(2,1)} async-done(((bf16[8,576,384]{2,1,0:T(8,128)(2,1)}), bf16[1,576,384]{2,1,0:T(8,128)(2,1)}) %reduce-scatter.2.cloned.1.call-update) | async-done | bytes 442384 | tf_op jit(solution)/shard_map/reduce_scatter | solution.py:236
  360.4 1.1 fusion.22
  361.7 1.6 collective-permute-start
  363.3 0.6 slice_bitcast_fusion
  363.9 3.5 collective-permute-done
  367.4 1.0 multiply_add_fusion
  (47 shorter events, 0.6 us)
Async XLA Ops:
  7.2 4.5 %copy-start = (bf16[192,3,384]{2,0,1:T(8,128)(2,1)S(1)}, bf16[192,3,384]{2,0,1:T(8,128)(2,1)}, u32[]{:S(2)}) copy-start(bf16[192,3,384]{2,0,1:T(8,128)(2,1)} %param.15) | copy-start | bytes 1327108
  7.2 33.2 %copy-start.3 = (bf16[2,256,384]{2,1,0:T(8,128)(2,1)S(1)}, bf16[2,256,384]{2,1,0:T(8,128)(2,1)}, u32[]{:S(2)}) copy-start(bf16[2,256,384]{2,1,0:T(8,128)(2,1)} %param.13) | copy-start | bytes 1179652
  7.2 97.1 %all-gather.3.cloned.1.call-start = ((), (), s32[]{:S(2)}) async-start(), calls=%async_computation.5 | async-start | bytes 6684672 | tf_op jit(solution)/shard_map/all_gather | solution.py:137
  12.5 27.8 %all-to-all-start = ((f32[16,3,384]{2,1,0:T(4,128)}), f32[16,3,384]{2,1,0:T(4,128)S(1)}, u32[]{:S(2)}, u32[]{:S(2)}) async-start(f32[16,3,384]{2,1,0:T(4,128)} %broadcast_in_dim.24), calls=%async_computation | async-start | bytes 196608 | tf_op jit(solution)/shard_map/all_to_all | solution.py:124
  43.5 4.7 %copy-start.6 = (bf16[768,192]{0,1:T(8,128)(2,1)S(1)}, bf16[768,192]{0,1:T(8,128)(2,1)}, u32[]{:S(2)}) copy-start(bf16[768,192]{0,1:T(8,128)(2,1)} %param.21) | copy-start | bytes 884740
  43.6 4.7 %copy-start.7 = (bf16[192,768]{1,0:T(8,128)(2,1)S(1)}, bf16[192,768]{1,0:T(8,128)(2,1)}, u32[]{:S(2)}) copy-start(bf16[192,768]{1,0:T(8,128)(2,1)} %param.17) | copy-start | bytes 884740
  43.6 47.2 %all-to-all-start.1 = ((bf16[576,8,384]{2,0,1:T(8,128)(2,1)}), bf16[576,8,384]{2,0,1:T(8,128)(2,1)}, u32[]{:S(2)}, u32[]{:S(2)}) async-start(bf16[576,8,384]{2,0,1:T(8,128)(2,1)} %broadcast_in_dim.26), calls=%async_computation.1 | async-start | bytes 7077888 | tf_op jit(solution)/shard_map/all_to_all | solution.py:148
  48.2 242.6 %all-gather.5.cloned.1.call-start = ((), (), s32[]{:S(2)}) async-start(), calls=%async_computation.6 | async-start | bytes 10027008 | tf_op jit(solution)/shard_map/all_gather | solution.py:152
  90.8 4.6 %copy-start.8 = (f32[128]{0:T(128)S(1)}, f32[128]{0:T(128)}, u32[]{:S(2)}) copy-start(f32[128]{0:T(128)} %param.18) | copy-start | bytes 1540
  90.8 4.7 %copy-start.9 = (f32[128]{0:T(128)S(1)}, f32[128]{0:T(128)}, u32[]{:S(2)}) copy-start(f32[128]{0:T(128)} %param.19) | copy-start | bytes 1540
  104.3 2.3 slice-start
  104.3 3.4 copy-start.4
  123.9 14.1 %copy-start.10 = (s32[2]{0:T(128)S(1)}, s32[2]{0:T(128)}, u32[]{:S(2)}) copy-start(s32[2]{0:T(128)} %param.22) | copy-start | bytes 28
  123.9 100.4 %all-to-all-start.2 = ((bf16[16,648,128]{2,1,0:T(8,128)(2,1)}), bf16[16,648,128]{2,1,0:T(8,128)(2,1)S(1)}, u32[]{:S(2)}, u32[]{:S(2)}) async-start(bf16[16,648,128]{2,1,0:T(8,128)(2,1)} %pad_maximum_fusion), calls=%async_computation.2 | async-start | bytes 5308416 | tf_op jit(solution)/shard_map/all_to_all | solution.py:199
  137.8 222.6 %reduce-scatter.2.cloned.1.call-start = ((), (), s32[]{:S(2)}) async-start(), calls=%async_computation.7 | async-start | bytes 3981312 | tf_op jit(solution)/shard_map/reduce_scatter | solution.py:236
  228.0 7.3 %copy-start.2 = (f32[1152,4608]{1,0:T(8,128)}, f32[1152,4608]{1,0:T(8,128)S(1)}, u32[]{:S(2)}) copy-start(f32[1152,4608]{1,0:T(8,128)S(1)} %get-tuple-element.43) | copy-start | bytes 63700996
  298.7 15.1 %slice-start.1 = ((bf16[3072,1024]{1,0:T(8,128)(2,1)}), bf16[3072,256]{1,0:T(8,128)(2,1)S(1)}, s32[]{:S(2)}) async-start(bf16[3072,1024]{1,0:T(8,128)(2,1)} %all-gather.3.cloned.1.call-done), calls=%async_computation.9 | async-start | bytes 3145728 | tf_op jit(solution)/shard_map/slice | solution.py:144
  319.8 40.6 %copy-start.5 = (bf16[1,2,32,384]{3,2,1,0:T(8,128)(2,1)S(1)}, bf16[1,2,32,384]{3,2,1,0:T(8,128)(2,1)}, u32[]{:S(2)}) copy-start(bf16[1,2,32,384]{3,2,1,0:T(8,128)(2,1)} %param.12) | copy-start | bytes 147460
  319.8 48.6 %copy-start.1 = (bf16[192,3,384]{2,0,1:T(8,128)(2,1)S(1)}, bf16[192,3,384]{2,0,1:T(8,128)(2,1)}, u32[]{:S(2)}) copy-start(bf16[192,3,384]{2,0,1:T(8,128)(2,1)} %param.15) | copy-start | bytes 1327108
  361.7 5.8 %collective-permute-start = (bf16[1,256,384]{2,1,0:T(8,128)(2,1)S(1)}, bf16[1,256,384]{2,1,0:T(8,128)(2,1)S(1)}, u32[]{:S(2)}, u32[]{:S(2)}) collective-permute-start(bf16[1,256,384]{2,1,0:T(8,128)(2,1)S(1)} %constant_dynamic-slice_fusion), channel_id=1, source_target_pairs={{0,128},{128,0},{1,129},{129,1},{2,130},{130,2},{3,131},{131,3},{4... | collective-permute-start | bytes 589832 | tf_op jit(solution)/shard_map/ppermute | solution.py:247
Sparse Core Ops, SparseCore 0:
  11.0 93.2 all-gather.2
  106.7 150.4 all-gather.4
  319.9 40.4 reduce-scatter.1
